TPU v7x, 256 devices: a whole 4x4x8 slice. The times are simulated.
256 devices in a mesh: roll: 32 (over y, z_lo, core), seq: 8 (over x, z_hi).
Axes of the slice: x: 4, y: 4, z: 8 (z_hi: 2, z_lo: 4; z = z_hi * 4 + z_lo), core: 2. Of those that a mesh axis runs over, the one named last changes fastest.
Arguments:
- queries: bfloat16 [65536, 3072], P(('roll', 'seq')), parts along dimension 0, may hold values from -7.5 to 7.5
- keys_in: bfloat16 [65536, 3072], P(('roll', 'seq')), parts along dimension 0, may hold values from -7.5 to 7.5
- values_in: bfloat16 [65536, 3072], P(('roll', 'seq')), parts along dimension 0, may hold values from -6 to 6
- latent_proj: bfloat16 [3072, 64], replicated, may hold values from -3 to 3
- conv_weight: bfloat16 [432, 512], replicated, may hold values from -0.3125 to 0.3125
- conv_bias: float32 [512], replicated, may hold values from -3 to 3
- pool_weight: float32 [8, 2, 8, 64], P('seq'), may hold values from -5 to 5
- tile_block: int32 [1024], P('roll'), parts along dimension 0, may hold values from 0 to 31, each once
- owner_slot: int32 [512], P('roll'), parts along dimension 0, may hold values from 0 to 15, each once
Outputs:
- decoded: bfloat16 [256, 2, 8, 64, 512], P(('roll', 'seq')), parts along dimension 0
- policy_features: float32 [512, 512], P(('roll', 'seq')), parts along dimension 0
There are 32 independent parts, one for each index of `roll`. A program takes and returns all parts, laid end to end along the dimension named above; an argument that names none is the same for every part. Nothing has to cross between parts.
Inputs may be any that keep to these rules, and one draw needn't show every extreme that they name: `tile_block`: each piece index once. `owner_slot`: each row once.
All inputs are finite; a program needn't handle non-finite values.
Results may differ from a plain program's by a relative error of at most 0.013.
Values may be sent and summed in bfloat16 or wider, within the bound.
No kernel may reach another device: no remote copies, remote signals or barrier semaphores. Data moves between devices by JAX's collectives and lax.ppermute only.
A program may use at most 64 MiB of HBM per device.

v0:
```python
import math

import jax
import jax.numpy as jnp
from jax import lax
from jax.sharding import PartitionSpec as P

H = 24
HD = 128
LC = 16
CO = 512
S_DEV = 256
RT = 4
WT = 32
TR = 2
BPD = 2
FT = 2
RL = 8
COLS = 64


def shifted(array, axis, by):
    length = lax.axis_size(axis)
    pairs = [(i, i + by) for i in range(length) if 0 <= i + by < length]
    return lax.ppermute(array, axis, pairs)


def swapped(array, axis, bit):
    return lax.ppermute(array, axis, [(i, i ^ 1 << bit) for i in range(lax.axis_size(axis))])


def heads_attention(query_all, key_all, value_all):
    length = query_all.shape[0]
    block_rows = min(512, length)
    score_scale = 1.0 / math.sqrt(query_all.shape[2])
    query_blocks = query_all.reshape(
        length // block_rows, block_rows, query_all.shape[1], query_all.shape[2]
    )

    def one_block(query_part):
        scores = (
            jnp.einsum("qhd,khd->hqk", query_part, key_all, preferred_element_type=jnp.float32)
            * score_scale
        )
        expo = jnp.exp(scores - jnp.max(scores, axis=-1, keepdims=True))
        totals = jnp.sum(expo, axis=-1, keepdims=True)
        mixed = jnp.einsum(
            "hqk,khd->qhd", expo.astype(jnp.bfloat16), value_all, preferred_element_type=jnp.float32
        )
        return (mixed / jnp.transpose(totals, (1, 0, 2))).astype(jnp.bfloat16)

    return lax.map(one_block, query_blocks).reshape(length, query_all.shape[1], query_all.shape[2])


def window_columns(volume):
    frame_count = volume.shape[0] - 2
    row_count = volume.shape[1] - 2
    col_count = volume.shape[2] - 2
    pieces = [
        volume[a : a + frame_count, b : b + row_count, c : c + col_count]
        for a in range(3)
        for b in range(3)
        for c in range(3)
    ]
    return jnp.concatenate(pieces, axis=-1).reshape(
        frame_count * row_count * col_count, 27 * volume.shape[3]
    )


def local(
    queries,
    keys_in,
    values_in,
    latent_proj,
    conv_weight,
    conv_bias,
    pool_weight,
    tile_block,
    owner_slot,
):
    group_count = lax.axis_size("seq")
    my_index = lax.axis_index("seq")
    seq_len = S_DEV * group_count
    heads_dev = H // group_count
    quarter = S_DEV // 4

    def to_groups(matrix):
        return matrix.reshape(S_DEV, group_count, heads_dev, HD)

    query_all = lax.all_to_all(to_groups(queries), "seq", split_axis=1, concat_axis=0, tiled=True)
    key_all = lax.all_to_all(to_groups(keys_in), "seq", split_axis=1, concat_axis=0, tiled=True)
    value_all = lax.all_to_all(to_groups(values_in), "seq", split_axis=1, concat_axis=0, tiled=True)
    mixed = heads_attention(query_all[:, 0], key_all[:, 0], value_all[:, 0])[:, None]
    flat_heads = mixed.reshape(seq_len, heads_dev * HD)
    ordered = flat_heads.reshape(4 * group_count, quarter, heads_dev * HD)[tile_block]
    ordered = ordered.reshape(seq_len, 1, heads_dev, HD)
    returned = lax.all_to_all(ordered, "seq", split_axis=0, concat_axis=1, tiled=True)
    tile_heads = returned.reshape(S_DEV, H * HD)
    latent = jnp.dot(tile_heads, latent_proj, preferred_element_type=jnp.float32).astype(
        jnp.bfloat16
    )
    tile_latent = (
        latent.reshape(FT, RT, WT, 2, 2, LC).transpose(0, 1, 3, 2, 4, 5).reshape(FT, RL, COLS * LC)
    )
    earlier = shifted(tile_latent, "seq", TR)
    extended = jnp.concatenate([earlier, tile_latent], axis=0)
    band_row = my_index % TR
    upper_band = band_row == 0
    outgoing = jnp.where(upper_band, extended[:, RL - 1 :], extended[:, :1])
    incoming = swapped(outgoing, "seq", 0)
    above = jnp.where(upper_band, jnp.zeros_like(incoming), incoming)
    below = jnp.where(upper_band, incoming, jnp.zeros_like(incoming))
    volume = jnp.concatenate([above, extended, below], axis=1).reshape(FT + 2, RL + 2, COLS, LC)
    volume = jnp.pad(volume, ((0, 0), (0, 0), (1, 1), (0, 0)))
    pre_act = (
        jnp.dot(window_columns(volume), conv_weight, preferred_element_type=jnp.float32) + conv_bias
    )
    decoded = pre_act.astype(jnp.bfloat16).reshape(1, FT, RL, COLS, CO)
    block_count = BPD * group_count
    band_voxels = group_count // TR * FT * TR * RL * (COLS // block_count)
    weighted = jax.nn.silu(pre_act).reshape(FT, RL, COLS, CO) * pool_weight[0][..., None]
    pooled_term = jnp.sum(weighted, axis=(0, 1)).reshape(block_count, COLS // block_count, CO).sum(
        axis=1
    ) / math.sqrt(band_voxels)
    total_pooled = lax.psum(pooled_term.astype(jnp.bfloat16), "seq").astype(jnp.float32)
    wanted_rows = my_index * BPD + jnp.arange(BPD, dtype=jnp.int32)
    chooser = (owner_slot[None, :] == wanted_rows[:, None]).astype(jnp.float32)
    policy = jnp.dot(
        chooser, total_pooled, precision=lax.Precision.HIGHEST, preferred_element_type=jnp.float32
    )
    return (decoded, policy)


def solution(mesh):
    placed = (
        P(("roll", "seq"), None),
        P(("roll", "seq"), None),
        P(("roll", "seq"), None),
        P(),
        P(),
        P(),
        P("seq", None, None, None),
        P("roll"),
        P("roll"),
    )
    return jax.shard_map(
        local,
        mesh=mesh,
        in_specs=placed,
        out_specs=(P(("roll", "seq"), None, None, None, None), P(("roll", "seq"), None)),
        check_vma=False,
    )
```

profile of v0, /device:TPU:56, one launch (start us, length us, event | category | flops | bytes accessed | tf_op | source)
XLA Modules:
  0.0 300.3 jit_solution(7077981178723374902)
XLA Ops:
  0.6 2.7 copy.76
  3.3 10.0 %all-to-all-start.1 = ((bf16[256,8,3,128]{0,3,2,1:T(8,128)(2,1)}), bf16[256,8,3,128]{0,3,2,1:T(8,128)(2,1)S(1)}, u32[]{:S(2)}, u32[]{:S(2)}) async-start(bf16[256,8,3,128]{0,3,2,1:T(8,128)(2,1)} %bitcast.79), calls=%async_computation.1 | async-start | bytes 3145728 | tf_op jit(solution)/shard_map/all_to_all | solution.py:91
  13.3 2.6 copy.78
  15.9 39.6 %all-to-all-done.1 = bf16[256,8,3,128]{0,3,2,1:T(8,128)(2,1)S(1)} async-done(((bf16[256,8,3,128]{0,3,2,1:T(8,128)(2,1)}), bf16[256,8,3,128]{0,3,2,1:T(8,128)(2,1)S(1)}, u32[]{:S(2)}, u32[]{:S(2)}) %all-to-all-start.1) | async-done | bytes 1572896 | tf_op jit(solution)/shard_map/all_to_all | solution.py:91
  56.6 4.3 %all-to-all-start.2 = ((bf16[256,8,3,128]{0,3,2,1:T(8,128)(2,1)}), bf16[256,8,3,128]{0,3,2,1:T(8,128)(2,1)}, u32[]{:S(2)}, u32[]{:S(2)}) async-start(bf16[256,8,3,128]{0,3,2,1:T(8,128)(2,1)} %bitcast.78), calls=%async_computation.2 | async-start | bytes 3145728 | tf_op jit(solution)/shard_map/all_to_all | solution.py:92
  61.0 2.6 copy.74
  63.5 29.7 %all-to-all-done.2 = bf16[256,8,3,128]{0,3,2,1:T(8,128)(2,1)} async-done(((bf16[256,8,3,128]{0,3,2,1:T(8,128)(2,1)}), bf16[256,8,3,128]{0,3,2,1:T(8,128)(2,1)}, u32[]{:S(2)}, u32[]{:S(2)}) %all-to-all-start.2) | async-done | bytes 1572896 | tf_op jit(solution)/shard_map/all_to_all | solution.py:92
  93.3 4.9 %all-to-all-start = ((bf16[256,8,3,128]{0,3,2,1:T(8,128)(2,1)}), bf16[256,8,3,128]{0,3,2,1:T(8,128)(2,1)}, u32[]{:S(2)}, u32[]{:S(2)}) async-start(bf16[256,8,3,128]{0,3,2,1:T(8,128)(2,1)} %bitcast.6), calls=%async_computation | async-start | bytes 3145728 | tf_op jit(solution)/shard_map/all_to_all | solution.py:90
  100.1 2.6 copy.79
  102.7 25.0 %all-to-all-done = bf16[256,8,3,128]{0,3,2,1:T(8,128)(2,1)} async-done(((bf16[256,8,3,128]{0,3,2,1:T(8,128)(2,1)}), bf16[256,8,3,128]{0,3,2,1:T(8,128)(2,1)}, u32[]{:S(2)}, u32[]{:S(2)}) %all-to-all-start) | async-done | bytes 1572896 | tf_op jit(solution)/shard_map/all_to_all | solution.py:90
  127.7 2.6 copy.75
  130.3 34.3 %while.10 = (s32[]{:T(128)}, bf16[4,512,3,128]{3,1,2,0:T(8,128)(2,1)}, bf16[4,512,3,128]{3,1,0,2:T(8,128)(2,1)}, bf16[2048,3,128]{2,0,1:T(8,128)(2,1)S(1)}, bf16[2048,3,128]{2,0,1:T(8,128)(2,1)}, /*index=5*/s32[]{:T(128)}) while((s32[]{:T(128)}, bf16[4,512,3,128]{3,1,2,0:T(8,128)(2,1)}, bf16[4,512,3,128]{3,1,0,2:T(8,128)(2,1)}, ...), condition=%wide.region_3.4_spmd, body=%wide.region_0.3_spmd.sunk | while | flops 1636168704 | bytes 48004192 | solution.py:52
  130.3 2.9 multiply_reduce_fusion.3
  133.2 2.5 fusion.46
  135.7 3.2 %fusion.47 = bf16[4,512,3,128]{3,1,2,0:T(8,128)(2,1)} fusion(bf16[4,512,3,128]{3,1,2,0:T(8,128)(2,1)} %get-tuple-element.145, s32[]{:T(128)} %get-tuple-element.144, bf16[2048,3,128]{2,0,1:T(8,128)(2,1)S(1)} %copy-done.2, f32[3,512,2048]{2,1,0:T(8,128)S(1)} %get-tuple-element.136, f32[3,512]{1,0:T(4,128)S(1)} %get-tuple-element.137, ...), kind=kOutput, calls=%fused_computation.12.clone.1 | convolution fusion | flops 815136768 | bytes 14561792 | tf_op jit(solution)/shard_map/while/body/eval_jaxpr/hqk,khd->qhd/dot_general | solution.py:47
  138.9 2.9 multiply_reduce_fusion.3
  141.8 2.5 fusion.46
  144.2 3.2 %fusion.47 = bf16[4,512,3,128]{3,1,2,0:T(8,128)(2,1)} fusion(bf16[4,512,3,128]{3,1,2,0:T(8,128)(2,1)} %get-tuple-element.145, s32[]{:T(128)} %get-tuple-element.144, bf16[2048,3,128]{2,0,1:T(8,128)(2,1)S(1)} %copy-done.2, f32[3,512,2048]{2,1,0:T(8,128)S(1)} %get-tuple-element.136, f32[3,512]{1,0:T(4,128)S(1)} %get-tuple-element.137, ...), kind=kOutput, calls=%fused_computation.12.clone.1 | convolution fusion | flops 815136768 | bytes 14561792 | tf_op jit(solution)/shard_map/while/body/eval_jaxpr/hqk,khd->qhd/dot_general | solution.py:47
  147.4 2.9 multiply_reduce_fusion.3
  150.3 2.5 fusion.46
  152.8 3.2 %fusion.47 = bf16[4,512,3,128]{3,1,2,0:T(8,128)(2,1)} fusion(bf16[4,512,3,128]{3,1,2,0:T(8,128)(2,1)} %get-tuple-element.145, s32[]{:T(128)} %get-tuple-element.144, bf16[2048,3,128]{2,0,1:T(8,128)(2,1)S(1)} %copy-done.2, f32[3,512,2048]{2,1,0:T(8,128)S(1)} %get-tuple-element.136, f32[3,512]{1,0:T(4,128)S(1)} %get-tuple-element.137, ...), kind=kOutput, calls=%fused_computation.12.clone.1 | convolution fusion | flops 815136768 | bytes 14561792 | tf_op jit(solution)/shard_map/while/body/eval_jaxpr/hqk,khd->qhd/dot_general | solution.py:47
  156.0 2.9 multiply_reduce_fusion.3
  158.9 2.5 fusion.46
  161.4 3.2 %fusion.47 = bf16[4,512,3,128]{3,1,2,0:T(8,128)(2,1)} fusion(bf16[4,512,3,128]{3,1,2,0:T(8,128)(2,1)} %get-tuple-element.145, s32[]{:T(128)} %get-tuple-element.144, bf16[2048,3,128]{2,0,1:T(8,128)(2,1)S(1)} %copy-done.2, f32[3,512,2048]{2,1,0:T(8,128)S(1)} %get-tuple-element.136, f32[3,512]{1,0:T(4,128)S(1)} %get-tuple-element.137, ...), kind=kOutput, calls=%fused_computation.12.clone.1 | convolution fusion | flops 815136768 | bytes 14561792 | tf_op jit(solution)/shard_map/while/body/eval_jaxpr/hqk,khd->qhd/dot_general | solution.py:47
  164.6 2.8 copy.81
  167.4 2.5 reshape_reshape_broadcast_in_dim_reshape.3
  169.9 3.3 %gather_fusion = bf16[32,64,384]{2,1,0:T(8,128)(2,1)} fusion(bf16[32,64,384]{2,1,0:T(8,128)(2,1)} %reshape_reshape_broadcast_in_dim_reshape.3, s32[1024]{0:T(1024)S(1)} %pad_clamp_fusion), kind=kCustom, calls=%fused_computation | custom fusion | bytes 3145856 | tf_op jit(solution)/shard_map/gather | solution.py:95
  173.2 3.9 %reshape.55 = bf16[2048,1,3,128]{3,2,0,1:T(4,128)(2,1)S(1)} reshape(bf16[32,64,384]{2,1,0:T(8,128)(2,1)} %gather_fusion) | data formatting | bytes 3145728 | tf_op jit(solution)/shard_map/reshape | solution.py:96
  177.2 43.1 %all_to_all.60 = bf16[2048,1,3,128]{3,2,1,0:T(4,128)(2,1)S(1)} all-to-all(bf16[2048,1,3,128]{3,2,1,0:T(4,128)(2,1)S(1)} %bitcast.75), channel_id=1, replica_groups=mesh['roll'=32,'seq'=8] {'seq'}, dimensions={0} | all-to-all | bytes 3145728 | tf_op jit(solution)/shard_map/all_to_all | solution.py:97
  229.1 7.0 %collective-permute-done.1 = bf16[4,1,1024]{2,1,0:T(2,128)(2,1)S(1)} collective-permute-done((bf16[4,1,1024]{2,1,0:T(2,128)(2,1)S(1)}, bf16[4,1,1024]{2,1,0:T(2,128)(2,1)S(1)}, u32[]{:S(2)}, u32[]{:S(2)}) %collective-permute-start.1) | collective-permute-done | bytes 8224 | tf_op jit(solution)/shard_map/ppermute | solution.py:29
  241.3 5.9 %concatenate.11 = bf16[2,8,64,432]{3,2,0,1:T(8,128)(2,1)S(1)} concatenate(bf16[2,8,64,16]{3,2,0,1:T(8,128)(2,1)} %get-tuple-element.100, bf16[2,8,64,16]{3,2,0,1:T(8,128)(2,1)} %get-tuple-element.99, bf16[2,8,64,16]{3,2,0,1:T(8,128)(2,1)} %get-tuple-element.75, bf16[2,8,64,16]{3,2,0,1:T(8,128)(2,1)} %get-tuple-element.76, bf16[2,8,64,16]{3,2,0,1:T(8,128)(2,1)} %get-tuple-element.98, ...), dimensions={3} | concatenate | bytes 1769472 | tf_op jit(solution)/shard_map/concatenate | solution.py:65
  250.1 49.3 %psum.7 = bf16[16,512]{1,0:T(8,128)(2,1)S(1)} all-reduce(bf16[16,512]{1,0:T(8,128)(2,1)S(1)} %multiply_convert_fusion), channel_id=1, replica_groups=mesh['roll'=32,'seq'=8] {'seq'}, use_global_device_ids=true, to_apply=%region_6.7 | all-reduce | flops 8192 | bytes 32768 | tf_op jit(solution)/shard_map/psum | solution.py:125
  (53 shorter events, 20.7 us)
Async XLA Ops:
  0.6 246.7 %copy-start = (bf16[432,512]{1,0:T(8,128)(2,1)S(1)}, bf16[432,512]{1,0:T(8,128)(2,1)}, u32[]{:S(2)}) copy-start(bf16[432,512]{1,0:T(8,128)(2,1)} %param.15) | copy-start | bytes 1327108
  3.3 52.2 %all-to-all-start.1 = ((bf16[256,8,3,128]{0,3,2,1:T(8,128)(2,1)}), bf16[256,8,3,128]{0,3,2,1:T(8,128)(2,1)S(1)}, u32[]{:S(2)}, u32[]{:S(2)}) async-start(bf16[256,8,3,128]{0,3,2,1:T(8,128)(2,1)} %bitcast.79), calls=%async_computation.1 | async-start | bytes 3145728 | tf_op jit(solution)/shard_map/all_to_all | solution.py:91
  55.5 1.1 copy-start.1
  56.6 36.6 %all-to-all-start.2 = ((bf16[256,8,3,128]{0,3,2,1:T(8,128)(2,1)}), bf16[256,8,3,128]{0,3,2,1:T(8,128)(2,1)}, u32[]{:S(2)}, u32[]{:S(2)}) async-start(bf16[256,8,3,128]{0,3,2,1:T(8,128)(2,1)} %bitcast.78), calls=%async_computation.2 | async-start | bytes 3145728 | tf_op jit(solution)/shard_map/all_to_all | solution.py:92
  93.2 4.9 %copy-start.6 = (s32[32]{0:T(128)S(1)}, s32[32]{0:T(128)}, u32[]{:S(2)}) copy-start(s32[32]{0:T(128)} %param.18) | copy-start | bytes 388
  93.3 34.5 %all-to-all-start = ((bf16[256,8,3,128]{0,3,2,1:T(8,128)(2,1)}), bf16[256,8,3,128]{0,3,2,1:T(8,128)(2,1)}, u32[]{:S(2)}, u32[]{:S(2)}) async-start(bf16[256,8,3,128]{0,3,2,1:T(8,128)(2,1)} %bitcast.6), calls=%async_computation | async-start | bytes 3145728 | tf_op jit(solution)/shard_map/all_to_all | solution.py:90
  133.2 2.5 copy-start.2
  141.8 2.5 copy-start.2
  150.3 2.5 copy-start.2
  158.9 2.5 copy-start.2
  220.5 1.6 copy-start.3
  224.6 3.6 %collective-permute-start = (bf16[2,8,1024]{2,1,0:T(8,128)(2,1)S(1)}, bf16[2,8,1024]{2,1,0:T(8,128)(2,1)S(1)}, u32[]{:S(2)}, u32[]{:S(2)}) collective-permute-start(bf16[2,8,1024]{2,1,0:T(8,128)(2,1)S(1)} %reshape.58), channel_id=1, source_target_pairs={{0,2},{1,3},{2,4},{3,5},{4,6},{5,7},{8,10},{9,11},{10,12},{11,13},... | collective-permute-start | bytes 98312 | tf_op jit(solution)/shard_map/ppermute | solution.py:25
  228.1 7.9 %collective-permute-start.1 = (bf16[4,1,1024]{2,1,0:T(2,128)(2,1)S(1)}, bf16[4,1,1024]{2,1,0:T(2,128)(2,1)S(1)}, u32[]{:S(2)}, u32[]{:S(2)}) collective-permute-start(bf16[4,1,1024]{2,1,0:T(2,128)(2,1)S(1)} %broadcast_select_fusion.2), channel_id=1, source_target_pairs={{0,1},{1,0},{2,3},{3,2},{4,5},{5,4},{6,7},{7,6},{8,9},{9,8},{10,11... | collective-permute-start | bytes 24584 | tf_op jit(solution)/shard_map/ppermute | solution.py:29
  247.2 0.7 copy-start.5
  247.9 1.9 copy-start.4
  249.8 49.7 %copy-start.7 = (s32[16]{0:T(128)S(1)}, s32[16]{0:T(128)}, u32[]{:S(2)}) copy-start(s32[16]{0:T(128)} %param.19) | copy-start | bytes 196
where the time goes:
time: 302 us; the launch traced here: 300 us
  waiting for transfers between devices  103 us (34%)
  blocking collectives  92.5 us (31%)
  local copies, waits for them, and re-layouts  42.8 us (14%)
  matrix products  28.8 us (10%)
  starting transfers between devices  22.1 us (7%)
  other arithmetic  10.3 us (3%)
    psum x1, blocking collectives, local(): lax.psum(pooled_term.astype(jnp.bfloat16), 'seq').astype(jnp.float32)  49.3 us
    all_to_all x1, blocking collectives, local(): lax.all_to_all(ordered, 'seq', split_axis=0, concat_axis=1, tiled=True)  43.1 us
    all_to_all x1, waiting for transfers between devices, local(): lax.all_to_all(to_groups(keys_in), 'seq', split_axis=1, concat_axis=0, ti...  39.6 us
    all_to_all x1, waiting for transfers between devices, local(): lax.all_to_all(to_groups(values_in), 'seq', split_axis=1, concat_axis=0,...  29.7 us
    all_to_all x1, waiting for transfers between devices, local(): lax.all_to_all(to_groups(queries), 'seq', split_axis=1, concat_axis=0, ti...  25 us
    dot_general x4, matrix products, one_block(): jnp.einsum('hqk,khd->qhd', expo.astype(jnp.bfloat16), value_all, preferre...  12.9 us
    dot_general x4, matrix products, one_block(): jnp.einsum('qhd,khd->hqk', query_part, key_all, preferred_element_type=jn...  11.5 us
    all_to_all x1, starting transfers between devices, local(): lax.all_to_all(to_groups(keys_in), 'seq', split_axis=1, concat_axis=0, ti...  10 us
  transfers between devices with their start and end apart: 5, of which 5 were waited for; matrix products, arithmetic and copies ran while one was open for 3% of the time, Pallas kernels for 0%

commit v1 on v0

--- a/solution.py
+++ b/solution.py
@@ -17,6 +17,7 @@
 FT = 2
 RL = 8
 COLS = 64
+QUERY_BLOCK = 512
 
 
 def shifted(array, axis, by):
@@ -29,27 +30,28 @@
     return lax.ppermute(array, axis, [(i, i ^ 1 << bit) for i in range(lax.axis_size(axis))])
 
 
-def heads_attention(query_all, key_all, value_all):
-    length = query_all.shape[0]
-    block_rows = min(512, length)
-    score_scale = 1.0 / math.sqrt(query_all.shape[2])
-    query_blocks = query_all.reshape(
-        length // block_rows, block_rows, query_all.shape[1], query_all.shape[2]
-    )
+def butterfly_sum(array, axis):
+    length = lax.axis_size(axis)
+    bit = 0
+    while (1 << bit) < length:
+        array = array + swapped(array, axis, bit)
+        bit += 1
+    return array
+
+
+def head_attention(query, key, value):
+    length = query.shape[0]
+    score_scale = 1.0 / math.sqrt(query.shape[1])
+    query_blocks = query.reshape(length // QUERY_BLOCK, QUERY_BLOCK, query.shape[1])
 
     def one_block(query_part):
-        scores = (
-            jnp.einsum("qhd,khd->hqk", query_part, key_all, preferred_element_type=jnp.float32)
-            * score_scale
-        )
+        scores = jnp.dot(query_part, key.T, preferred_element_type=jnp.float32) * score_scale
         expo = jnp.exp(scores - jnp.max(scores, axis=-1, keepdims=True))
         totals = jnp.sum(expo, axis=-1, keepdims=True)
-        mixed = jnp.einsum(
-            "hqk,khd->qhd", expo.astype(jnp.bfloat16), value_all, preferred_element_type=jnp.float32
-        )
-        return (mixed / jnp.transpose(totals, (1, 0, 2))).astype(jnp.bfloat16)
+        mixed = jnp.dot(expo.astype(jnp.bfloat16), value, preferred_element_type=jnp.float32)
+        return (mixed / totals).astype(jnp.bfloat16)
 
-    return lax.map(one_block, query_blocks).reshape(length, query_all.shape[1], query_all.shape[2])
+    return lax.map(one_block, query_blocks).reshape(length, query.shape[1])
 
 
 def window_columns(volume):
@@ -87,18 +89,22 @@
     def to_groups(matrix):
         return matrix.reshape(S_DEV, group_count, heads_dev, HD)
 
-    query_all = lax.all_to_all(to_groups(queries), "seq", split_axis=1, concat_axis=0, tiled=True)
-    key_all = lax.all_to_all(to_groups(keys_in), "seq", split_axis=1, concat_axis=0, tiled=True)
-    value_all = lax.all_to_all(to_groups(values_in), "seq", split_axis=1, concat_axis=0, tiled=True)
-    mixed = heads_attention(query_all[:, 0], key_all[:, 0], value_all[:, 0])[:, None]
-    flat_heads = mixed.reshape(seq_len, heads_dev * HD)
-    ordered = flat_heads.reshape(4 * group_count, quarter, heads_dev * HD)[tile_block]
-    ordered = ordered.reshape(seq_len, 1, heads_dev, HD)
-    returned = lax.all_to_all(ordered, "seq", split_axis=0, concat_axis=1, tiled=True)
-    tile_heads = returned.reshape(S_DEV, H * HD)
-    latent = jnp.dot(tile_heads, latent_proj, preferred_element_type=jnp.float32).astype(
-        jnp.bfloat16
-    )
+    q_groups, k_groups, v_groups = to_groups(queries), to_groups(keys_in), to_groups(values_in)
+    partial = None
+    for slot in range(heads_dev):
+        stacked = jnp.stack(
+            [q_groups[:, :, slot], k_groups[:, :, slot], v_groups[:, :, slot]], axis=2
+        )
+        gathered = lax.all_to_all(stacked, "seq", split_axis=1, concat_axis=0, tiled=True)
+        head_out = head_attention(gathered[:, 0, 0], gathered[:, 0, 1], gathered[:, 0, 2])
+        proj_rows = lax.dynamic_slice_in_dim(latent_proj, (my_index * heads_dev + slot) * HD, HD, 0)
+        term = jnp.dot(head_out, proj_rows, preferred_element_type=jnp.float32)
+        partial = term if partial is None else partial + term
+
+    ordered = partial.reshape(4 * group_count, quarter, 4 * LC)[tile_block]
+    ordered = ordered.reshape(group_count, S_DEV, 4 * LC)
+    returned = lax.all_to_all(ordered, "seq", split_axis=0, concat_axis=0, tiled=True)
+    latent = jnp.sum(returned, axis=0).astype(jnp.bfloat16)
     tile_latent = (
         latent.reshape(FT, RT, WT, 2, 2, LC).transpose(0, 1, 3, 2, 4, 5).reshape(FT, RL, COLS * LC)
     )
@@ -122,7 +128,7 @@
     pooled_term = jnp.sum(weighted, axis=(0, 1)).reshape(block_count, COLS // block_count, CO).sum(
         axis=1
     ) / math.sqrt(band_voxels)
-    total_pooled = lax.psum(pooled_term.astype(jnp.bfloat16), "seq").astype(jnp.float32)
+    total_pooled = butterfly_sum(pooled_term, "seq")
     wanted_rows = my_index * BPD + jnp.arange(BPD, dtype=jnp.int32)
     chooser = (owner_slot[None, :] == wanted_rows[:, None]).astype(jnp.float32)
     policy = jnp.dot(

time: 302 us -> 232 us (0.77)
  the two profiles are of different devices: /device:TPU:56 before, /device:TPU:80 now
where the time goes in v1:
time: 232 us; the launch traced here: 230 us
  waiting for transfers between devices  84.4 us (36%)
  starting transfers between devices  42.2 us (18%)
  local copies, waits for them, and re-layouts  36 us (16%)
  matrix products  28.8 us (12%)
  blocking collectives  22.1 us (10%)
  other arithmetic  15.7 us (7%)
    all_to_all x3, waiting for transfers between devices, local(): lax.all_to_all(stacked, 'seq', split_axis=1, concat_axis=0, tiled=True)  64.9 us
    all_to_all x3, starting transfers between devices, local(): lax.all_to_all(stacked, 'seq', split_axis=1, concat_axis=0, tiled=True)  32.6 us
    all_to_all x1, blocking collectives, local(): lax.all_to_all(ordered, 'seq', split_axis=0, concat_axis=0, tiled=True)  22.1 us
    ppermute x4, waiting for transfers between devices, swapped(): lax.ppermute(array, axis, [(i, i ^ 1 << bit) for i in range(lax.axis_size...  17.9 us
    dot_general x12, matrix products, one_block(): jnp.dot(expo.astype(jnp.bfloat16), value, preferred_element_type=jnp.floa...  13.3 us
    reduce_sum x12, other arithmetic, one_block(): totals = jnp.sum(expo, axis=-1, keepdims=True)  9.87 us
    dot_general x12, matrix products, one_block(): jnp.dot(query_part, key.T, preferred_element_type=jnp.float32) * score_scale  9.45 us
    unnamed x26, local copies, waits for them, and re-layouts  7.78 us
  transfers between devices with their start and end apart: 8, of which 7 were waited for; matrix products, arithmetic and copies ran while one was open for 15% of the time, Pallas kernels for 0%

profile of v1, /device:TPU:80, one launch (start us, length us, event | category | flops | bytes accessed | tf_op | source)
XLA Modules:
  0.0 230.3 jit_solution(15857319578600572505)
XLA Ops:
  0.7 2.7 %copy.76 = bf16[256,3072]{0,1:T(8,128)(2,1)} copy(bf16[256,3072]{1,0:T(8,128)(2,1)} %param.15) | data formatting | bytes 3145728 | tf_op args[0]
  3.4 1.6 copy.77
  5.0 1.7 copy.78
  11.5 9.3 %all-to-all-start = ((bf16[256,8,3,128]{0,3,2,1:T(8,128)(2,1)}), bf16[256,8,3,128]{0,3,2,1:T(8,128)(2,1)S(1)}, u32[]{:S(2)}, u32[]{:S(2)}) async-start(bf16[256,8,3,128]{0,3,2,1:T(8,128)(2,1)} %pad_maximum_fusion), calls=%async_computation | async-start | bytes 3145728 | tf_op jit(solution)/shard_map/all_to_all | solution.py:98
  20.8 2.7 %pad_maximum_fusion.1 = bf16[256,8,3,128]{0,3,2,1:T(8,128)(2,1)} fusion(bf16[256,8,1,128]{0,3,2,1:T(8,128)(2,1)} %get-tuple-element.134, bf16[256,8,1,128]{0,3,2,1:T(8,128)(2,1)} %get-tuple-element.172, bf16[256,8,1,128]{0,3,2,1:T(8,128)(2,1)} %get-tuple-element.128), kind=kLoop, calls=%fused_computation.55 | loop fusion | flops 1572864 | bytes 3145728 | tf_op jit(solution)/shard_map/stack | solution.py:95
  24.9 38.1 %all-to-all-done = bf16[256,8,3,128]{0,3,2,1:T(8,128)(2,1)S(1)} async-done(((bf16[256,8,3,128]{0,3,2,1:T(8,128)(2,1)}), bf16[256,8,3,128]{0,3,2,1:T(8,128)(2,1)S(1)}, u32[]{:S(2)}, u32[]{:S(2)}) %all-to-all-start) | async-done | bytes 1572896 | tf_op jit(solution)/shard_map/all_to_all | solution.py:98
  63.0 19.7 %all-to-all-start.1 = ((bf16[256,8,3,128]{0,3,2,1:T(8,128)(2,1)}), bf16[256,8,3,128]{0,3,2,1:T(8,128)(2,1)}, u32[]{:S(2)}, u32[]{:S(2)}) async-start(bf16[256,8,3,128]{0,3,2,1:T(8,128)(2,1)} %pad_maximum_fusion.1), calls=%async_computation.1 | async-start | bytes 3145728 | tf_op jit(solution)/shard_map/all_to_all | solution.py:98
  82.7 1.6 copy.79
  85.8 10.1 %while.30 = (s32[]{:T(128)}, bf16[4,512,128]{2,1,0:T(8,128)(2,1)S(1)}, bf16[4,512,128]{2,1,0:T(8,128)(2,1)S(1)}, bf16[2048,128]{1,0:T(8,128)(2,1)S(1)}, bf16[2048,128]{1,0:T(8,128)(2,1)S(1)}, /*index=5*/s32[]{:T(128)}) while((s32[]{:T(128)}, bf16[4,512,128]{2,1,0:T(8,128)(2,1)S(1)}, bf16[4,512,128]{2,1,0:T(8,128)(2,1)S(1)}, ...), condition=%wide.region_3.4_spmd, body=%wide.region_0.3_spmd.sunk | while | flops 545389568 | bytes 13903949 | solution.py:54
  96.0 26.9 %all-to-all-done.1 = bf16[256,8,3,128]{0,3,2,1:T(8,128)(2,1)} async-done(((bf16[256,8,3,128]{0,3,2,1:T(8,128)(2,1)}), bf16[256,8,3,128]{0,3,2,1:T(8,128)(2,1)}, u32[]{:S(2)}, u32[]{:S(2)}) %all-to-all-start.1) | async-done | bytes 1572896 | tf_op jit(solution)/shard_map/all_to_all | solution.py:98
  122.8 3.6 %all-to-all-start.2 = ((bf16[256,8,3,128]{0,3,2,1:T(8,128)(2,1)}), bf16[256,8,3,128]{0,3,2,1:T(8,128)(2,1)S(1)}, u32[]{:S(2)}, u32[]{:S(2)}) async-start(bf16[256,8,3,128]{0,3,2,1:T(8,128)(2,1)} %pad_maximum_fusion.2), calls=%async_computation.2 | async-start | bytes 3145728 | tf_op jit(solution)/shard_map/all_to_all | solution.py:98
  126.4 2.6 %copy.80 = bf16[8,256,1,3,128]{4,1,0,3,2:T(8,128)(2,1)} copy(bf16[8,256,1,3,128]{1,4,3,0,2:T(8,128)(2,1)} %bitcast.17) | data formatting | bytes 3145728 | tf_op jit(solution)/shard_map/all_to_all | solution.py:98
  129.0 2.3 slice_bitcast_fusion.2
  132.2 13.3 %while.31 = (s32[]{:T(128)}, bf16[4,512,128]{2,1,0:T(8,128)(2,1)}, bf16[4,512,128]{2,1,0:T(8,128)(2,1)S(1)}, bf16[2048,128]{1,0:T(8,128)(2,1)S(1)}, bf16[2048,128]{1,0:T(8,128)(2,1)}, /*index=5*/s32[]{:T(128)}) while((s32[]{:T(128)}, bf16[4,512,128]{2,1,0:T(8,128)(2,1)}, bf16[4,512,128]{2,1,0:T(8,128)(2,1)S(1)}, ...), condition=%wide.region_7.8_spmd, body=%wide.region_4.7_spmd.sunk | while | flops 545389568 | bytes 16001637 | solution.py:54
  134.0 1.5 fusion.121
  137.3 1.5 fusion.121
  140.7 1.5 fusion.121
  144.0 1.5 fusion.121
  145.5 1.6 copy.81
  148.7 10.1 %while.32 = (s32[]{:T(128)}, bf16[4,512,128]{2,1,0:T(8,128)(2,1)S(1)}, bf16[4,512,128]{2,1,0:T(8,128)(2,1)S(1)}, bf16[2048,128]{1,0:T(8,128)(2,1)S(1)}, bf16[2048,128]{1,0:T(8,128)(2,1)S(1)}, /*index=5*/s32[]{:T(128)}) while((s32[]{:T(128)}, bf16[4,512,128]{2,1,0:T(8,128)(2,1)S(1)}, bf16[4,512,128]{2,1,0:T(8,128)(2,1)S(1)}, ...), condition=%wide.region_11.12_spmd, body=%wide.region_8.11_spmd.sunk | while | flops 545389568 | bytes 13903949 | solution.py:54
  163.5 22.1 %all_to_all.59 = f32[8,256,64]{1,2,0:T(8,128)S(1)} all-to-all(f32[8,256,64]{1,2,0:T(8,128)S(1)} %copy.83), channel_id=1, replica_groups=mesh['roll'=32,'seq'=8] {'seq'}, dimensions={0} | all-to-all | bytes 1048576 | tf_op jit(solution)/shard_map/all_to_all | solution.py:106
  186.4 2.2 collective-permute-start
  188.6 1.6 collective-permute-done
  191.4 6.6 %collective-permute-done.1 = bf16[4,1,1024]{2,1,0:T(2,128)(2,1)S(1)} collective-permute-done((bf16[4,1,1024]{2,1,0:T(2,128)(2,1)S(1)}, bf16[4,1,1024]{2,1,0:T(2,128)(2,1)S(1)}, u32[]{:S(2)}, u32[]{:S(2)}) %collective-permute-start.1) | collective-permute-done | bytes 8224 | tf_op jit(solution)/shard_map/ppermute | solution.py:30
  200.1 1.8 pad_slice_fusion
  203.1 5.9 %concatenate.11 = bf16[2,8,64,432]{3,2,0,1:T(8,128)(2,1)S(1)} concatenate(bf16[2,8,64,16]{3,2,0,1:T(8,128)(2,1)} %get-tuple-element.168, bf16[2,8,64,16]{3,2,0,1:T(8,128)(2,1)} %get-tuple-element.167, bf16[2,8,64,16]{3,2,0,1:T(8,128)(2,1)} %get-tuple-element.143, bf16[2,8,64,16]{3,2,0,1:T(8,128)(2,1)} %get-tuple-element.144, bf16[2,8,64,16]{3,2,0,1:T(8,128)(2,1)} %get-tuple-element.166, ...), dimensions={3} | concatenate | bytes 1769472 | tf_op jit(solution)/shard_map/concatenate | solution.py:67
  209.7 1.9 divide_multiply_fusion
  213.1 6.8 %collective-permute-done.2 = f32[16,512]{1,0:T(8,128)S(1)} collective-permute-done((f32[16,512]{1,0:T(8,128)S(1)}, f32[16,512]{1,0:T(8,128)S(1)}, u32[]{:S(2)}, u32[]{:S(2)}) %collective-permute-start.2) | collective-permute-done | bytes 32800 | tf_op jit(solution)/shard_map/ppermute | solution.py:30
  219.9 2.3 %collective-permute-start.3 = (f32[16,512]{1,0:T(8,128)S(1)}, f32[16,512]{1,0:T(8,128)S(1)}, u32[]{:S(2)}, u32[]{:S(2)}) collective-permute-start(f32[16,512]{1,0:T(8,128)S(1)} %fusion.81), channel_id=1, source_target_pairs={{0,2},{1,3},{2,0},{3,1},{4,6},{5,7},{6,4},{7,5},{8,10},{9,11},{10,... | collective-permute-start | bytes 98312 | tf_op jit(solution)/shard_map/ppermute | solution.py:30
  222.2 1.9 collective-permute-done.3
  224.1 2.8 %collective-permute-start.4 = (f32[16,512]{1,0:T(8,128)S(1)}, f32[16,512]{1,0:T(8,128)S(1)}, u32[]{:S(2)}, u32[]{:S(2)}) collective-permute-start(f32[16,512]{1,0:T(8,128)S(1)} %add.89), channel_id=1, source_target_pairs={{0,4},{1,5},{2,6},{3,7},{4,0},{5,1},{6,2},{7,3},{8,12},{9,13},{10,... | collective-permute-start | bytes 98312 | tf_op jit(solution)/shard_map/ppermute | solution.py:30
  226.9 2.6 %collective-permute-done.4 = f32[16,512]{1,0:T(8,128)S(1)} collective-permute-done((f32[16,512]{1,0:T(8,128)S(1)}, f32[16,512]{1,0:T(8,128)S(1)}, u32[]{:S(2)}, u32[]{:S(2)}) %collective-permute-start.4) | collective-permute-done | bytes 32800 | tf_op jit(solution)/shard_map/ppermute | solution.py:30
  (104 shorter events, 50.4 us)
Async XLA Ops:
  0.6 208.5 %copy-start = (bf16[432,512]{1,0:T(8,128)(2,1)S(1)}, bf16[432,512]{1,0:T(8,128)(2,1)}, u32[]{:S(2)}) copy-start(bf16[432,512]{1,0:T(8,128)(2,1)} %param.19) | copy-start | bytes 1327108
  0.6 2.8 %copy-start.6 = (bf16[256,3072]{1,0:T(8,128)(2,1)S(1)}, bf16[256,3072]{1,0:T(8,128)(2,1)}, u32[]{:S(2)}) copy-start(bf16[256,3072]{1,0:T(8,128)(2,1)} %param.16) | copy-start | bytes 4718596
  6.7 1.8 copy-start.1
  6.7 2.3 copy-start.2
  11.5 9.3 %copy-start.11 = (s32[32]{0:T(128)S(1)}, s32[32]{0:T(128)}, u32[]{:S(2)}) copy-start(s32[32]{0:T(128)} %param.22) | copy-start | bytes 388
  11.5 51.4 %all-to-all-start = ((bf16[256,8,3,128]{0,3,2,1:T(8,128)(2,1)}), bf16[256,8,3,128]{0,3,2,1:T(8,128)(2,1)S(1)}, u32[]{:S(2)}, u32[]{:S(2)}) async-start(bf16[256,8,3,128]{0,3,2,1:T(8,128)(2,1)} %pad_maximum_fusion), calls=%async_computation | async-start | bytes 3145728 | tf_op jit(solution)/shard_map/all_to_all | solution.py:98
  20.8 2.8 %copy-start.5 = (bf16[256,8,1,128]{0,3,2,1:T(8,128)(2,1)S(1)}, bf16[256,8,1,128]{0,3,2,1:T(8,128)(2,1)}, u32[]{:S(2)}) copy-start(bf16[256,8,1,128]{0,3,2,1:T(8,128)(2,1)} %get-tuple-element.133) | copy-start | bytes 1572868
  63.0 59.9 %all-to-all-start.1 = ((bf16[256,8,3,128]{0,3,2,1:T(8,128)(2,1)}), bf16[256,8,3,128]{0,3,2,1:T(8,128)(2,1)}, u32[]{:S(2)}, u32[]{:S(2)}) async-start(bf16[256,8,3,128]{0,3,2,1:T(8,128)(2,1)} %pad_maximum_fusion.1), calls=%async_computation.1 | async-start | bytes 3145728 | tf_op jit(solution)/shard_map/all_to_all | solution.py:98
  95.9 26.9 %copy-start.3 = (bf16[4,512,128]{2,1,0:T(8,128)(2,1)}, bf16[4,512,128]{2,1,0:T(8,128)(2,1)S(1)}, u32[]{:S(2)}) copy-start(bf16[4,512,128]{2,1,0:T(8,128)(2,1)S(1)} %get-tuple-element.83) | copy-start | bytes 1572868
  122.8 22.7 %all-to-all-start.2 = ((bf16[256,8,3,128]{0,3,2,1:T(8,128)(2,1)}), bf16[256,8,3,128]{0,3,2,1:T(8,128)(2,1)S(1)}, u32[]{:S(2)}, u32[]{:S(2)}) async-start(bf16[256,8,3,128]{0,3,2,1:T(8,128)(2,1)} %pad_maximum_fusion.2), calls=%async_computation.2 | async-start | bytes 3145728 | tf_op jit(solution)/shard_map/all_to_all | solution.py:98
  133.0 1.0 copy-start.7
  136.3 1.0 copy-start.7
  139.6 1.0 copy-start.7
  143.0 1.0 copy-start.7
  148.7 10.2 %copy-start.4 = (bf16[4,512,128]{2,1,0:T(8,128)(2,1)S(1)}, bf16[4,512,128]{2,1,0:T(8,128)(2,1)}, u32[]{:S(2)}) copy-start(bf16[4,512,128]{2,1,0:T(8,128)(2,1)} %copy-done.3) | copy-start | bytes 1572868
  186.4 3.8 %collective-permute-start = (bf16[2,8,1024]{2,1,0:T(8,128)(2,1)S(1)}, bf16[2,8,1024]{2,1,0:T(8,128)(2,1)S(1)}, u32[]{:S(2)}, u32[]{:S(2)}) collective-permute-start(bf16[2,8,1024]{2,1,0:T(8,128)(2,1)S(1)} %reshape.70), channel_id=1, source_target_pairs={{0,2},{1,3},{2,4},{3,5},{4,6},{5,7},{8,10},{9,11},{10,12},{11,13},... | collective-permute-start | bytes 98312 | tf_op jit(solution)/shard_map/ppermute | solution.py:26
  190.2 7.7 %collective-permute-start.1 = (bf16[4,1,1024]{2,1,0:T(2,128)(2,1)S(1)}, bf16[4,1,1024]{2,1,0:T(2,128)(2,1)S(1)}, u32[]{:S(2)}, u32[]{:S(2)}) collective-permute-start(bf16[4,1,1024]{2,1,0:T(2,128)(2,1)S(1)} %broadcast_select_fusion.2), channel_id=1, source_target_pairs={{0,1},{1,0},{2,3},{3,2},{4,5},{5,4},{6,7},{7,6},{8,9},{9,8},{10,11... | collective-permute-start | bytes 24584 | tf_op jit(solution)/shard_map/ppermute | solution.py:30
  209.0 0.7 copy-start.10
  209.7 1.9 copy-start.8
  211.6 17.9 %copy-start.9 = (s32[16]{0:T(128)S(1)}, s32[16]{0:T(128)}, u32[]{:S(2)}) copy-start(s32[16]{0:T(128)} %param.23) | copy-start | bytes 196
  212.0 7.9 %collective-permute-start.2 = (f32[16,512]{1,0:T(8,128)S(1)}, f32[16,512]{1,0:T(8,128)S(1)}, u32[]{:S(2)}, u32[]{:S(2)}) collective-permute-start(f32[16,512]{1,0:T(8,128)S(1)} %broadcast_multiply_fusion), channel_id=1, source_target_pairs={{0,1},{1,0},{2,3},{3,2},{4,5},{5,4},{6,7},{7,6},{8,9},{9,8},{10,11... | collective-permute-start | bytes 98312 | tf_op jit(solution)/shard_map/ppermute | solution.py:30
  219.9 4.2 %collective-permute-start.3 = (f32[16,512]{1,0:T(8,128)S(1)}, f32[16,512]{1,0:T(8,128)S(1)}, u32[]{:S(2)}, u32[]{:S(2)}) collective-permute-start(f32[16,512]{1,0:T(8,128)S(1)} %fusion.81), channel_id=1, source_target_pairs={{0,2},{1,3},{2,0},{3,1},{4,6},{5,7},{6,4},{7,5},{8,10},{9,11},{10,... | collective-permute-start | bytes 98312 | tf_op jit(solution)/shard_map/ppermute | solution.py:30
  224.1 5.4 %collective-permute-start.4 = (f32[16,512]{1,0:T(8,128)S(1)}, f32[16,512]{1,0:T(8,128)S(1)}, u32[]{:S(2)}, u32[]{:S(2)}) collective-permute-start(f32[16,512]{1,0:T(8,128)S(1)} %add.89), channel_id=1, source_target_pairs={{0,4},{1,5},{2,6},{3,7},{4,0},{5,1},{6,2},{7,3},{8,12},{9,13},{10,... | collective-permute-start | bytes 98312 | tf_op jit(solution)/shard_map/ppermute | solution.py:30

commit v2 on v1

--- a/solution.py
+++ b/solution.py
@@ -37,6 +37,17 @@
         array = array + swapped(array, axis, bit)
         bit += 1
     return array
+
+
+def exchange_sum(blocks, axis, my_index):
+    length = lax.axis_size(axis)
+    total = lax.dynamic_index_in_dim(blocks, my_index, 0, keepdims=False)
+    for step in range(1, length):
+        piece = lax.dynamic_index_in_dim(blocks, (my_index + step) % length, 0, keepdims=False)
+        total = total + lax.ppermute(
+            piece, axis, [(i, (i + step) % length) for i in range(length)]
+        )
+    return total
 
 
 def head_attention(query, key, value):
@@ -103,24 +114,35 @@
 
     ordered = partial.reshape(4 * group_count, quarter, 4 * LC)[tile_block]
     ordered = ordered.reshape(group_count, S_DEV, 4 * LC)
-    returned = lax.all_to_all(ordered, "seq", split_axis=0, concat_axis=0, tiled=True)
-    latent = jnp.sum(returned, axis=0).astype(jnp.bfloat16)
+    latent = exchange_sum(ordered, "seq", my_index).astype(jnp.bfloat16)
     tile_latent = (
         latent.reshape(FT, RT, WT, 2, 2, LC).transpose(0, 1, 3, 2, 4, 5).reshape(FT, RL, COLS * LC)
     )
-    earlier = shifted(tile_latent, "seq", TR)
-    extended = jnp.concatenate([earlier, tile_latent], axis=0)
     band_row = my_index % TR
     upper_band = band_row == 0
-    outgoing = jnp.where(upper_band, extended[:, RL - 1 :], extended[:, :1])
-    incoming = swapped(outgoing, "seq", 0)
+    outgoing = jnp.where(upper_band, tile_latent[:, RL - 1 :], tile_latent[:, :1])
+    earlier = shifted(tile_latent, "seq", TR)
+    beside = swapped(outgoing, "seq", 0)
+    diagonal = lax.ppermute(
+        outgoing,
+        "seq",
+        [(i, (i ^ 1) + TR) for i in range(group_count) if (i ^ 1) + TR < group_count],
+    )
+    extended = jnp.concatenate([earlier, tile_latent], axis=0)
+    incoming = jnp.concatenate([diagonal, beside], axis=0)
     above = jnp.where(upper_band, jnp.zeros_like(incoming), incoming)
     below = jnp.where(upper_band, incoming, jnp.zeros_like(incoming))
     volume = jnp.concatenate([above, extended, below], axis=1).reshape(FT + 2, RL + 2, COLS, LC)
     volume = jnp.pad(volume, ((0, 0), (0, 0), (1, 1), (0, 0)))
-    pre_act = (
-        jnp.dot(window_columns(volume), conv_weight, preferred_element_type=jnp.float32) + conv_bias
-    )
+    kernel = conv_weight.reshape(3, 3, 3, LC, CO)
+    pre_act = lax.conv_general_dilated(
+        volume[None],
+        kernel,
+        window_strides=(1, 1, 1),
+        padding="VALID",
+        dimension_numbers=("NDHWC", "DHWIO", "NDHWC"),
+        preferred_element_type=jnp.float32,
+    )[0] + conv_bias
     decoded = pre_act.astype(jnp.bfloat16).reshape(1, FT, RL, COLS, CO)
     block_count = BPD * group_count
     band_voxels = group_count // TR * FT * TR * RL * (COLS // block_count)
@@ -128,12 +150,12 @@
     pooled_term = jnp.sum(weighted, axis=(0, 1)).reshape(block_count, COLS // block_count, CO).sum(
         axis=1
     ) / math.sqrt(band_voxels)
-    total_pooled = butterfly_sum(pooled_term, "seq")
-    wanted_rows = my_index * BPD + jnp.arange(BPD, dtype=jnp.int32)
-    chooser = (owner_slot[None, :] == wanted_rows[:, None]).astype(jnp.float32)
-    policy = jnp.dot(
-        chooser, total_pooled, precision=lax.Precision.HIGHEST, preferred_element_type=jnp.float32
+    slots = jnp.arange(block_count, dtype=jnp.int32)
+    chooser = (owner_slot[None, :] == slots[:, None]).astype(jnp.float32)
+    by_owner = jnp.dot(
+        chooser, pooled_term, precision=lax.Precision.HIGHEST, preferred_element_type=jnp.float32
     )
+    policy = exchange_sum(by_owner.reshape(group_count, BPD, CO), "seq", my_index)
     return (decoded, policy)
 
 

time: 232 us -> 243 us (1.047)
  starting transfers between devices: 42.2 us -> 83.4 us
  blocking collectives: 22.1 us -> 0 us
  waiting for transfers between devices: 84.4 us -> 78.4 us
    ppermute x0 -> x15, starting transfers between devices: none -> 47.1 us  [the longest x14 38.9 us: exchange_sum(): lax.ppermute(piece, axis, [(i, (i + step) % length) for i in range(length)])]
    all_to_all x1 -> x0, blocking collectives: 22.1 us -> none  [local(): lax.all_to_all(ordered, 'seq', split_axis=0, concat_axis=0, tiled=True)]
    ppermute x4 -> x1, waiting for transfers between devices: 17.9 us -> 0.01 us  [swapped(): lax.ppermute(array, axis, [(i, i ^ 1 << bit) for i in range(lax.axis_size...]
    ppermute x0 -> x15, waiting for transfers between devices: none -> 12.5 us  [the longest x14 12.5 us: exchange_sum(): lax.ppermute(piece, axis, [(i, (i + step) % length) for i in range(length)])]
    ppermute x4 -> x1, starting transfers between devices: 7.38 us -> 0.09 us  [swapped(): lax.ppermute(array, axis, [(i, i ^ 1 << bit) for i in range(lax.axis_size...]
    concatenate x3 -> x4, local copies, waits for them, and re-layouts: 6.07 us -> 0.34 us  [local(): incoming = jnp.concatenate([diagonal, beside], axis=0)]
    slice x3 -> x0, local copies, waits for them, and re-layouts: 4.52 us -> none  [window_columns(): volume[a:a + frame_count, b:b + row_count, c:c + col_count]]
    conv_general_dilated x0 -> x4, local copies, waits for them, and re-layouts: none -> 4.4 us  [local(): lax.conv_general_dilated(volume[None], kernel, window_strides=(1, 1, 1),...]
  transfers between devices with their start and end apart: 8 -> 20, of which waited for: 7 -> 7; matrix products, arithmetic and copies ran while one was open for 15% -> 16% of each run, Pallas kernels for 0% -> 0%
where the time goes in v2:
time: 243 us; the launch traced here: 241 us
  starting transfers between devices  83.4 us (34%)
  waiting for transfers between devices  78.4 us (32%)
  local copies, waits for them, and re-layouts  33.9 us (14%)
  matrix products  27.3 us (11%)
  other arithmetic  17.1 us (7%)
    all_to_all x3, waiting for transfers between devices, local(): lax.all_to_all(stacked, 'seq', split_axis=1, concat_axis=0, tiled=True)  64.9 us
    ppermute x14, starting transfers between devices, exchange_sum(): lax.ppermute(piece, axis, [(i, (i + step) % length) for i in range(length)])  38.9 us
    all_to_all x3, starting transfers between devices, local(): lax.all_to_all(stacked, 'seq', split_axis=1, concat_axis=0, tiled=True)  32.6 us
    dot_general x12, matrix products, one_block(): jnp.dot(expo.astype(jnp.bfloat16), value, preferred_element_type=jnp.floa...  13.2 us
    ppermute x14, waiting for transfers between devices, exchange_sum(): lax.ppermute(piece, axis, [(i, (i + step) % length) for i in range(length)])  12.5 us
    reduce_sum x12, other arithmetic, one_block(): totals = jnp.sum(expo, axis=-1, keepdims=True)  9.84 us
    dot_general x12, matrix products, one_block(): jnp.dot(query_part, key.T, preferred_element_type=jnp.float32) * score_scale  9.44 us
    ppermute x1, starting transfers between devices, local(): lax.ppermute(outgoing, 'seq', [(i, (i ^ 1) + TR) for i in range(group_cou...  8.2 us
  transfers between devices with their start and end apart: 20, of which 7 were waited for; matrix products, arithmetic and copies ran while one was open for 16% of the time, Pallas kernels for 0%

profile of v2, /device:TPU:80, one launch (start us, length us, event | category | flops | bytes accessed | tf_op | source)
XLA Modules:
  0.0 241.4 jit_solution(14955616741855011813)
XLA Ops:
  0.6 1.8 copy.117
  3.6 1.7 copy.115
  5.3 2.6 %copy.116 = bf16[256,3072]{0,1:T(8,128)(2,1)} copy(bf16[256,3072]{1,0:T(8,128)(2,1)} %param.16) | data formatting | bytes 3145728 | tf_op args[1]
  7.9 2.7 %fusion.120 = (bf16[256,8,1,128]{0,3,2,1:T(8,128)(2,1)S(1)}, bf16[256,8,1,128]{0,3,2,1:T(8,128)(2,1)}, bf16[256,8,1,128]{0,3,2,1:T(8,128)(2,1)S(1)}, bf16[256,8,...) fusion(bf16[256,8,3,128]{0,3,2,1:T(8,128)(2,1)S(1)} %bitcast.184, ...), kind=kLoop, calls=%fused_computation.144 | loop fusion | bytes 6291456 | tf_op jit(solution)/shard_map/slice | solution.py:107
  11.9 9.3 %all-to-all-start = ((bf16[256,8,3,128]{0,3,2,1:T(8,128)(2,1)}), bf16[256,8,3,128]{0,3,2,1:T(8,128)(2,1)S(1)}, u32[]{:S(2)}, u32[]{:S(2)}) async-start(bf16[256,8,3,128]{0,3,2,1:T(8,128)(2,1)} %pad_maximum_fusion), calls=%async_computation | async-start | bytes 3145728 | tf_op jit(solution)/shard_map/all_to_all | solution.py:109
  21.2 2.7 %pad_maximum_fusion.1 = bf16[256,8,3,128]{0,3,2,1:T(8,128)(2,1)} fusion(bf16[256,8,1,128]{0,3,2,1:T(8,128)(2,1)} %get-tuple-element.142, bf16[256,8,1,128]{0,3,2,1:T(8,128)(2,1)} %get-tuple-element.170, bf16[256,8,1,128]{0,3,2,1:T(8,128)(2,1)} %get-tuple-element.136), kind=kLoop, calls=%fused_computation.58 | loop fusion | flops 1572864 | bytes 3145728 | tf_op jit(solution)/shard_map/stack | solution.py:106
  25.3 38.1 %all-to-all-done = bf16[256,8,3,128]{0,3,2,1:T(8,128)(2,1)S(1)} async-done(((bf16[256,8,3,128]{0,3,2,1:T(8,128)(2,1)}), bf16[256,8,3,128]{0,3,2,1:T(8,128)(2,1)S(1)}, u32[]{:S(2)}, u32[]{:S(2)}) %all-to-all-start) | async-done | bytes 1572896 | tf_op jit(solution)/shard_map/all_to_all | solution.py:109
  63.4 19.7 %all-to-all-start.1 = ((bf16[256,8,3,128]{0,3,2,1:T(8,128)(2,1)}), bf16[256,8,3,128]{0,3,2,1:T(8,128)(2,1)}, u32[]{:S(2)}, u32[]{:S(2)}) async-start(bf16[256,8,3,128]{0,3,2,1:T(8,128)(2,1)} %pad_maximum_fusion.1), calls=%async_computation.1 | async-start | bytes 3145728 | tf_op jit(solution)/shard_map/all_to_all | solution.py:109
  86.2 10.1 %while.30 = (s32[]{:T(128)}, bf16[4,512,128]{2,1,0:T(8,128)(2,1)S(1)}, bf16[4,512,128]{2,1,0:T(8,128)(2,1)S(1)}, bf16[2048,128]{1,0:T(8,128)(2,1)S(1)}, bf16[2048,128]{1,0:T(8,128)(2,1)S(1)}, /*index=5*/s32[]{:T(128)}) while((s32[]{:T(128)}, bf16[4,512,128]{2,1,0:T(8,128)(2,1)S(1)}, bf16[4,512,128]{2,1,0:T(8,128)(2,1)S(1)}, ...), condition=%wide.region_3.4_spmd, body=%wide.region_0.3_spmd.sunk | while | flops 545389568 | bytes 13903957 | solution.py:65
  96.4 26.9 %all-to-all-done.1 = bf16[256,8,3,128]{0,3,2,1:T(8,128)(2,1)} async-done(((bf16[256,8,3,128]{0,3,2,1:T(8,128)(2,1)}), bf16[256,8,3,128]{0,3,2,1:T(8,128)(2,1)}, u32[]{:S(2)}, u32[]{:S(2)}) %all-to-all-start.1) | async-done | bytes 1572896 | tf_op jit(solution)/shard_map/all_to_all | solution.py:109
  123.2 3.6 %all-to-all-start.2 = ((bf16[256,8,3,128]{0,3,2,1:T(8,128)(2,1)}), bf16[256,8,3,128]{0,3,2,1:T(8,128)(2,1)S(1)}, u32[]{:S(2)}, u32[]{:S(2)}) async-start(bf16[256,8,3,128]{0,3,2,1:T(8,128)(2,1)} %pad_maximum_fusion.2), calls=%async_computation.2 | async-start | bytes 3145728 | tf_op jit(solution)/shard_map/all_to_all | solution.py:109
  126.8 2.6 %copy.119 = bf16[8,256,1,3,128]{4,1,0,3,2:T(8,128)(2,1)} copy(bf16[8,256,1,3,128]{1,4,3,0,2:T(8,128)(2,1)} %bitcast.17) | data formatting | bytes 3145728 | tf_op jit(solution)/shard_map/all_to_all | solution.py:109
  129.4 2.2 slice_bitcast_fusion.4
  132.5 13.3 %while.31 = (s32[]{:T(128)}, bf16[4,512,128]{2,1,0:T(8,128)(2,1)}, bf16[4,512,128]{2,1,0:T(8,128)(2,1)S(1)}, bf16[2048,128]{1,0:T(8,128)(2,1)S(1)}, bf16[2048,128]{1,0:T(8,128)(2,1)}, /*index=5*/s32[]{:T(128)}) while((s32[]{:T(128)}, bf16[4,512,128]{2,1,0:T(8,128)(2,1)}, bf16[4,512,128]{2,1,0:T(8,128)(2,1)S(1)}, ...), condition=%wide.region_7.8_spmd, body=%wide.region_4.7_spmd.sunk | while | flops 545389568 | bytes 16001137 | solution.py:65
  147.4 2.3 slice_bitcast_fusion.2
  149.8 11.0 %while.32 = (s32[]{:T(128)}, bf16[4,512,128]{2,1,0:T(8,128)(2,1)S(1)}, bf16[4,512,128]{2,1,0:T(8,128)(2,1)S(1)}, bf16[2048,128]{1,0:T(8,128)(2,1)S(1)}, bf16[2048,128]{1,0:T(8,128)(2,1)}, /*index=5*/s32[]{:T(128)}) while((s32[]{:T(128)}, bf16[4,512,128]{2,1,0:T(8,128)(2,1)S(1)}, bf16[4,512,128]{2,1,0:T(8,128)(2,1)S(1)}, ...), condition=%wide.region_11.12_spmd, body=%wide.region_8.11_spmd.sunk | while | flops 545389568 | bytes 16001137 | solution.py:65
  165.0 8.2 %collective-permute-start.6 = (f32[256,64]{0,1:T(8,128)S(1)}, f32[256,64]{0,1:T(8,128)S(1)}, u32[]{:S(2)}, u32[]{:S(2)}) collective-permute-start(f32[256,64]{0,1:T(8,128)S(1)} %bitcast.203), channel_id=1, source_target_pairs={{0,7},{1,0},{2,1},{3,2},{4,3},{5,4},{6,5},{7,6},{8,15},{9,8},{10,9... | collective-permute-start | bytes 196616 | tf_op jit(solution)/shard_map/ppermute | solution.py:47
  175.0 2.8 %collective-permute-start.3 = (f32[256,64]{0,1:T(8,128)S(1)}, f32[256,64]{0,1:T(8,128)S(1)}, u32[]{:S(2)}, u32[]{:S(2)}) collective-permute-start(f32[256,64]{0,1:T(8,128)S(1)} %bitcast.198), channel_id=1, source_target_pairs={{0,4},{1,5},{2,6},{3,7},{4,0},{5,1},{6,2},{7,3},{8,12},{9,13},{10,... | collective-permute-start | bytes 196616 | tf_op jit(solution)/shard_map/ppermute | solution.py:47
  177.9 3.7 %collective-permute-start.2 = (f32[256,64]{0,1:T(8,128)S(1)}, f32[256,64]{0,1:T(8,128)S(1)}, u32[]{:S(2)}, u32[]{:S(2)}) collective-permute-start(f32[256,64]{0,1:T(8,128)S(1)} %bitcast.199), channel_id=1, source_target_pairs={{0,3},{1,4},{2,5},{3,6},{4,7},{5,0},{6,1},{7,2},{8,11},{9,12},{10,... | collective-permute-start | bytes 196616 | tf_op jit(solution)/shard_map/ppermute | solution.py:47
  181.7 2.1 collective-permute-start.1
  185.4 3.2 %collective-permute-done.2 = f32[256,64]{0,1:T(8,128)S(1)} collective-permute-done((f32[256,64]{0,1:T(8,128)S(1)}, f32[256,64]{0,1:T(8,128)S(1)}, u32[]{:S(2)}, u32[]{:S(2)}) %collective-permute-start.2) | collective-permute-done | bytes 65568 | tf_op jit(solution)/shard_map/ppermute | solution.py:47
  189.2 4.9 %collective-permute-done = f32[256,64]{0,1:T(8,128)S(1)} collective-permute-done((f32[256,64]{0,1:T(8,128)S(1)}, f32[256,64]{0,1:T(8,128)S(1)}, u32[]{:S(2)}, u32[]{:S(2)}) %collective-permute-start) | collective-permute-done | bytes 65568 | tf_op jit(solution)/shard_map/ppermute | solution.py:47
  194.9 8.2 %collective-permute-start.7 = (bf16[2,1,1024]{2,1,0:T(2,128)(2,1)S(1)}, bf16[2,1,1024]{2,1,0:T(2,128)(2,1)S(1)}, u32[]{:S(2)}, u32[]{:S(2)}) collective-permute-start(bf16[2,1,1024]{2,1,0:T(2,128)(2,1)S(1)} %broadcast_select_fusion), channel_id=1, source_target_pairs={{0,3},{1,2},{2,5},{3,4},{4,7},{5,6},{8,11},{9,10},{10,13},{11,12},... | collective-permute-start | bytes 12296 | tf_op jit(solution)/shard_map/ppermute | solution.py:126
  203.2 3.7 %collective-permute-start.9 = (bf16[2,8,1024]{2,1,0:T(8,128)(2,1)S(1)}, bf16[2,8,1024]{2,1,0:T(8,128)(2,1)S(1)}, u32[]{:S(2)}, u32[]{:S(2)}) collective-permute-start(bf16[2,8,1024]{2,1,0:T(8,128)(2,1)S(1)} %reshape.145), channel_id=1, source_target_pairs={{0,2},{1,3},{2,4},{3,5},{4,6},{5,7},{8,10},{9,11},{10,12},{11,13},... | collective-permute-start | bytes 98312 | tf_op jit(solution)/shard_map/ppermute | solution.py:26
  209.9 2.2 copy.137
  216.2 4.0 %collective-permute-start.16 = (f32[2,512]{1,0:T(2,128)S(1)}, f32[2,512]{1,0:T(2,128)S(1)}, u32[]{:S(2)}, u32[]{:S(2)}) collective-permute-start(f32[2,512]{1,0:T(2,128)S(1)} %get-tuple-element.159), channel_id=1, source_target_pairs={{0,7},{1,0},{2,1},{3,2},{4,3},{5,4},{6,5},{7,6},{8,15},{9,8},{10,9... | collective-permute-start | bytes 12296 | tf_op jit(solution)/shard_map/ppermute | solution.py:47
  220.2 2.0 collective-permute-start.15
  222.6 4.2 %collective-permute-start.14 = (f32[2,512]{1,0:T(2,128)S(1)}, f32[2,512]{1,0:T(2,128)S(1)}, u32[]{:S(2)}, u32[]{:S(2)}) collective-permute-start(f32[2,512]{1,0:T(2,128)S(1)} %get-tuple-element.161), channel_id=1, source_target_pairs={{0,5},{1,6},{2,7},{3,0},{4,1},{5,2},{6,3},{7,4},{8,13},{9,14},{10,... | collective-permute-start | bytes 12296 | tf_op jit(solution)/shard_map/ppermute | solution.py:47
  226.8 2.7 %collective-permute-start.12 = (f32[2,512]{1,0:T(2,128)S(1)}, f32[2,512]{1,0:T(2,128)S(1)}, u32[]{:S(2)}, u32[]{:S(2)}) collective-permute-start(f32[2,512]{1,0:T(2,128)S(1)} %get-tuple-element.163), channel_id=1, source_target_pairs={{0,3},{1,4},{2,5},{3,6},{4,7},{5,0},{6,1},{7,2},{8,11},{9,12},{10,... | collective-permute-start | bytes 12296 | tf_op jit(solution)/shard_map/ppermute | solution.py:47
  229.5 1.7 collective-permute-start.11
  231.2 4.5 %collective-permute-start.10 = (f32[2,512]{1,0:T(2,128)S(1)}, f32[2,512]{1,0:T(2,128)S(1)}, u32[]{:S(2)}, u32[]{:S(2)}) collective-permute-start(f32[2,512]{1,0:T(2,128)S(1)} %get-tuple-element.158), channel_id=1, source_target_pairs={{0,1},{1,2},{2,3},{3,4},{4,5},{5,6},{6,7},{7,0},{8,9},{9,10},{10,1... | collective-permute-start | bytes 12296 | tf_op jit(solution)/shard_map/ppermute | solution.py:47
  237.1 3.7 %collective-permute-done.10 = f32[2,512]{1,0:T(2,128)S(1)} collective-permute-done((f32[2,512]{1,0:T(2,128)S(1)}, f32[2,512]{1,0:T(2,128)S(1)}, u32[]{:S(2)}, u32[]{:S(2)}) %collective-permute-start.10) | collective-permute-done | bytes 4128 | tf_op jit(solution)/shard_map/ppermute | solution.py:47
  (151 shorter events, 62.3 us)
Async XLA Ops:
  0.6 211.5 %copy-start = (bf16[432,512]{1,0:T(8,128)(2,1)S(1)}, bf16[432,512]{1,0:T(8,128)(2,1)}, u32[]{:S(2)}) copy-start(bf16[432,512]{1,0:T(8,128)(2,1)} %param.19) | copy-start | bytes 1327108
  7.9 2.7 %copy-start.5 = (bf16[256,8,1,128]{0,3,2,1:T(8,128)(2,1)S(1)}, bf16[256,8,1,128]{0,3,2,1:T(8,128)(2,1)}, u32[]{:S(2)}) copy-start(bf16[256,8,1,128]{0,3,2,1:T(8,128)(2,1)} %get-tuple-element.143) | copy-start | bytes 1572868
  11.9 9.3 %copy-start.11 = (s32[32]{0:T(128)S(1)}, s32[32]{0:T(128)}, u32[]{:S(2)}) copy-start(s32[32]{0:T(128)} %param.22) | copy-start | bytes 388
  11.9 51.4 %all-to-all-start = ((bf16[256,8,3,128]{0,3,2,1:T(8,128)(2,1)}), bf16[256,8,3,128]{0,3,2,1:T(8,128)(2,1)S(1)}, u32[]{:S(2)}, u32[]{:S(2)}) async-start(bf16[256,8,3,128]{0,3,2,1:T(8,128)(2,1)} %pad_maximum_fusion), calls=%async_computation | async-start | bytes 3145728 | tf_op jit(solution)/shard_map/all_to_all | solution.py:109
  21.2 2.8 %copy-start.4 = (bf16[256,8,1,128]{0,3,2,1:T(8,128)(2,1)S(1)}, bf16[256,8,1,128]{0,3,2,1:T(8,128)(2,1)}, u32[]{:S(2)}) copy-start(bf16[256,8,1,128]{0,3,2,1:T(8,128)(2,1)} %get-tuple-element.141) | copy-start | bytes 1572868
  63.4 59.9 %all-to-all-start.1 = ((bf16[256,8,3,128]{0,3,2,1:T(8,128)(2,1)}), bf16[256,8,3,128]{0,3,2,1:T(8,128)(2,1)}, u32[]{:S(2)}, u32[]{:S(2)}) async-start(bf16[256,8,3,128]{0,3,2,1:T(8,128)(2,1)} %pad_maximum_fusion.1), calls=%async_computation.1 | async-start | bytes 3145728 | tf_op jit(solution)/shard_map/all_to_all | solution.py:109
  96.4 26.9 %copy-start.1 = (bf16[4,512,128]{2,1,0:T(8,128)(2,1)}, bf16[4,512,128]{2,1,0:T(8,128)(2,1)S(1)}, u32[]{:S(2)}) copy-start(bf16[4,512,128]{2,1,0:T(8,128)(2,1)S(1)} %get-tuple-element.83) | copy-start | bytes 1572868
  123.2 22.6 %all-to-all-start.2 = ((bf16[256,8,3,128]{0,3,2,1:T(8,128)(2,1)}), bf16[256,8,3,128]{0,3,2,1:T(8,128)(2,1)S(1)}, u32[]{:S(2)}, u32[]{:S(2)}) async-start(bf16[256,8,3,128]{0,3,2,1:T(8,128)(2,1)} %pad_maximum_fusion.2), calls=%async_computation.2 | async-start | bytes 3145728 | tf_op jit(solution)/shard_map/all_to_all | solution.py:109
  136.6 1.0 copy-start.6
  140.0 1.0 copy-start.6
  149.7 11.0 %copy-start.2 = (bf16[4,512,128]{2,1,0:T(8,128)(2,1)S(1)}, bf16[4,512,128]{2,1,0:T(8,128)(2,1)}, u32[]{:S(2)}) copy-start(bf16[4,512,128]{2,1,0:T(8,128)(2,1)} %copy-done.1) | copy-start | bytes 1572868
  149.8 12.0 %copy-start.3 = (bf16[4,512,128]{2,1,0:T(8,128)(2,1)S(1)}, bf16[4,512,128]{2,1,0:T(8,128)(2,1)}, u32[]{:S(2)}) copy-start(bf16[4,512,128]{2,1,0:T(8,128)(2,1)} %get-tuple-element.84) | copy-start | bytes 1572868
  164.8 38.4 %copy-start.8 = (f32[1,2,8,64]{3,2,1,0:T(8,128)S(1)}, f32[1,2,8,64]{3,2,1,0:T(8,128)}, u32[]{:S(2)}) copy-start(f32[1,2,8,64]{3,2,1,0:T(8,128)} %param.21) | copy-start | bytes 12292
  165.0 16.7 %collective-permute-start.6 = (f32[256,64]{0,1:T(8,128)S(1)}, f32[256,64]{0,1:T(8,128)S(1)}, u32[]{:S(2)}, u32[]{:S(2)}) collective-permute-start(f32[256,64]{0,1:T(8,128)S(1)} %bitcast.203), channel_id=1, source_target_pairs={{0,7},{1,0},{2,1},{3,2},{4,3},{5,4},{6,5},{7,6},{8,15},{9,8},{10,9... | collective-permute-start | bytes 196616 | tf_op jit(solution)/shard_map/ppermute | solution.py:47
  173.3 10.5 %collective-permute-start.5 = (f32[256,64]{0,1:T(8,128)S(1)}, f32[256,64]{0,1:T(8,128)S(1)}, u32[]{:S(2)}, u32[]{:S(2)}) collective-permute-start(f32[256,64]{0,1:T(8,128)S(1)} %bitcast.202), channel_id=1, source_target_pairs={{0,6},{1,7},{2,0},{3,1},{4,2},{5,3},{6,4},{7,5},{8,14},{9,15},{10,... | collective-permute-start | bytes 196616 | tf_op jit(solution)/shard_map/ppermute | solution.py:47
  174.3 11.1 %collective-permute-start.4 = (f32[256,64]{0,1:T(8,128)S(1)}, f32[256,64]{0,1:T(8,128)S(1)}, u32[]{:S(2)}, u32[]{:S(2)}) collective-permute-start(f32[256,64]{0,1:T(8,128)S(1)} %bitcast.197), channel_id=1, source_target_pairs={{0,5},{1,6},{2,7},{3,0},{4,1},{5,2},{6,3},{7,4},{8,13},{9,14},{10,... | collective-permute-start | bytes 196616 | tf_op jit(solution)/shard_map/ppermute | solution.py:47
  175.0 10.4 %collective-permute-start.3 = (f32[256,64]{0,1:T(8,128)S(1)}, f32[256,64]{0,1:T(8,128)S(1)}, u32[]{:S(2)}, u32[]{:S(2)}) collective-permute-start(f32[256,64]{0,1:T(8,128)S(1)} %bitcast.198), channel_id=1, source_target_pairs={{0,4},{1,5},{2,6},{3,7},{4,0},{5,1},{6,2},{7,3},{8,12},{9,13},{10,... | collective-permute-start | bytes 196616 | tf_op jit(solution)/shard_map/ppermute | solution.py:47
  177.9 10.8 %collective-permute-start.2 = (f32[256,64]{0,1:T(8,128)S(1)}, f32[256,64]{0,1:T(8,128)S(1)}, u32[]{:S(2)}, u32[]{:S(2)}) collective-permute-start(f32[256,64]{0,1:T(8,128)S(1)} %bitcast.199), channel_id=1, source_target_pairs={{0,3},{1,4},{2,5},{3,6},{4,7},{5,0},{6,1},{7,2},{8,11},{9,12},{10,... | collective-permute-start | bytes 196616 | tf_op jit(solution)/shard_map/ppermute | solution.py:47
  181.7 7.5 %collective-permute-start.1 = (f32[256,64]{0,1:T(8,128)S(1)}, f32[256,64]{0,1:T(8,128)S(1)}, u32[]{:S(2)}, u32[]{:S(2)}) collective-permute-start(f32[256,64]{0,1:T(8,128)S(1)} %bitcast.201), channel_id=1, source_target_pairs={{0,2},{1,3},{2,4},{3,5},{4,6},{5,7},{6,0},{7,1},{8,10},{9,11},{10,... | collective-permute-start | bytes 196616 | tf_op jit(solution)/shard_map/ppermute | solution.py:47
  183.8 10.3 %collective-permute-start = (f32[256,64]{0,1:T(8,128)S(1)}, f32[256,64]{0,1:T(8,128)S(1)}, u32[]{:S(2)}, u32[]{:S(2)}) collective-permute-start(f32[256,64]{0,1:T(8,128)S(1)} %bitcast.200), channel_id=1, source_target_pairs={{0,1},{1,2},{2,3},{3,4},{4,5},{5,6},{6,7},{7,0},{8,9},{9,10},{10,1... | collective-permute-start | bytes 196616 | tf_op jit(solution)/shard_map/ppermute | solution.py:47
  194.8 12.2 %collective-permute-start.8 = (bf16[2,1,1024]{2,1,0:T(2,128)(2,1)S(1)}, bf16[2,1,1024]{2,1,0:T(2,128)(2,1)S(1)}, u32[]{:S(2)}, u32[]{:S(2)}) collective-permute-start(bf16[2,1,1024]{2,1,0:T(2,128)(2,1)S(1)} %broadcast_select_fusion), channel_id=1, source_target_pairs={{0,1},{1,0},{2,3},{3,2},{4,5},{5,4},{6,7},{7,6},{8,9},{9,8},{10,11... | collective-permute-start | bytes 12296 | tf_op jit(solution)/shard_map/ppermute | solution.py:30
  194.9 12.3 %collective-permute-start.7 = (bf16[2,1,1024]{2,1,0:T(2,128)(2,1)S(1)}, bf16[2,1,1024]{2,1,0:T(2,128)(2,1)S(1)}, u32[]{:S(2)}, u32[]{:S(2)}) collective-permute-start(bf16[2,1,1024]{2,1,0:T(2,128)(2,1)S(1)} %broadcast_select_fusion), channel_id=1, source_target_pairs={{0,3},{1,2},{2,5},{3,4},{4,7},{5,6},{8,11},{9,10},{10,13},{11,12},... | collective-permute-start | bytes 12296 | tf_op jit(solution)/shard_map/ppermute | solution.py:126
  203.2 5.2 %collective-permute-start.9 = (bf16[2,8,1024]{2,1,0:T(8,128)(2,1)S(1)}, bf16[2,8,1024]{2,1,0:T(8,128)(2,1)S(1)}, u32[]{:S(2)}, u32[]{:S(2)}) collective-permute-start(bf16[2,8,1024]{2,1,0:T(8,128)(2,1)S(1)} %reshape.145), channel_id=1, source_target_pairs={{0,2},{1,3},{2,4},{3,5},{4,6},{5,7},{8,10},{9,11},{10,12},{11,13},... | collective-permute-start | bytes 98312 | tf_op jit(solution)/shard_map/ppermute | solution.py:26
  209.0 3.1 %copy-start.9 = (f32[512]{0:T(512)S(1)}, f32[512]{0:T(512)}, u32[]{:S(2)}) copy-start(f32[512]{0:T(512)} %param.20) | copy-start | bytes 6148
  209.0 3.1 %copy-start.12 = (pred[8,9]{0,1:T(8,128)(4,1)S(1)}, pred[8,9]{0,1:T(8,128)(4,1)}, u32[]{:S(2)}) copy-start(pred[8,9]{0,1:T(8,128)(4,1)} %constant.182) | copy-start | bytes 220
  216.2 13.3 %collective-permute-start.16 = (f32[2,512]{1,0:T(2,128)S(1)}, f32[2,512]{1,0:T(2,128)S(1)}, u32[]{:S(2)}, u32[]{:S(2)}) collective-permute-start(f32[2,512]{1,0:T(2,128)S(1)} %get-tuple-element.159), channel_id=1, source_target_pairs={{0,7},{1,0},{2,1},{3,2},{4,3},{5,4},{6,5},{7,6},{8,15},{9,8},{10,9... | collective-permute-start | bytes 12296 | tf_op jit(solution)/shard_map/ppermute | solution.py:47
  220.2 11.0 %collective-permute-start.15 = (f32[2,512]{1,0:T(2,128)S(1)}, f32[2,512]{1,0:T(2,128)S(1)}, u32[]{:S(2)}, u32[]{:S(2)}) collective-permute-start(f32[2,512]{1,0:T(2,128)S(1)} %get-tuple-element.160), channel_id=1, source_target_pairs={{0,6},{1,7},{2,0},{3,1},{4,2},{5,3},{6,4},{7,5},{8,14},{9,15},{10,... | collective-permute-start | bytes 12296 | tf_op jit(solution)/shard_map/ppermute | solution.py:47
  222.6 14.5 %collective-permute-start.14 = (f32[2,512]{1,0:T(2,128)S(1)}, f32[2,512]{1,0:T(2,128)S(1)}, u32[]{:S(2)}, u32[]{:S(2)}) collective-permute-start(f32[2,512]{1,0:T(2,128)S(1)} %get-tuple-element.161), channel_id=1, source_target_pairs={{0,5},{1,6},{2,7},{3,0},{4,1},{5,2},{6,3},{7,4},{8,13},{9,14},{10,... | collective-permute-start | bytes 12296 | tf_op jit(solution)/shard_map/ppermute | solution.py:47
  226.7 10.4 %collective-permute-start.13 = (f32[2,512]{1,0:T(2,128)S(1)}, f32[2,512]{1,0:T(2,128)S(1)}, u32[]{:S(2)}, u32[]{:S(2)}) collective-permute-start(f32[2,512]{1,0:T(2,128)S(1)} %get-tuple-element.162), channel_id=1, source_target_pairs={{0,4},{1,5},{2,6},{3,7},{4,0},{5,1},{6,2},{7,3},{8,12},{9,13},{10,... | collective-permute-start | bytes 12296 | tf_op jit(solution)/shard_map/ppermute | solution.py:47
  226.8 10.3 %collective-permute-start.12 = (f32[2,512]{1,0:T(2,128)S(1)}, f32[2,512]{1,0:T(2,128)S(1)}, u32[]{:S(2)}, u32[]{:S(2)}) collective-permute-start(f32[2,512]{1,0:T(2,128)S(1)} %get-tuple-element.163), channel_id=1, source_target_pairs={{0,3},{1,4},{2,5},{3,6},{4,7},{5,0},{6,1},{7,2},{8,11},{9,12},{10,... | collective-permute-start | bytes 12296 | tf_op jit(solution)/shard_map/ppermute | solution.py:47
  229.5 7.6 %collective-permute-start.11 = (f32[2,512]{1,0:T(2,128)S(1)}, f32[2,512]{1,0:T(2,128)S(1)}, u32[]{:S(2)}, u32[]{:S(2)}) collective-permute-start(f32[2,512]{1,0:T(2,128)S(1)} %get-tuple-element.164), channel_id=1, source_target_pairs={{0,2},{1,3},{2,4},{3,5},{4,6},{5,7},{6,0},{7,1},{8,10},{9,11},{10,... | collective-permute-start | bytes 12296 | tf_op jit(solution)/shard_map/ppermute | solution.py:47
  231.2 9.6 %collective-permute-start.10 = (f32[2,512]{1,0:T(2,128)S(1)}, f32[2,512]{1,0:T(2,128)S(1)}, u32[]{:S(2)}, u32[]{:S(2)}) collective-permute-start(f32[2,512]{1,0:T(2,128)S(1)} %get-tuple-element.158), channel_id=1, source_target_pairs={{0,1},{1,2},{2,3},{3,4},{4,5},{5,6},{6,7},{7,0},{8,9},{9,10},{10,1... | collective-permute-start | bytes 12296 | tf_op jit(solution)/shard_map/ppermute | solution.py:47
  (7 other events, 7.3 us)

commit v3 on v2

--- a/solution.py
+++ b/solution.py
@@ -1,6 +1,7 @@
 import math
 
 import jax
+import numpy as np
 import jax.numpy as jnp
 from jax import lax
 from jax.sharding import PartitionSpec as P
@@ -37,6 +38,24 @@
         array = array + swapped(array, axis, bit)
         bit += 1
     return array
+
+
+def halo_tables(tile_count):
+    quarter = S_DEV // 4
+    tile_token = np.arange(S_DEV)
+    positions, offsets = [], []
+    for tile in range(tile_count):
+        band = tile % TR
+        token_row = 0 if band == 0 else RT - 1
+        row_tokens = np.array(
+            [f * RT * WT + token_row * WT + c for f in range(FT) for c in range(WT)]
+        )
+        earlier = tile - TR if tile >= TR else 0
+        diagonal = (tile - TR) ^ 1 if tile >= TR else 0
+        parts = [(earlier, tile_token), (tile, tile_token), (diagonal, row_tokens), (tile ^ 1, row_tokens)]
+        positions.append(np.concatenate([4 * src + idx // quarter for src, idx in parts]))
+        offsets.append(np.concatenate([idx % quarter for src, idx in parts]))
+    return np.stack(positions).astype(np.int32), np.stack(offsets).astype(np.int32)
 
 
 def exchange_sum(blocks, axis, my_index):
@@ -112,22 +131,31 @@
         term = jnp.dot(head_out, proj_rows, preferred_element_type=jnp.float32)
         partial = term if partial is None else partial + term
 
-    ordered = partial.reshape(4 * group_count, quarter, 4 * LC)[tile_block]
-    ordered = ordered.reshape(group_count, S_DEV, 4 * LC)
-    latent = exchange_sum(ordered, "seq", my_index).astype(jnp.bfloat16)
-    tile_latent = (
-        latent.reshape(FT, RT, WT, 2, 2, LC).transpose(0, 1, 3, 2, 4, 5).reshape(FT, RL, COLS * LC)
-    )
+    positions, offsets = halo_tables(group_count)
+    token_ids = tile_block[positions] * quarter + offsets
+    outgoing = partial[token_ids.reshape(-1)].reshape(group_count, -1, 4 * LC)
+    returned = lax.all_to_all(outgoing, "seq", split_axis=0, concat_axis=0, tiled=True)
+    tokens = jnp.sum(returned, axis=0).astype(jnp.bfloat16)
     band_row = my_index % TR
     upper_band = band_row == 0
-    outgoing = jnp.where(upper_band, tile_latent[:, RL - 1 :], tile_latent[:, :1])
-    earlier = shifted(tile_latent, "seq", TR)
-    beside = swapped(outgoing, "seq", 0)
-    diagonal = lax.ppermute(
-        outgoing,
-        "seq",
-        [(i, (i ^ 1) + TR) for i in range(group_count) if (i ^ 1) + TR < group_count],
-    )
+    has_earlier = my_index >= TR
+
+    def to_tile(flat):
+        return (
+            flat.reshape(FT, RT, WT, 2, 2, LC).transpose(0, 1, 3, 2, 4, 5).reshape(FT, RL, COLS * LC)
+        )
+
+    def to_row(flat):
+        rows = flat.reshape(FT, WT, 2, 2 * LC)
+        return jnp.where(upper_band, rows[:, :, 0], rows[:, :, 1]).reshape(FT, 1, COLS * LC)
+
+    earlier = jnp.where(has_earlier, to_tile(tokens[:S_DEV]), jnp.zeros((), jnp.bfloat16))
+    tile_latent = to_tile(tokens[S_DEV : 2 * S_DEV])
+    halo_len = FT * WT
+    diagonal = jnp.where(
+        has_earlier, to_row(tokens[2 * S_DEV : 2 * S_DEV + halo_len]), jnp.zeros((), jnp.bfloat16)
+    )
+    beside = to_row(tokens[2 * S_DEV + halo_len :])
     extended = jnp.concatenate([earlier, tile_latent], axis=0)
     incoming = jnp.concatenate([diagonal, beside], axis=0)
     above = jnp.where(upper_band, jnp.zeros_like(incoming), incoming)
@@ -155,7 +183,12 @@
     by_owner = jnp.dot(
         chooser, pooled_term, precision=lax.Precision.HIGHEST, preferred_element_type=jnp.float32
     )
-    policy = exchange_sum(by_owner.reshape(group_count, BPD, CO), "seq", my_index)
+    policy = jnp.sum(
+        lax.all_to_all(
+            by_owner.reshape(group_count, BPD, CO), "seq", split_axis=0, concat_axis=0, tiled=True
+        ),
+        axis=0,
+    )
     return (decoded, policy)
 
 

time: 243 us -> 235 us (0.967)
  starting transfers between devices: 83.4 us -> 32.9 us
  local copies, waits for them, and re-layouts: 33.9 us -> 82.2 us
  waiting for transfers between devices: 78.4 us -> 72.1 us
    ppermute x17 -> x0, starting transfers between devices: 50.9 us -> none  [the longest x14 38.9 us: exchange_sum(): lax.ppermute(piece, axis, [(i, (i + step) % length) for i in range(length)])]
    gather x1 -> x2, local copies, waits for them, and re-layouts: 0.62 us -> 48.5 us  [the longest x1 30.7 us: local(): token_ids = tile_block[positions] * quarter + offsets]
    all_to_all x0 -> x2, waiting for transfers between devices: none -> 31.3 us  [the longest x1 22.5 us: local(): lax.all_to_all(outgoing, 'seq', split_axis=0, concat_axis=0, tiled=True)]
    all_to_all x3, waiting for transfers between devices: 64.9 us -> 40.8 us  [local(): lax.all_to_all(stacked, 'seq', split_axis=1, concat_axis=0, tiled=True)]
    ppermute x17 -> x0, waiting for transfers between devices: 13.4 us -> none  [the longest x14 12.5 us: exchange_sum(): lax.ppermute(piece, axis, [(i, (i + step) % length) for i in range(length)])]
    all_to_all x0 -> x2, starting transfers between devices: none -> 8.34 us  [the longest x1 5 us: local(): lax.all_to_all(outgoing, 'seq', split_axis=0, concat_axis=0, tiled=True)]
    all_to_all x3, starting transfers between devices: 32.6 us -> 24.5 us  [local(): lax.all_to_all(stacked, 'seq', split_axis=1, concat_axis=0, tiled=True)]
    reshape x3 -> x4, local copies, waits for them, and re-layouts: 0.77 us -> 3.24 us  [the longest x1 2.94 us: local(): outgoing = partial[token_ids.reshape(-1)].reshape(group_count, -1, 4 * LC)]
  transfers between devices with their start and end apart: 20 -> 5, of which waited for: 7 -> 5; matrix products, arithmetic and copies ran while one was open for 16% -> 29% of each run, Pallas kernels for 0% -> 0%
where the time goes in v3:
time: 235 us; the launch traced here: 233 us
  local copies, waits for them, and re-layouts  82.2 us (35%)
  waiting for transfers between devices  72.1 us (31%)
  starting transfers between devices  32.9 us (14%)
  matrix products  27.7 us (12%)
  other arithmetic  17.2 us (7%)
    all_to_all x3, waiting for transfers between devices, local(): lax.all_to_all(stacked, 'seq', split_axis=1, concat_axis=0, tiled=True)  40.8 us
    gather x1, local copies, waits for them, and re-layouts, local(): token_ids = tile_block[positions] * quarter + offsets  30.7 us
    all_to_all x3, starting transfers between devices, local(): lax.all_to_all(stacked, 'seq', split_axis=1, concat_axis=0, tiled=True)  24.5 us
    all_to_all x1, waiting for transfers between devices, local(): lax.all_to_all(outgoing, 'seq', split_axis=0, concat_axis=0, tiled=True)  22.5 us
    gather x1, local copies, waits for them, and re-layouts, local(): outgoing = partial[token_ids.reshape(-1)].reshape(group_count, -1, 4 * LC)  17.7 us
    dot_general x12, matrix products, one_block(): jnp.dot(expo.astype(jnp.bfloat16), value, preferred_element_type=jnp.floa...  13.3 us
    reduce_sum x12, other arithmetic, one_block(): totals = jnp.sum(expo, axis=-1, keepdims=True)  9.87 us
    dot_general x12, matrix products, one_block(): jnp.dot(query_part, key.T, preferred_element_type=jnp.float32) * score_scale  9.45 us
  transfers between devices with their start and end apart: 5, of which 5 were waited for; matrix products, arithmetic and copies ran while one was open for 29% of the time, Pallas kernels for 0%

profile of v3, /device:TPU:80, one launch (start us, length us, event | category | flops | bytes accessed | tf_op | source)
XLA Modules:
  0.0 233.3 jit_solution(10360151437006155917)
XLA Ops:
  0.6 1.8 copy.107
  3.4 1.7 copy.108
  6.3 1.7 copy.109
  10.9 9.3 %all-to-all-start = ((bf16[256,8,3,128]{0,3,2,1:T(8,128)(2,1)}), bf16[256,8,3,128]{0,3,2,1:T(8,128)(2,1)S(1)}, u32[]{:S(2)}, u32[]{:S(2)}) async-start(bf16[256,8,3,128]{0,3,2,1:T(8,128)(2,1)} %pad_maximum_fusion), calls=%async_computation | async-start | bytes 3145728 | tf_op jit(solution)/shard_map/all_to_all | solution.py:128
  20.2 30.7 %gather_fusion = s32[5120]{0:T(1024)S(1)} fusion(s32[32]{0:T(128)S(1)} %copy-done.1, s32[5120]{0:T(1024)S(1)} %broadcast_clamp_fusion.1), kind=kCustom, calls=%fused_computation | custom fusion | bytes 61440 | tf_op jit(solution)/shard_map/gather | solution.py:135
  50.9 2.6 %pad_maximum_fusion.1 = bf16[256,8,3,128]{0,3,2,1:T(8,128)(2,1)} fusion(bf16[256,8,1,128]{0,3,2,1:T(8,128)(2,1)} %get-tuple-element.142, bf16[256,8,1,128]{0,3,2,1:T(8,128)(2,1)} %get-tuple-element.139, bf16[256,8,1,128]{0,3,2,1:T(8,128)(2,1)S(1)} %get-tuple-element.136), kind=kLoop, calls=%fused_computation.59 | loop fusion | flops 1572864 | bytes 3145728 | tf_op jit(solution)/shard_map/stack | solution.py:125
  54.9 7.3 %all-to-all-done = bf16[256,8,3,128]{0,3,2,1:T(8,128)(2,1)S(1)} async-done(((bf16[256,8,3,128]{0,3,2,1:T(8,128)(2,1)}), bf16[256,8,3,128]{0,3,2,1:T(8,128)(2,1)S(1)}, u32[]{:S(2)}, u32[]{:S(2)}) %all-to-all-start) | async-done | bytes 1572896 | tf_op jit(solution)/shard_map/all_to_all | solution.py:128
  62.2 4.3 %all-to-all-start.1 = ((bf16[256,8,3,128]{0,3,2,1:T(8,128)(2,1)}), bf16[256,8,3,128]{0,3,2,1:T(8,128)(2,1)}, u32[]{:S(2)}, u32[]{:S(2)}) async-start(bf16[256,8,3,128]{0,3,2,1:T(8,128)(2,1)} %pad_maximum_fusion.1), calls=%async_computation.1 | async-start | bytes 3145728 | tf_op jit(solution)/shard_map/all_to_all | solution.py:128
  66.5 1.6 copy.110
  68.1 1.5 slice_bitcast_fusion.6
  69.6 10.1 %while.30 = (s32[]{:T(128)}, bf16[4,512,128]{2,1,0:T(8,128)(2,1)S(1)}, bf16[4,512,128]{2,1,0:T(8,128)(2,1)S(1)}, bf16[2048,128]{1,0:T(8,128)(2,1)S(1)}, bf16[2048,128]{1,0:T(8,128)(2,1)S(1)}, /*index=5*/s32[]{:T(128)}) while((s32[]{:T(128)}, bf16[4,512,128]{2,1,0:T(8,128)(2,1)S(1)}, bf16[4,512,128]{2,1,0:T(8,128)(2,1)S(1)}, ...), condition=%wide.region_3.4_spmd, body=%wide.region_0.3_spmd.sunk | while | flops 545389568 | bytes 13903949 | solution.py:84
  79.8 27.4 %all-to-all-done.1 = bf16[256,8,3,128]{0,3,2,1:T(8,128)(2,1)} async-done(((bf16[256,8,3,128]{0,3,2,1:T(8,128)(2,1)}), bf16[256,8,3,128]{0,3,2,1:T(8,128)(2,1)}, u32[]{:S(2)}, u32[]{:S(2)}) %all-to-all-start.1) | async-done | bytes 1572896 | tf_op jit(solution)/shard_map/all_to_all | solution.py:128
  107.2 11.0 %all-to-all-start.2 = ((bf16[256,8,3,128]{0,3,2,1:T(8,128)(2,1)}), bf16[256,8,3,128]{0,3,2,1:T(8,128)(2,1)S(1)}, u32[]{:S(2)}, u32[]{:S(2)}) async-start(bf16[256,8,3,128]{0,3,2,1:T(8,128)(2,1)} %pad_maximum_fusion.2), calls=%async_computation.2 | async-start | bytes 3145728 | tf_op jit(solution)/shard_map/all_to_all | solution.py:128
  118.2 2.6 %copy.111 = bf16[8,256,1,3,128]{4,1,0,3,2:T(8,128)(2,1)} copy(bf16[8,256,1,3,128]{1,4,3,0,2:T(8,128)(2,1)} %bitcast.17) | data formatting | bytes 3145728 | tf_op jit(solution)/shard_map/all_to_all | solution.py:128
  120.8 2.2 slice_bitcast_fusion.4
  123.9 13.4 %while.31 = (s32[]{:T(128)}, bf16[4,512,128]{2,1,0:T(8,128)(2,1)}, bf16[4,512,128]{2,1,0:T(8,128)(2,1)S(1)}, bf16[2048,128]{1,0:T(8,128)(2,1)S(1)}, bf16[2048,128]{1,0:T(8,128)(2,1)}, /*index=5*/s32[]{:T(128)}) while((s32[]{:T(128)}, bf16[4,512,128]{2,1,0:T(8,128)(2,1)}, bf16[4,512,128]{2,1,0:T(8,128)(2,1)S(1)}, ...), condition=%wide.region_7.8_spmd, body=%wide.region_4.7_spmd.sunk | while | flops 545389568 | bytes 16001637 | solution.py:84
  125.8 1.5 fusion.138
  129.1 1.5 fusion.138
  132.4 1.5 fusion.138
  135.8 1.5 fusion.138
  137.3 6.1 %all-to-all-done.2 = bf16[256,8,3,128]{0,3,2,1:T(8,128)(2,1)S(1)} async-done(((bf16[256,8,3,128]{0,3,2,1:T(8,128)(2,1)}), bf16[256,8,3,128]{0,3,2,1:T(8,128)(2,1)S(1)}, u32[]{:S(2)}, u32[]{:S(2)}) %all-to-all-start.2) | async-done | bytes 1572896 | tf_op jit(solution)/shard_map/all_to_all | solution.py:128
  143.4 1.6 copy.112
  145.0 1.5 slice_bitcast_fusion.2
  146.6 10.1 %while.32 = (s32[]{:T(128)}, bf16[4,512,128]{2,1,0:T(8,128)(2,1)S(1)}, bf16[4,512,128]{2,1,0:T(8,128)(2,1)S(1)}, bf16[2048,128]{1,0:T(8,128)(2,1)S(1)}, bf16[2048,128]{1,0:T(8,128)(2,1)S(1)}, /*index=5*/s32[]{:T(128)}) while((s32[]{:T(128)}, bf16[4,512,128]{2,1,0:T(8,128)(2,1)S(1)}, bf16[4,512,128]{2,1,0:T(8,128)(2,1)S(1)}, ...), condition=%wide.region_11.12_spmd, body=%wide.region_8.11_spmd.sunk | while | flops 545389568 | bytes 13903949 | solution.py:84
  160.4 17.7 %gather_fusion.1 = f32[5120,64]{1,0:T(8,128)} fusion(f32[2048,64]{1,0:T(8,128)S(1)} %copy.113, s32[5120]{0:T(1024)S(1)} %broadcast_clamp_fusion), kind=kCustom, calls=%fused_computation.1 | custom fusion | bytes 2641920 | tf_op jit(solution)/shard_map/gather | solution.py:136
  178.2 2.9 %copy.114 = f32[8,640,64]{1,2,0:T(8,128)} copy(f32[8,640,64]{2,1,0:T(8,128)} %bitcast.129) | data formatting | bytes 2621440 | tf_op jit(solution)/shard_map/reshape | solution.py:136
  181.1 5.0 %all-to-all-start.3 = ((f32[8,640,64]{1,2,0:T(8,128)}), f32[8,640,64]{1,2,0:T(8,128)S(1)}, u32[]{:S(2)}, u32[]{:S(2)}) async-start(f32[8,640,64]{1,2,0:T(8,128)} %copy.114), calls=%async_computation.3 | async-start | bytes 2621440 | tf_op jit(solution)/shard_map/all_to_all | solution.py:137
  186.2 22.5 %all-to-all-done.3 = f32[8,640,64]{1,2,0:T(8,128)S(1)} async-done(((f32[8,640,64]{1,2,0:T(8,128)}), f32[8,640,64]{1,2,0:T(8,128)S(1)}, u32[]{:S(2)}, u32[]{:S(2)}) %all-to-all-start.3) | async-done | bytes 1310752 | tf_op jit(solution)/shard_map/all_to_all | solution.py:137
  212.0 2.2 copy.125
  214.3 1.5 add_convert_fusion
  219.3 3.3 %all-to-all-start.4 = ((f32[8,2,512]{2,1,0:T(2,128)}), f32[8,2,512]{2,1,0:T(2,128)S(1)}, u32[]{:S(2)}, u32[]{:S(2)}) async-start(f32[8,2,512]{2,1,0:T(2,128)} %reshape.225), calls=%async_computation.4 | async-start | bytes 65536 | tf_op jit(solution)/shard_map/all_to_all | solution.py:187
  224.0 8.7 %all-to-all-done.4 = f32[8,2,512]{2,1,0:T(2,128)S(1)} async-done(((f32[8,2,512]{2,1,0:T(2,128)}), f32[8,2,512]{2,1,0:T(2,128)S(1)}, u32[]{:S(2)}, u32[]{:S(2)}) %all-to-all-start.4) | async-done | bytes 32800 | tf_op jit(solution)/shard_map/all_to_all | solution.py:187
  (119 shorter events, 47.3 us)
Async XLA Ops:
  0.6 213.6 %copy-start = (bf16[432,512]{1,0:T(8,128)(2,1)S(1)}, bf16[432,512]{1,0:T(8,128)(2,1)}, u32[]{:S(2)}) copy-start(bf16[432,512]{1,0:T(8,128)(2,1)} %param.22) | copy-start | bytes 1327108
  8.0 1.1 copy-start.6
  8.0 1.6 copy-start.7
  10.9 9.3 %copy-start.9 = (s32[5120]{0:T(1024)S(1)}, s32[5120]{0:T(1024)}, u32[]{:S(2)}) copy-start(s32[5120]{0:T(1024)} %constant.107) | copy-start | bytes 61444
  10.9 9.3 %copy-start.1 = (s32[32]{0:T(128)S(1)}, s32[32]{0:T(128)}, u32[]{:S(2)}) copy-start(s32[32]{0:T(128)} %param.25) | copy-start | bytes 388
  10.9 51.3 %all-to-all-start = ((bf16[256,8,3,128]{0,3,2,1:T(8,128)(2,1)}), bf16[256,8,3,128]{0,3,2,1:T(8,128)(2,1)S(1)}, u32[]{:S(2)}, u32[]{:S(2)}) async-start(bf16[256,8,3,128]{0,3,2,1:T(8,128)(2,1)} %pad_maximum_fusion), calls=%async_computation | async-start | bytes 3145728 | tf_op jit(solution)/shard_map/all_to_all | solution.py:128
  50.9 2.6 %copy-start.4 = (bf16[256,8,1,128]{0,3,2,1:T(8,128)(2,1)S(1)}, bf16[256,8,1,128]{0,3,2,1:T(8,128)(2,1)}, u32[]{:S(2)}) copy-start(bf16[256,8,1,128]{0,3,2,1:T(8,128)(2,1)} %get-tuple-element.138) | copy-start | bytes 1572868
  50.9 2.6 %copy-start.5 = (bf16[256,8,1,128]{0,3,2,1:T(8,128)(2,1)S(1)}, bf16[256,8,1,128]{0,3,2,1:T(8,128)(2,1)}, u32[]{:S(2)}) copy-start(bf16[256,8,1,128]{0,3,2,1:T(8,128)(2,1)} %get-tuple-element.141) | copy-start | bytes 1572868
  53.6 1.3 copy-start.10
  62.2 45.0 %all-to-all-start.1 = ((bf16[256,8,3,128]{0,3,2,1:T(8,128)(2,1)}), bf16[256,8,3,128]{0,3,2,1:T(8,128)(2,1)}, u32[]{:S(2)}, u32[]{:S(2)}) async-start(bf16[256,8,3,128]{0,3,2,1:T(8,128)(2,1)} %pad_maximum_fusion.1), calls=%async_computation.1 | async-start | bytes 3145728 | tf_op jit(solution)/shard_map/all_to_all | solution.py:128
  79.8 27.5 %copy-start.2 = (bf16[4,512,128]{2,1,0:T(8,128)(2,1)}, bf16[4,512,128]{2,1,0:T(8,128)(2,1)S(1)}, u32[]{:S(2)}) copy-start(bf16[4,512,128]{2,1,0:T(8,128)(2,1)S(1)} %get-tuple-element.83) | copy-start | bytes 1572868
  107.2 36.2 %all-to-all-start.2 = ((bf16[256,8,3,128]{0,3,2,1:T(8,128)(2,1)}), bf16[256,8,3,128]{0,3,2,1:T(8,128)(2,1)S(1)}, u32[]{:S(2)}, u32[]{:S(2)}) async-start(bf16[256,8,3,128]{0,3,2,1:T(8,128)(2,1)} %pad_maximum_fusion.2), calls=%async_computation.2 | async-start | bytes 3145728 | tf_op jit(solution)/shard_map/all_to_all | solution.py:128
  124.7 1.0 copy-start.8
  128.1 1.0 copy-start.8
  131.4 1.0 copy-start.8
  134.7 1.0 copy-start.8
  146.5 10.2 %copy-start.3 = (bf16[4,512,128]{2,1,0:T(8,128)(2,1)S(1)}, bf16[4,512,128]{2,1,0:T(8,128)(2,1)}, u32[]{:S(2)}) copy-start(bf16[4,512,128]{2,1,0:T(8,128)(2,1)} %copy-done.2) | copy-start | bytes 1572868
  181.1 5.0 %copy-start.11 = (f32[1,2,8,64]{3,2,1,0:T(8,128)S(1)}, f32[1,2,8,64]{3,2,1,0:T(8,128)}, u32[]{:S(2)}) copy-start(f32[1,2,8,64]{3,2,1,0:T(8,128)} %param.24) | copy-start | bytes 12292
  181.1 27.6 %all-to-all-start.3 = ((f32[8,640,64]{1,2,0:T(8,128)}), f32[8,640,64]{1,2,0:T(8,128)S(1)}, u32[]{:S(2)}, u32[]{:S(2)}) async-start(f32[8,640,64]{1,2,0:T(8,128)} %copy.114), calls=%async_computation.3 | async-start | bytes 2621440 | tf_op jit(solution)/shard_map/all_to_all | solution.py:137
  211.1 3.1 %copy-start.12 = (f32[512]{0:T(512)S(1)}, f32[512]{0:T(512)}, u32[]{:S(2)}) copy-start(f32[512]{0:T(512)} %param.23) | copy-start | bytes 6148
  211.1 3.1 %copy-start.14 = (pred[8,9]{0,1:T(8,128)(4,1)S(1)}, pred[8,9]{0,1:T(8,128)(4,1)}, u32[]{:S(2)}) copy-start(pred[8,9]{0,1:T(8,128)(4,1)} %constant.105) | copy-start | bytes 220
  217.5 1.0 copy-start.13
  219.3 13.4 %all-to-all-start.4 = ((f32[8,2,512]{2,1,0:T(2,128)}), f32[8,2,512]{2,1,0:T(2,128)S(1)}, u32[]{:S(2)}, u32[]{:S(2)}) async-start(f32[8,2,512]{2,1,0:T(2,128)} %reshape.225), calls=%async_computation.4 | async-start | bytes 65536 | tf_op jit(solution)/shard_map/all_to_all | solution.py:187

commit v4 on v3

--- a/solution.py
+++ b/solution.py
@@ -40,22 +40,23 @@
     return array
 
 
-def halo_tables(tile_count):
-    quarter = S_DEV // 4
-    tile_token = np.arange(S_DEV)
-    positions, offsets = [], []
-    for tile in range(tile_count):
-        band = tile % TR
-        token_row = 0 if band == 0 else RT - 1
-        row_tokens = np.array(
-            [f * RT * WT + token_row * WT + c for f in range(FT) for c in range(WT)]
-        )
-        earlier = tile - TR if tile >= TR else 0
-        diagonal = (tile - TR) ^ 1 if tile >= TR else 0
-        parts = [(earlier, tile_token), (tile, tile_token), (diagonal, row_tokens), (tile ^ 1, row_tokens)]
-        positions.append(np.concatenate([4 * src + idx // quarter for src, idx in parts]))
-        offsets.append(np.concatenate([idx % quarter for src, idx in parts]))
-    return np.stack(positions).astype(np.int32), np.stack(offsets).astype(np.int32)
+def halo_tokens(tiled, tile):
+    token_row = 0 if tile % TR == 0 else RT - 1
+
+    def row_of(source):
+        return jnp.concatenate(
+            [
+                tiled[source, f * RT * WT + token_row * WT : f * RT * WT + (token_row + 1) * WT]
+                for f in range(FT)
+            ],
+            axis=0,
+        )
+
+    earlier = tile - TR if tile >= TR else 0
+    diagonal = (tile - TR) ^ 1 if tile >= TR else 0
+    return jnp.concatenate(
+        [tiled[earlier], tiled[tile], row_of(diagonal), row_of(tile ^ 1)], axis=0
+    )
 
 
 def exchange_sum(blocks, axis, my_index):
@@ -123,17 +124,17 @@
     partial = None
     for slot in range(heads_dev):
         stacked = jnp.stack(
-            [q_groups[:, :, slot], k_groups[:, :, slot], v_groups[:, :, slot]], axis=2
-        )
-        gathered = lax.all_to_all(stacked, "seq", split_axis=1, concat_axis=0, tiled=True)
-        head_out = head_attention(gathered[:, 0, 0], gathered[:, 0, 1], gathered[:, 0, 2])
+            [q_groups[:, :, slot], k_groups[:, :, slot], v_groups[:, :, slot]], axis=0
+        )
+        gathered = lax.all_to_all(stacked, "seq", split_axis=2, concat_axis=1, tiled=True)
+        head_out = head_attention(gathered[0, :, 0], gathered[1, :, 0], gathered[2, :, 0])
         proj_rows = lax.dynamic_slice_in_dim(latent_proj, (my_index * heads_dev + slot) * HD, HD, 0)
         term = jnp.dot(head_out, proj_rows, preferred_element_type=jnp.float32)
         partial = term if partial is None else partial + term
 
-    positions, offsets = halo_tables(group_count)
-    token_ids = tile_block[positions] * quarter + offsets
-    outgoing = partial[token_ids.reshape(-1)].reshape(group_count, -1, 4 * LC)
+    tiled = partial.reshape(4 * group_count, quarter, 4 * LC)[tile_block]
+    tiled = tiled.reshape(group_count, S_DEV, 4 * LC)
+    outgoing = jnp.stack([halo_tokens(tiled, tile) for tile in range(group_count)])
     returned = lax.all_to_all(outgoing, "seq", split_axis=0, concat_axis=0, tiled=True)
     tokens = jnp.sum(returned, axis=0).astype(jnp.bfloat16)
     band_row = my_index % TR

time: 235 us -> 223 us (0.949)
  local copies, waits for them, and re-layouts: 82.2 us -> 43.6 us
  waiting for transfers between devices: 72.1 us -> 90.3 us
  starting transfers between devices: 32.9 us -> 45.3 us
  other arithmetic: 17.2 us -> 13.8 us
    gather x2 -> x1, local copies, waits for them, and re-layouts: 48.5 us -> 0.62 us  [local(): tiled = partial.reshape(4 * group_count, quarter, 4 * LC)[tile_block]]
    all_to_all x3, waiting for transfers between devices: 40.8 us -> 64.8 us  [local(): lax.all_to_all(stacked, 'seq', split_axis=2, concat_axis=1, tiled=True)]
    all_to_all x3, starting transfers between devices: 24.5 us -> 32.6 us  [local(): lax.all_to_all(stacked, 'seq', split_axis=2, concat_axis=1, tiled=True)]
    another operation x3 -> x10, local copies, waits for them, and re-layouts: 1.01 us -> 8.73 us  [the longest x6 7.06 us: local(): jnp.stack([q_groups[:, :, slot], k_groups[:, :, slot], v_groups[:, :, slo...]
    unnamed x33 -> x52, local copies, waits for them, and re-layouts: 7.15 us -> 13.3 us
    all_to_all x1, waiting for transfers between devices: 22.5 us -> 16.8 us  [local(): lax.all_to_all(outgoing, 'seq', split_axis=0, concat_axis=0, tiled=True)]
    squeeze x3 -> x8, local copies, waits for them, and re-layouts: 5.17 us -> 0.68 us  [the longest x7 0.6 us: halo_tokens(): tiled[tile]]
    all_to_all x1, starting transfers between devices: 5 us -> 9.34 us  [local(): lax.all_to_all(outgoing, 'seq', split_axis=0, concat_axis=0, tiled=True)]
  transfers between devices with their start and end apart: 5 -> 5, of which waited for: 5 -> 4; matrix products, arithmetic and copies ran while one was open for 29% -> 17% of each run, Pallas kernels for 0% -> 0%
where the time goes in v4:
time: 223 us; the launch traced here: 222 us
  waiting for transfers between devices  90.3 us (40%)
  starting transfers between devices  45.3 us (20%)
  local copies, waits for them, and re-layouts  43.6 us (20%)
  matrix products  27.7 us (12%)
  other arithmetic  13.8 us (6%)
    all_to_all x3, waiting for transfers between devices, local(): lax.all_to_all(stacked, 'seq', split_axis=2, concat_axis=1, tiled=True)  64.8 us
    all_to_all x3, starting transfers between devices, local(): lax.all_to_all(stacked, 'seq', split_axis=2, concat_axis=1, tiled=True)  32.6 us
    all_to_all x1, waiting for transfers between devices, local(): lax.all_to_all(outgoing, 'seq', split_axis=0, concat_axis=0, tiled=True)  16.8 us
    unnamed x52, local copies, waits for them, and re-layouts  13.3 us
    dot_general x12, matrix products, one_block(): jnp.dot(expo.astype(jnp.bfloat16), value, preferred_element_type=jnp.floa...  13.2 us
    reduce_sum x12, other arithmetic, one_block(): totals = jnp.sum(expo, axis=-1, keepdims=True)  9.87 us
    dot_general x12, matrix products, one_block(): jnp.dot(query_part, key.T, preferred_element_type=jnp.float32) * score_scale  9.45 us
    all_to_all x1, starting transfers between devices, local(): lax.all_to_all(outgoing, 'seq', split_axis=0, concat_axis=0, tiled=True)  9.34 us
  transfers between devices with their start and end apart: 5, of which 4 were waited for; matrix products, arithmetic and copies ran while one was open for 17% of the time, Pallas kernels for 0%

profile of v4, /device:TPU:80, one launch (start us, length us, event | category | flops | bytes accessed | tf_op | source)
XLA Modules:
  0.0 222.0 jit_solution(15119934374990293907)
XLA Ops:
  0.6 1.8 copy.223
  3.5 1.7 copy.224
  6.3 1.7 copy.226
  11.0 9.1 %all-to-all-start = ((bf16[3,256,8,128]{1,3,0,2:T(8,128)(2,1)}), bf16[3,256,8,128]{1,3,0,2:T(8,128)(2,1)S(1)}, u32[]{:S(2)}, u32[]{:S(2)}) async-start(bf16[3,256,8,128]{1,3,0,2:T(8,128)(2,1)} %copy.228), calls=%async_computation | async-start | bytes 3145728 | tf_op jit(solution)/shard_map/all_to_all | solution.py:129
  20.2 1.5 pad_maximum_fusion.1
  21.7 1.3 copy.232
  24.4 37.9 %all-to-all-done = bf16[3,256,8,128]{1,3,0,2:T(8,128)(2,1)S(1)} async-done(((bf16[3,256,8,128]{1,3,0,2:T(8,128)(2,1)}), bf16[3,256,8,128]{1,3,0,2:T(8,128)(2,1)S(1)}, u32[]{:S(2)}, u32[]{:S(2)}) %all-to-all-start) | async-done | bytes 1572896 | tf_op jit(solution)/shard_map/all_to_all | solution.py:129
  62.3 19.7 %all-to-all-start.1 = ((bf16[3,256,8,128]{1,3,0,2:T(8,128)(2,1)}), bf16[3,256,8,128]{1,3,0,2:T(8,128)(2,1)}, u32[]{:S(2)}, u32[]{:S(2)}) async-start(bf16[3,256,8,128]{1,3,0,2:T(8,128)(2,1)} %copy.232), calls=%async_computation.1 | async-start | bytes 3145728 | tf_op jit(solution)/shard_map/all_to_all | solution.py:129
  82.1 1.6 copy.229
  83.6 1.5 fusion.102
  85.2 10.1 %while.30 = (s32[]{:T(128)}, bf16[4,512,128]{2,1,0:T(8,128)(2,1)S(1)}, bf16[4,512,128]{2,1,0:T(8,128)(2,1)S(1)}, bf16[2048,128]{1,0:T(8,128)(2,1)S(1)}, bf16[2048,128]{1,0:T(8,128)(2,1)S(1)}, /*index=5*/s32[]{:T(128)}) while((s32[]{:T(128)}, bf16[4,512,128]{2,1,0:T(8,128)(2,1)S(1)}, bf16[4,512,128]{2,1,0:T(8,128)(2,1)S(1)}, ...), condition=%wide.region_3.4_spmd, body=%wide.region_0.3_spmd.sunk | while | flops 545389568 | bytes 13903949 | solution.py:85
  95.3 26.9 %all-to-all-done.1 = bf16[3,256,8,128]{1,3,0,2:T(8,128)(2,1)} async-done(((bf16[3,256,8,128]{1,3,0,2:T(8,128)(2,1)}), bf16[3,256,8,128]{1,3,0,2:T(8,128)(2,1)}, u32[]{:S(2)}, u32[]{:S(2)}) %all-to-all-start.1) | async-done | bytes 1572896 | tf_op jit(solution)/shard_map/all_to_all | solution.py:129
  122.2 3.8 %all-to-all-start.2 = ((bf16[3,256,8,128]{1,3,0,2:T(8,128)(2,1)}), bf16[3,256,8,128]{1,3,0,2:T(8,128)(2,1)S(1)}, u32[]{:S(2)}, u32[]{:S(2)}) async-start(bf16[3,256,8,128]{1,3,0,2:T(8,128)(2,1)} %copy.236), calls=%async_computation.2 | async-start | bytes 3145728 | tf_op jit(solution)/shard_map/all_to_all | solution.py:129
  126.0 2.6 %copy.233 = bf16[3,256,8,128]{3,1,2,0:T(8,128)(2,1)} copy(bf16[3,256,8,128]{1,3,0,2:T(8,128)(2,1)} %all-to-all-done.1) | data formatting | bytes 3145728 | tf_op jit(solution)/shard_map/all_to_all | solution.py:129
  128.6 2.3 %fusion.101 = (bf16[1,8,256,1,128]{4,2,1,3,0:T(8,128)(2,1)}, bf16[1,8,256,1,128]{4,2,1,3,0:T(8,128)(2,1)S(1)}, bf16[1,8,256,1,128]{4,2,1,3,0:T(8,128)(2,1)S(1)}) fusion(bf16[3,8,256,1,128]{4,2,1,3,0:T(8,128)(2,1)} %bitcast.196), kind=kLoop, calls=%fused_computation.122 | loop fusion | bytes 3145728 | tf_op jit(solution)/shard_map/slice | solution.py:130
  131.7 13.3 %while.31 = (s32[]{:T(128)}, bf16[4,512,128]{2,1,0:T(8,128)(2,1)}, bf16[4,512,128]{2,1,0:T(8,128)(2,1)S(1)}, bf16[2048,128]{1,0:T(8,128)(2,1)S(1)}, bf16[2048,128]{1,0:T(8,128)(2,1)}, /*index=5*/s32[]{:T(128)}) while((s32[]{:T(128)}, bf16[4,512,128]{2,1,0:T(8,128)(2,1)}, bf16[4,512,128]{2,1,0:T(8,128)(2,1)S(1)}, ...), condition=%wide.region_7.8_spmd, body=%wide.region_4.7_spmd.sunk | while | flops 545389568 | bytes 16001637 | solution.py:85
  133.5 1.5 fusion.140
  136.9 1.5 fusion.140
  140.2 1.5 fusion.140
  143.5 1.5 fusion.140
  145.0 1.6 copy.237
  146.6 1.5 fusion.100
  148.1 10.1 %while.32 = (s32[]{:T(128)}, bf16[4,512,128]{2,1,0:T(8,128)(2,1)S(1)}, bf16[4,512,128]{2,1,0:T(8,128)(2,1)S(1)}, bf16[2048,128]{1,0:T(8,128)(2,1)S(1)}, bf16[2048,128]{1,0:T(8,128)(2,1)S(1)}, /*index=5*/s32[]{:T(128)}) while((s32[]{:T(128)}, bf16[4,512,128]{2,1,0:T(8,128)(2,1)S(1)}, bf16[4,512,128]{2,1,0:T(8,128)(2,1)S(1)}, ...), condition=%wide.region_11.12_spmd, body=%wide.region_8.11_spmd.sunk | while | flops 545389568 | bytes 13903949 | solution.py:85
  159.3 1.3 convolution_add_fusion.1
  171.2 9.3 %all-to-all-start.3 = ((f32[8,640,64]{1,2,0:T(8,128)}), f32[8,640,64]{1,2,0:T(8,128)S(1)}, u32[]{:S(2)}, u32[]{:S(2)}) async-start(f32[8,640,64]{1,2,0:T(8,128)} %bitcast_dynamic-update-slice_fusion), calls=%async_computation.3 | async-start | bytes 2621440 | tf_op jit(solution)/shard_map/all_to_all | solution.py:138
  180.6 16.8 %all-to-all-done.3 = f32[8,640,64]{1,2,0:T(8,128)S(1)} async-done(((f32[8,640,64]{1,2,0:T(8,128)}), f32[8,640,64]{1,2,0:T(8,128)S(1)}, u32[]{:S(2)}, u32[]{:S(2)}) %all-to-all-start.3) | async-done | bytes 1310752 | tf_op jit(solution)/shard_map/all_to_all | solution.py:138
  200.7 2.2 copy.283
  202.9 1.5 add_convert_fusion
  204.8 1.4 copy.285
  207.9 3.3 %all-to-all-start.4 = ((f32[8,2,512]{2,1,0:T(2,128)}), f32[8,2,512]{2,1,0:T(2,128)S(1)}, u32[]{:S(2)}, u32[]{:S(2)}) async-start(f32[8,2,512]{2,1,0:T(2,128)} %reshape.231), calls=%async_computation.4 | async-start | bytes 65536 | tf_op jit(solution)/shard_map/all_to_all | solution.py:188
  211.3 1.3 copy.288
  212.6 8.7 %all-to-all-done.4 = f32[8,2,512]{2,1,0:T(2,128)S(1)} async-done(((f32[8,2,512]{2,1,0:T(2,128)}), f32[8,2,512]{2,1,0:T(2,128)S(1)}, u32[]{:S(2)}, u32[]{:S(2)}) %all-to-all-start.4) | async-done | bytes 32800 | tf_op jit(solution)/shard_map/all_to_all | solution.py:188
  (156 shorter events, 52.6 us)
Async XLA Ops:
  0.6 202.2 %copy-start = (bf16[432,512]{1,0:T(8,128)(2,1)S(1)}, bf16[432,512]{1,0:T(8,128)(2,1)}, u32[]{:S(2)}) copy-start(bf16[432,512]{1,0:T(8,128)(2,1)} %param.19) | copy-start | bytes 1327108
  8.0 1.1 copy-start.4
  8.0 1.6 copy-start.5
  11.0 51.3 %all-to-all-start = ((bf16[3,256,8,128]{1,3,0,2:T(8,128)(2,1)}), bf16[3,256,8,128]{1,3,0,2:T(8,128)(2,1)S(1)}, u32[]{:S(2)}, u32[]{:S(2)}) async-start(bf16[3,256,8,128]{1,3,0,2:T(8,128)(2,1)} %copy.228), calls=%async_computation | async-start | bytes 3145728 | tf_op jit(solution)/shard_map/all_to_all | solution.py:129
  21.7 1.3 copy-start.3
  23.1 1.3 copy-start.10
  62.3 59.9 %all-to-all-start.1 = ((bf16[3,256,8,128]{1,3,0,2:T(8,128)(2,1)}), bf16[3,256,8,128]{1,3,0,2:T(8,128)(2,1)}, u32[]{:S(2)}, u32[]{:S(2)}) async-start(bf16[3,256,8,128]{1,3,0,2:T(8,128)(2,1)} %copy.232), calls=%async_computation.1 | async-start | bytes 3145728 | tf_op jit(solution)/shard_map/all_to_all | solution.py:129
  95.3 26.9 %copy-start.1 = (bf16[4,512,128]{2,1,0:T(8,128)(2,1)}, bf16[4,512,128]{2,1,0:T(8,128)(2,1)S(1)}, u32[]{:S(2)}) copy-start(bf16[4,512,128]{2,1,0:T(8,128)(2,1)S(1)} %get-tuple-element.83) | copy-start | bytes 1572868
  122.2 22.8 %all-to-all-start.2 = ((bf16[3,256,8,128]{1,3,0,2:T(8,128)(2,1)}), bf16[3,256,8,128]{1,3,0,2:T(8,128)(2,1)S(1)}, u32[]{:S(2)}, u32[]{:S(2)}) async-start(bf16[3,256,8,128]{1,3,0,2:T(8,128)(2,1)} %copy.236), calls=%async_computation.2 | async-start | bytes 3145728 | tf_op jit(solution)/shard_map/all_to_all | solution.py:129
  132.5 1.0 copy-start.6
  135.8 1.0 copy-start.6
  139.1 1.0 copy-start.6
  142.5 1.0 copy-start.6
  148.1 10.2 %copy-start.2 = (bf16[4,512,128]{2,1,0:T(8,128)(2,1)S(1)}, bf16[4,512,128]{2,1,0:T(8,128)(2,1)}, u32[]{:S(2)}) copy-start(bf16[4,512,128]{2,1,0:T(8,128)(2,1)} %copy-done.1) | copy-start | bytes 1572868
  169.6 10.9 %copy-start.7 = (f32[1,2,8,64]{3,2,1,0:T(8,128)S(1)}, f32[1,2,8,64]{3,2,1,0:T(8,128)}, u32[]{:S(2)}) copy-start(f32[1,2,8,64]{3,2,1,0:T(8,128)} %param.21) | copy-start | bytes 12292
  171.2 26.2 %all-to-all-start.3 = ((f32[8,640,64]{1,2,0:T(8,128)}), f32[8,640,64]{1,2,0:T(8,128)S(1)}, u32[]{:S(2)}, u32[]{:S(2)}) async-start(f32[8,640,64]{1,2,0:T(8,128)} %bitcast_dynamic-update-slice_fusion), calls=%async_computation.3 | async-start | bytes 2621440 | tf_op jit(solution)/shard_map/all_to_all | solution.py:138
  199.8 3.1 %copy-start.8 = (f32[512]{0:T(512)S(1)}, f32[512]{0:T(512)}, u32[]{:S(2)}) copy-start(f32[512]{0:T(512)} %param.20) | copy-start | bytes 6148
  199.8 3.1 %copy-start.11 = (pred[8,9]{0,1:T(8,128)(4,1)S(1)}, pred[8,9]{0,1:T(8,128)(4,1)}, u32[]{:S(2)}) copy-start(pred[8,9]{0,1:T(8,128)(4,1)} %constant.92) | copy-start | bytes 220
  206.1 1.0 copy-start.9
  207.9 13.4 %all-to-all-start.4 = ((f32[8,2,512]{2,1,0:T(2,128)}), f32[8,2,512]{2,1,0:T(2,128)S(1)}, u32[]{:S(2)}, u32[]{:S(2)}) async-start(f32[8,2,512]{2,1,0:T(2,128)} %reshape.231), calls=%async_computation.4 | async-start | bytes 65536 | tf_op jit(solution)/shard_map/all_to_all | solution.py:188

commit v5 on v3

--- a/solution.py
+++ b/solution.py
@@ -41,21 +41,23 @@
 
 
 def halo_tables(tile_count):
-    quarter = S_DEV // 4
-    tile_token = np.arange(S_DEV)
-    positions, offsets = [], []
+    positions, halves = [], []
     for tile in range(tile_count):
-        band = tile % TR
-        token_row = 0 if band == 0 else RT - 1
-        row_tokens = np.array(
-            [f * RT * WT + token_row * WT + c for f in range(FT) for c in range(WT)]
-        )
+        lower = 0 if tile % TR == 0 else 1
         earlier = tile - TR if tile >= TR else 0
         diagonal = (tile - TR) ^ 1 if tile >= TR else 0
-        parts = [(earlier, tile_token), (tile, tile_token), (diagonal, row_tokens), (tile ^ 1, row_tokens)]
-        positions.append(np.concatenate([4 * src + idx // quarter for src, idx in parts]))
-        offsets.append(np.concatenate([idx % quarter for src, idx in parts]))
-    return np.stack(positions).astype(np.int32), np.stack(offsets).astype(np.int32)
+        pos, half = [], []
+        for src in (earlier, tile):
+            for q in range(4):
+                pos += [4 * src + q, 4 * src + q]
+                half += [0, 1]
+        for src in (diagonal, tile ^ 1):
+            for f in range(FT):
+                pos.append(4 * src + 2 * f + lower)
+                half.append(lower)
+        positions.append(pos)
+        halves.append(half)
+    return np.array(positions, np.int32), np.array(halves, np.int32)
 
 
 def exchange_sum(blocks, axis, my_index):
@@ -116,24 +118,25 @@
     heads_dev = H // group_count
     quarter = S_DEV // 4
 
-    def to_groups(matrix):
-        return matrix.reshape(S_DEV, group_count, heads_dev, HD)
-
-    q_groups, k_groups, v_groups = to_groups(queries), to_groups(keys_in), to_groups(values_in)
+    slot_width = group_count * HD
     partial = None
     for slot in range(heads_dev):
+        columns = slice(slot * slot_width, (slot + 1) * slot_width)
         stacked = jnp.stack(
-            [q_groups[:, :, slot], k_groups[:, :, slot], v_groups[:, :, slot]], axis=2
-        )
-        gathered = lax.all_to_all(stacked, "seq", split_axis=1, concat_axis=0, tiled=True)
-        head_out = head_attention(gathered[:, 0, 0], gathered[:, 0, 1], gathered[:, 0, 2])
-        proj_rows = lax.dynamic_slice_in_dim(latent_proj, (my_index * heads_dev + slot) * HD, HD, 0)
+            [queries[:, columns], keys_in[:, columns], values_in[:, columns]], axis=0
+        ).reshape(3, S_DEV, group_count, HD)
+        gathered = lax.all_to_all(stacked, "seq", split_axis=2, concat_axis=1, tiled=True)
+        head_out = head_attention(gathered[0, :, 0], gathered[1, :, 0], gathered[2, :, 0])
+        proj_rows = lax.dynamic_slice_in_dim(latent_proj, (slot * group_count + my_index) * HD, HD, 0)
         term = jnp.dot(head_out, proj_rows, preferred_element_type=jnp.float32)
         partial = term if partial is None else partial + term
 
-    positions, offsets = halo_tables(group_count)
-    token_ids = tile_block[positions] * quarter + offsets
-    outgoing = partial[token_ids.reshape(-1)].reshape(group_count, -1, 4 * LC)
+    positions, halves = halo_tables(group_count)
+    picks = jnp.sum(
+        jnp.where(positions[..., None] == np.arange(4 * group_count), tile_block, 0), axis=-1
+    )
+    half_pieces = partial.reshape(8 * group_count, quarter // 2, 4 * LC)
+    outgoing = half_pieces[picks * 2 + halves].reshape(group_count, -1, 4 * LC)
     returned = lax.all_to_all(outgoing, "seq", split_axis=0, concat_axis=0, tiled=True)
     tokens = jnp.sum(returned, axis=0).astype(jnp.bfloat16)
     band_row = my_index % TR

time: 235 us -> 219 us (0.932)
  local copies, waits for them, and re-layouts: 82.2 us -> 48.7 us
  starting transfers between devices: 32.9 us -> 43.7 us
  waiting for transfers between devices: 72.1 us -> 77 us
    gather x2 -> x1, local copies, waits for them, and re-layouts: 48.5 us -> 2.37 us  [local(): outgoing = half_pieces[picks * 2 + halves].reshape(group_count, -1, 4 * LC)]
    all_to_all x3, waiting for transfers between devices: 40.8 us -> 51.6 us  [local(): lax.all_to_all(stacked, 'seq', split_axis=2, concat_axis=1, tiled=True)]
    all_to_all x3, starting transfers between devices: 24.5 us -> 32.6 us  [local(): lax.all_to_all(stacked, 'seq', split_axis=2, concat_axis=1, tiled=True)]
    slice x3 -> x6, local copies, waits for them, and re-layouts: 3.24 us -> 11.3 us  [the longest x3 4.14 us: local(): gathered[2, :, 0]]
    another operation x3 -> x6, local copies, waits for them, and re-layouts: 1.01 us -> 7.82 us  [the longest x3 6.81 us: local(): jnp.stack([queries[:, columns], keys_in[:, columns], values_in[:, columns...]
    unnamed x33, local copies, waits for them, and re-layouts: 7.15 us -> 13.9 us
    all_to_all x1, waiting for transfers between devices: 22.5 us -> 16.7 us  [local(): lax.all_to_all(outgoing, 'seq', split_axis=0, concat_axis=0, tiled=True)]
    all_to_all x3 -> x0, local copies, waits for them, and re-layouts: 5.74 us -> none  [local(): lax.all_to_all(stacked, 'seq', split_axis=1, concat_axis=0, tiled=True)]
  transfers between devices with their start and end apart: 5 -> 5, of which waited for: 5 -> 5; matrix products, arithmetic and copies ran while one was open for 29% -> 22% of each run, Pallas kernels for 0% -> 0%
where the time goes in v5:
time: 219 us; the launch traced here: 217 us
  waiting for transfers between devices  77 us (35%)
  local copies, waits for them, and re-layouts  48.7 us (22%)
  starting transfers between devices  43.7 us (20%)
  matrix products  27.6 us (13%)
  other arithmetic  18.9 us (9%)
    all_to_all x3, waiting for transfers between devices, local(): lax.all_to_all(stacked, 'seq', split_axis=2, concat_axis=1, tiled=True)  51.6 us
    all_to_all x3, starting transfers between devices, local(): lax.all_to_all(stacked, 'seq', split_axis=2, concat_axis=1, tiled=True)  32.6 us
    all_to_all x1, waiting for transfers between devices, local(): lax.all_to_all(outgoing, 'seq', split_axis=0, concat_axis=0, tiled=True)  16.7 us
    unnamed x33, local copies, waits for them, and re-layouts  13.9 us
    dot_general x12, matrix products, one_block(): jnp.dot(expo.astype(jnp.bfloat16), value, preferred_element_type=jnp.floa...  13.2 us
    reduce_sum x12, other arithmetic, one_block(): totals = jnp.sum(expo, axis=-1, keepdims=True)  9.81 us
    dot_general x12, matrix products, one_block(): jnp.dot(query_part, key.T, preferred_element_type=jnp.float32) * score_scale  9.46 us
    all_to_all x1, waiting for transfers between devices, local(): lax.all_to_all(by_owner.reshape(group_count, BPD, CO), 'seq', split_axis=...  8.73 us
  transfers between devices with their start and end apart: 5, of which 5 were waited for; matrix products, arithmetic and copies ran while one was open for 22% of the time, Pallas kernels for 0%

profile of v5, /device:TPU:80, one launch (start us, length us, event | category | flops | bytes accessed | tf_op | source)
XLA Modules:
  0.0 217.1 jit_solution(11921631891233360568)
XLA Ops:
  0.6 2.4 %fusion.101 = (bf16[256,1024]{1,0:T(8,128)(2,1)S(1)}, bf16[256,1024]{1,0:T(8,128)(2,1)}, bf16[256,1024]{1,0:T(8,128)(2,1)S(1)}) fusion(bf16[256,3072]{1,0:T(8,128)(2,1)} %param.17), kind=kLoop, calls=%fused_computation.106 | loop fusion | bytes 3145728 | tf_op jit(solution)/shard_map/slice | solution.py:126
  4.0 2.3 %fusion.102 = (bf16[256,1024]{1,0:T(8,128)(2,1)S(1)}, bf16[256,1024]{1,0:T(8,128)(2,1)}, bf16[256,1024]{1,0:T(8,128)(2,1)S(1)}) fusion(bf16[256,3072]{1,0:T(8,128)(2,1)} %param.18), kind=kLoop, calls=%fused_computation.107 | loop fusion | bytes 3145728 | tf_op jit(solution)/shard_map/slice | solution.py:126
  7.3 2.4 %fusion.103 = (bf16[256,1024]{1,0:T(8,128)(2,1)}, bf16[256,1024]{1,0:T(8,128)(2,1)}, bf16[256,1024]{1,0:T(8,128)(2,1)S(1)}) fusion(bf16[256,3072]{1,0:T(8,128)(2,1)} %param.19), kind=kLoop, calls=%fused_computation.108 | loop fusion | bytes 3145728 | tf_op jit(solution)/shard_map/slice | solution.py:126
  10.8 1.5 pad_maximum_fusion
  12.3 1.6 copy.123
  13.9 9.1 %all-to-all-start = ((bf16[3,256,8,128]{3,1,0,2:T(8,128)(2,1)}), bf16[3,256,8,128]{3,1,0,2:T(8,128)(2,1)S(1)}, u32[]{:S(2)}, u32[]{:S(2)}) async-start(bf16[3,256,8,128]{3,1,0,2:T(8,128)(2,1)} %copy.123), calls=%async_computation | async-start | bytes 3145728 | tf_op jit(solution)/shard_map/all_to_all | solution.py:128
  23.0 2.0 copy.156
  25.1 2.0 copy.157
  27.1 2.0 copy.158
  29.2 2.7 %pad_maximum_fusion.1 = bf16[3,256,8,128]{1,3,2,0:T(8,128)(2,1)} fusion(bf16[1,256,8,128]{1,3,2,0:T(8,128)(2,1)} %bitcast.146, bf16[1,256,8,128]{1,3,2,0:T(8,128)(2,1)} %bitcast.144, bf16[1,256,8,128]{1,3,2,0:T(8,128)(2,1)} %bitcast.142), kind=kLoop, calls=%fused_computation.58 | loop fusion | flops 1572864 | bytes 3145728 | tf_op jit(solution)/shard_map/stack | solution.py:125
  31.9 2.6 %copy.127 = bf16[3,256,8,128]{3,1,0,2:T(8,128)(2,1)} copy(bf16[3,256,8,128]{1,3,2,0:T(8,128)(2,1)} %pad_maximum_fusion.1) | data formatting | bytes 3145728 | tf_op jit(solution)/shard_map/stack | solution.py:125
  37.7 2.4 %pad_maximum_fusion.2 = bf16[3,256,8,128]{1,3,2,0:T(8,128)(2,1)} fusion(bf16[1,256,8,128]{1,3,2,0:T(8,128)(2,1)S(1)} %bitcast.147, bf16[1,256,8,128]{1,3,2,0:T(8,128)(2,1)} %bitcast.143, bf16[1,256,8,128]{1,3,2,0:T(8,128)(2,1)S(1)} %bitcast.141), kind=kLoop, calls=%fused_computation.59 | loop fusion | flops 1572864 | bytes 3145728 | tf_op jit(solution)/shard_map/stack | solution.py:125
  40.1 2.6 %copy.131 = bf16[3,256,8,128]{3,1,0,2:T(8,128)(2,1)} copy(bf16[3,256,8,128]{1,3,2,0:T(8,128)(2,1)} %pad_maximum_fusion.2) | data formatting | bytes 3145728 | tf_op jit(solution)/shard_map/stack | solution.py:125
  43.3 21.9 %all-to-all-done = bf16[3,256,8,128]{3,1,0,2:T(8,128)(2,1)S(1)} async-done(((bf16[3,256,8,128]{3,1,0,2:T(8,128)(2,1)}), bf16[3,256,8,128]{3,1,0,2:T(8,128)(2,1)S(1)}, u32[]{:S(2)}, u32[]{:S(2)}) %all-to-all-start) | async-done | bytes 1572896 | tf_op jit(solution)/shard_map/all_to_all | solution.py:128
  65.2 19.7 %all-to-all-start.1 = ((bf16[3,256,8,128]{3,1,0,2:T(8,128)(2,1)}), bf16[3,256,8,128]{3,1,0,2:T(8,128)(2,1)}, u32[]{:S(2)}, u32[]{:S(2)}) async-start(bf16[3,256,8,128]{3,1,0,2:T(8,128)(2,1)} %copy.127), calls=%async_computation.1 | async-start | bytes 3145728 | tf_op jit(solution)/shard_map/all_to_all | solution.py:128
  85.9 11.0 %while.30 = (s32[]{:T(128)}, bf16[4,512,128]{2,1,0:T(8,128)(2,1)S(1)}, bf16[4,512,128]{2,1,0:T(8,128)(2,1)S(1)}, bf16[2048,128]{1,0:T(8,128)(2,1)S(1)}, bf16[2048,128]{1,0:T(8,128)(2,1)}, /*index=5*/s32[]{:T(128)}) while((s32[]{:T(128)}, bf16[4,512,128]{2,1,0:T(8,128)(2,1)S(1)}, bf16[4,512,128]{2,1,0:T(8,128)(2,1)S(1)}, ...), condition=%wide.region_3.4_spmd, body=%wide.region_0.3_spmd.sunk | while | flops 545389568 | bytes 16001129 | solution.py:86
  97.0 28.1 %all-to-all-done.1 = bf16[3,256,8,128]{3,1,0,2:T(8,128)(2,1)} async-done(((bf16[3,256,8,128]{3,1,0,2:T(8,128)(2,1)}), bf16[3,256,8,128]{3,1,0,2:T(8,128)(2,1)}, u32[]{:S(2)}, u32[]{:S(2)}) %all-to-all-start.1) | async-done | bytes 1572896 | tf_op jit(solution)/shard_map/all_to_all | solution.py:128
  125.1 3.8 %all-to-all-start.2 = ((bf16[3,256,8,128]{3,1,0,2:T(8,128)(2,1)}), bf16[3,256,8,128]{3,1,0,2:T(8,128)(2,1)S(1)}, u32[]{:S(2)}, u32[]{:S(2)}) async-start(bf16[3,256,8,128]{3,1,0,2:T(8,128)(2,1)} %copy.131), calls=%async_computation.2 | async-start | bytes 3145728 | tf_op jit(solution)/shard_map/all_to_all | solution.py:128
  128.9 2.3 %fusion.104 = (bf16[1,8,256,1,128]{4,2,0,1,3:T(8,128)(2,1)}, bf16[1,8,256,1,128]{4,2,0,1,3:T(8,128)(2,1)S(1)}, bf16[1,8,256,1,128]{4,2,0,1,3:T(8,128)(2,1)S(1)}) fusion(bf16[3,8,256,1,128]{4,2,0,1,3:T(8,128)(2,1)} %bitcast.20), kind=kLoop, calls=%fused_computation.109 | loop fusion | bytes 3145728 | tf_op jit(solution)/shard_map/slice | solution.py:129
  132.0 13.3 %while.31 = (s32[]{:T(128)}, bf16[4,512,128]{2,1,0:T(8,128)(2,1)}, bf16[4,512,128]{2,1,0:T(8,128)(2,1)S(1)}, bf16[2048,128]{1,0:T(8,128)(2,1)S(1)}, bf16[2048,128]{1,0:T(8,128)(2,1)}, /*index=5*/s32[]{:T(128)}) while((s32[]{:T(128)}, bf16[4,512,128]{2,1,0:T(8,128)(2,1)}, bf16[4,512,128]{2,1,0:T(8,128)(2,1)S(1)}, ...), condition=%wide.region_7.8_spmd, body=%wide.region_4.7_spmd.sunk | while | flops 545389568 | bytes 16001637 | solution.py:86
  133.8 1.5 fusion.141
  137.2 1.5 fusion.141
  140.5 1.5 fusion.141
  145.3 1.6 all-to-all-done.2
  147.9 11.0 %while.32 = (s32[]{:T(128)}, bf16[4,512,128]{2,1,0:T(8,128)(2,1)S(1)}, bf16[4,512,128]{2,1,0:T(8,128)(2,1)S(1)}, bf16[2048,128]{1,0:T(8,128)(2,1)S(1)}, bf16[2048,128]{1,0:T(8,128)(2,1)}, /*index=5*/s32[]{:T(128)}) while((s32[]{:T(128)}, bf16[4,512,128]{2,1,0:T(8,128)(2,1)S(1)}, bf16[4,512,128]{2,1,0:T(8,128)(2,1)S(1)}, ...), condition=%wide.region_11.12_spmd, body=%wide.region_8.11_spmd.sunk | while | flops 545389568 | bytes 16001129 | solution.py:86
  162.7 2.4 %gather_fusion = f32[160,32,64]{2,1,0:T(8,128)} fusion(f32[64,32,64]{2,1,0:T(8,128)S(1)} %bitcast.128, s32[1024]{0:T(1024)S(1)} %pad_clamp_fusion), kind=kCustom, calls=%fused_computation | custom fusion | bytes 2622080 | tf_op jit(solution)/shard_map/gather | solution.py:139
  165.1 2.9 %copy.134 = f32[8,640,64]{1,2,0:T(8,128)} copy(f32[8,640,64]{2,1,0:T(8,128)} %bitcast.129) | data formatting | bytes 2621440 | tf_op jit(solution)/shard_map/reshape | solution.py:139
  168.0 7.7 %all-to-all-start.3 = ((f32[8,640,64]{1,2,0:T(8,128)}), f32[8,640,64]{1,2,0:T(8,128)S(1)}, u32[]{:S(2)}, u32[]{:S(2)}) async-start(f32[8,640,64]{1,2,0:T(8,128)} %copy.134), calls=%async_computation.3 | async-start | bytes 2621440 | tf_op jit(solution)/shard_map/all_to_all | solution.py:140
  175.9 16.7 %all-to-all-done.3 = f32[8,640,64]{1,2,0:T(8,128)S(1)} async-done(((f32[8,640,64]{1,2,0:T(8,128)}), f32[8,640,64]{1,2,0:T(8,128)S(1)}, u32[]{:S(2)}, u32[]{:S(2)}) %all-to-all-start.3) | async-done | bytes 1310752 | tf_op jit(solution)/shard_map/all_to_all | solution.py:140
  195.8 2.2 copy.145
  203.1 3.3 %all-to-all-start.4 = ((f32[8,2,512]{2,1,0:T(2,128)}), f32[8,2,512]{2,1,0:T(2,128)S(1)}, u32[]{:S(2)}, u32[]{:S(2)}) async-start(f32[8,2,512]{2,1,0:T(2,128)} %reshape.224), calls=%async_computation.4 | async-start | bytes 65536 | tf_op jit(solution)/shard_map/all_to_all | solution.py:190
  207.8 8.7 %all-to-all-done.4 = f32[8,2,512]{2,1,0:T(2,128)S(1)} async-done(((f32[8,2,512]{2,1,0:T(2,128)}), f32[8,2,512]{2,1,0:T(2,128)S(1)}, u32[]{:S(2)}, u32[]{:S(2)}) %all-to-all-start.4) | async-done | bytes 32800 | tf_op jit(solution)/shard_map/all_to_all | solution.py:190
  (135 shorter events, 54.3 us)
Async XLA Ops:
  0.6 197.4 %copy-start = (bf16[432,512]{1,0:T(8,128)(2,1)S(1)}, bf16[432,512]{1,0:T(8,128)(2,1)}, u32[]{:S(2)}) copy-start(bf16[432,512]{1,0:T(8,128)(2,1)} %param.21) | copy-start | bytes 1327108
  13.9 51.3 %all-to-all-start = ((bf16[3,256,8,128]{3,1,0,2:T(8,128)(2,1)}), bf16[3,256,8,128]{3,1,0,2:T(8,128)(2,1)S(1)}, u32[]{:S(2)}, u32[]{:S(2)}) async-start(bf16[3,256,8,128]{3,1,0,2:T(8,128)(2,1)} %copy.123), calls=%async_computation | async-start | bytes 3145728 | tf_op jit(solution)/shard_map/all_to_all | solution.py:128
  35.4 2.2 %copy-start.3 = (bf16[256,1024]{0,1:T(8,128)(2,1)S(1)}, bf16[256,1024]{0,1:T(8,128)(2,1)}, u32[]{:S(2)}) copy-start(bf16[256,1024]{0,1:T(8,128)(2,1)} %copy.159) | copy-start | bytes 1572868
  40.1 2.6 %copy-start.7 = (pred[8,20,32]{2,0,1:T(8,128)(4,1)S(1)}, pred[8,20,32]{2,0,1:T(8,128)(4,1)}, u32[]{:S(2)}) copy-start(pred[8,20,32]{2,0,1:T(8,128)(4,1)} %constant.88.clone) | copy-start | bytes 15364
  40.1 2.6 %copy-start.11 = (s32[32]{0:T(128)S(1)}, s32[32]{0:T(128)}, u32[]{:S(2)}) copy-start(s32[32]{0:T(128)} %param.24) | copy-start | bytes 388
  40.1 3.1 %copy-start.8 = (s32[8,20]{0,1:T(8,128)S(1)}, s32[8,20]{0,1:T(8,128)}, u32[]{:S(2)}) copy-start(s32[8,20]{0,1:T(8,128)} %constant.89.clone) | copy-start | bytes 1924
  65.2 59.9 %all-to-all-start.1 = ((bf16[3,256,8,128]{3,1,0,2:T(8,128)(2,1)}), bf16[3,256,8,128]{3,1,0,2:T(8,128)(2,1)}, u32[]{:S(2)}, u32[]{:S(2)}) async-start(bf16[3,256,8,128]{3,1,0,2:T(8,128)(2,1)} %copy.127), calls=%async_computation.1 | async-start | bytes 3145728 | tf_op jit(solution)/shard_map/all_to_all | solution.py:128
  86.7 1.0 copy-start.4
  89.5 1.0 copy-start.4
  92.2 1.0 copy-start.4
  95.0 1.0 copy-start.4
  96.9 28.1 %copy-start.1 = (bf16[4,512,128]{2,1,0:T(8,128)(2,1)}, bf16[4,512,128]{2,1,0:T(8,128)(2,1)S(1)}, u32[]{:S(2)}) copy-start(bf16[4,512,128]{2,1,0:T(8,128)(2,1)S(1)} %get-tuple-element.83) | copy-start | bytes 1572868
  125.1 21.8 %all-to-all-start.2 = ((bf16[3,256,8,128]{3,1,0,2:T(8,128)(2,1)}), bf16[3,256,8,128]{3,1,0,2:T(8,128)(2,1)S(1)}, u32[]{:S(2)}, u32[]{:S(2)}) async-start(bf16[3,256,8,128]{3,1,0,2:T(8,128)(2,1)} %copy.131), calls=%async_computation.2 | async-start | bytes 3145728 | tf_op jit(solution)/shard_map/all_to_all | solution.py:128
  132.8 1.0 copy-start.5
  136.1 1.0 copy-start.5
  139.4 1.0 copy-start.5
  142.8 1.0 copy-start.5
  147.9 11.0 %copy-start.2 = (bf16[4,512,128]{2,1,0:T(8,128)(2,1)S(1)}, bf16[4,512,128]{2,1,0:T(8,128)(2,1)}, u32[]{:S(2)}) copy-start(bf16[4,512,128]{2,1,0:T(8,128)(2,1)} %copy-done.1) | copy-start | bytes 1572868
  148.7 1.0 copy-start.6
  151.5 1.0 copy-start.6
  154.2 1.0 copy-start.6
  157.0 1.0 copy-start.6
  165.1 10.7 %copy-start.9 = (f32[1,2,8,64]{3,2,1,0:T(8,128)S(1)}, f32[1,2,8,64]{3,2,1,0:T(8,128)}, u32[]{:S(2)}) copy-start(f32[1,2,8,64]{3,2,1,0:T(8,128)} %param.23) | copy-start | bytes 12292
  168.0 24.6 %all-to-all-start.3 = ((f32[8,640,64]{1,2,0:T(8,128)}), f32[8,640,64]{1,2,0:T(8,128)S(1)}, u32[]{:S(2)}, u32[]{:S(2)}) async-start(f32[8,640,64]{1,2,0:T(8,128)} %copy.134), calls=%async_computation.3 | async-start | bytes 2621440 | tf_op jit(solution)/shard_map/all_to_all | solution.py:140
  194.8 3.3 %copy-start.10 = (f32[512]{0:T(512)S(1)}, f32[512]{0:T(512)}, u32[]{:S(2)}) copy-start(f32[512]{0:T(512)} %param.22) | copy-start | bytes 6148
  194.8 3.3 %copy-start.13 = (pred[8,9]{0,1:T(8,128)(4,1)S(1)}, pred[8,9]{0,1:T(8,128)(4,1)}, u32[]{:S(2)}) copy-start(pred[8,9]{0,1:T(8,128)(4,1)} %constant.98) | copy-start | bytes 220
  201.3 1.0 copy-start.12
  203.1 13.4 %all-to-all-start.4 = ((f32[8,2,512]{2,1,0:T(2,128)}), f32[8,2,512]{2,1,0:T(2,128)S(1)}, u32[]{:S(2)}, u32[]{:S(2)}) async-start(f32[8,2,512]{2,1,0:T(2,128)} %reshape.224), calls=%async_computation.4 | async-start | bytes 65536 | tf_op jit(solution)/shard_map/all_to_all | solution.py:190

commit v6 on v5

--- a/solution.py
+++ b/solution.py
@@ -4,6 +4,8 @@
 import numpy as np
 import jax.numpy as jnp
 from jax import lax
+from jax.experimental import pallas as pl
+from jax.experimental.pallas import tpu as pltpu
 from jax.sharding import PartitionSpec as P
 
 H = 24
@@ -71,6 +73,33 @@
     return total
 
 
+def slot_operand(queries, keys_in, values_in, slot, group_count):
+    sources = (queries, keys_in, values_in)
+    base = slot * group_count * HD
+
+    def kernel(q_ref, k_ref, v_ref, out_ref, sems):
+        copies = []
+        for part, src in enumerate((q_ref, k_ref, v_ref)):
+            for group in range(group_count):
+                copy = pltpu.make_async_copy(
+                    src.at[:, pl.ds(base + group * HD, HD)],
+                    out_ref.at[group, part],
+                    sems.at[part * group_count + group],
+                )
+                copy.start()
+                copies.append(copy)
+        for copy in copies:
+            copy.wait()
+
+    return pl.pallas_call(
+        kernel,
+        out_shape=jax.ShapeDtypeStruct((group_count, 3, S_DEV, HD), queries.dtype),
+        in_specs=[pl.BlockSpec(memory_space=pl.ANY)] * 3,
+        out_specs=pl.BlockSpec(memory_space=pl.ANY),
+        scratch_shapes=[pltpu.SemaphoreType.DMA((3 * group_count,))],
+    )(*sources)
+
+
 def head_attention(query, key, value):
     length = query.shape[0]
     score_scale = 1.0 / math.sqrt(query.shape[1])
@@ -118,15 +147,13 @@
     heads_dev = H // group_count
     quarter = S_DEV // 4
 
-    slot_width = group_count * HD
     partial = None
     for slot in range(heads_dev):
-        columns = slice(slot * slot_width, (slot + 1) * slot_width)
-        stacked = jnp.stack(
-            [queries[:, columns], keys_in[:, columns], values_in[:, columns]], axis=0
-        ).reshape(3, S_DEV, group_count, HD)
-        gathered = lax.all_to_all(stacked, "seq", split_axis=2, concat_axis=1, tiled=True)
-        head_out = head_attention(gathered[0, :, 0], gathered[1, :, 0], gathered[2, :, 0])
+        stacked = slot_operand(queries, keys_in, values_in, slot, group_count)
+        gathered = lax.all_to_all(stacked, "seq", split_axis=0, concat_axis=0, tiled=True)
+        head_out = head_attention(
+            *(gathered[:, part].reshape(seq_len, HD) for part in range(3))
+        )
         proj_rows = lax.dynamic_slice_in_dim(latent_proj, (slot * group_count + my_index) * HD, HD, 0)
         term = jnp.dot(head_out, proj_rows, preferred_element_type=jnp.float32)
         partial = term if partial is None else partial + term

time: 219 us -> 320 us (1.46)
  Pallas kernels: 0 us -> 147 us
  local copies, waits for them, and re-layouts: 48.7 us -> 22.4 us
  waiting for transfers between devices: 77 us -> 57 us
  other arithmetic: 18.9 us -> 12.3 us
  starting transfers between devices: 43.7 us -> 49.5 us
    pallas_call x0 -> x3, Pallas kernels: none -> 147 us  [slot_operand(): pl.pallas_call(kernel, out_shape=jax.ShapeDtypeStruct((group_count, 3, S_...]
    all_to_all x3, waiting for transfers between devices: 51.6 us -> 31.5 us  [local(): lax.all_to_all(stacked, 'seq', split_axis=0, concat_axis=0, tiled=True)]
    unnamed x33 -> x22, local copies, waits for them, and re-layouts: 13.9 us -> 1.52 us
    slice x6 -> x3, local copies, waits for them, and re-layouts: 11.3 us -> 4.15 us  [local(): gathered[:, part].reshape(seq_len, HD)]
    another operation x6 -> x3, local copies, waits for them, and re-layouts: 7.82 us -> 1.01 us  [the longest x3 6.81 us: local(): jnp.stack([queries[:, columns], keys_in[:, columns], values_in[:, columns...]
    another operation x3 -> x0, other arithmetic: 6.6 us -> none  [local(): jnp.stack([queries[:, columns], keys_in[:, columns], values_in[:, columns...]
    all_to_all x3, starting transfers between devices: 32.6 us -> 38.3 us  [local(): lax.all_to_all(stacked, 'seq', split_axis=0, concat_axis=0, tiled=True)]
  transfers between devices with their start and end apart: 5 -> 5, of which waited for: 5 -> 4; matrix products, arithmetic and copies ran while one was open for 22% -> 9% of each run, Pallas kernels for 0% -> 31%
where the time goes in v6:
time: 320 us; the launch traced here: 317 us
  Pallas kernels  147 us (46%)
  waiting for transfers between devices  57 us (18%)
  starting transfers between devices  49.5 us (15%)
  matrix products  27.6 us (9%)
  local copies, waits for them, and re-layouts  22.4 us (7%)
  other arithmetic  12.3 us (4%)
    pallas_call x3, Pallas kernels, slot_operand(): pl.pallas_call(kernel, out_shape=jax.ShapeDtypeStruct((group_count, 3, S_...  147 us
    all_to_all x3, starting transfers between devices, local(): lax.all_to_all(stacked, 'seq', split_axis=0, concat_axis=0, tiled=True)  38.3 us
    all_to_all x3, waiting for transfers between devices, local(): lax.all_to_all(stacked, 'seq', split_axis=0, concat_axis=0, tiled=True)  31.5 us
    all_to_all x1, waiting for transfers between devices, local(): lax.all_to_all(outgoing, 'seq', split_axis=0, concat_axis=0, tiled=True)  16.8 us
    dot_general x12, matrix products, one_block(): jnp.dot(expo.astype(jnp.bfloat16), value, preferred_element_type=jnp.floa...  13.1 us
    reduce_sum x12, other arithmetic, one_block(): totals = jnp.sum(expo, axis=-1, keepdims=True)  9.81 us
    dot_general x12, matrix products, one_block(): jnp.dot(query_part, key.T, preferred_element_type=jnp.float32) * score_scale  9.45 us
    all_to_all x1, waiting for transfers between devices, local(): lax.all_to_all(by_owner.reshape(group_count, BPD, CO), 'seq', split_axis=...  8.73 us
  transfers between devices with their start and end apart: 5, of which 4 were waited for; matrix products, arithmetic and copies ran while one was open for 9% of the time, Pallas kernels for 31%

profile of v6, /device:TPU:80, one launch (start us, length us, event | category | flops | bytes accessed | tf_op | source)
XLA Modules:
  0.0 316.9 jit_solution(14895178080556240037)
XLA Ops:
  0.6 49.0 %shard_map.122 = bf16[8,3,256,128]{3,2,1,0:T(8,128)(2,1)} custom-call(bf16[256,3072]{1,0:T(8,128)(2,1)} %q_ref.5, bf16[256,3072]{1,0:T(8,128)(2,1)} %k_ref.5, bf16[256,3072]{1,0:T(8,128)(2,1)} %v_ref.5), custom_call_target="tpu_custom_call" | custom-call | tf_op jit(solution)/shard_map/pallas_call | solution.py:94
  49.6 9.1 %all-to-all-start = ((bf16[8,3,256,128]{3,2,1,0:T(8,128)(2,1)}), bf16[8,3,256,128]{3,2,1,0:T(8,128)(2,1)S(1)}, u32[]{:S(2)}, u32[]{:S(2)}) async-start(bf16[8,3,256,128]{3,2,1,0:T(8,128)(2,1)} %shard_map.122), calls=%async_computation | async-start | bytes 3145728 | tf_op jit(solution)/shard_map/all_to_all | solution.py:153
  58.8 49.0 %shard_map.123 = bf16[8,3,256,128]{3,2,1,0:T(8,128)(2,1)} custom-call(bf16[256,3072]{1,0:T(8,128)(2,1)} %q_ref.5, bf16[256,3072]{1,0:T(8,128)(2,1)} %k_ref.5, bf16[256,3072]{1,0:T(8,128)(2,1)} %v_ref.5), custom_call_target="tpu_custom_call" | custom-call | tf_op jit(solution)/shard_map/pallas_call | solution.py:94
  107.8 49.0 %shard_map.124 = bf16[8,3,256,128]{3,2,1,0:T(8,128)(2,1)} custom-call(bf16[256,3072]{1,0:T(8,128)(2,1)} %q_ref.5, bf16[256,3072]{1,0:T(8,128)(2,1)} %k_ref.5, bf16[256,3072]{1,0:T(8,128)(2,1)} %v_ref.5), custom_call_target="tpu_custom_call" | custom-call | tf_op jit(solution)/shard_map/pallas_call | solution.py:94
  157.4 9.6 %all-to-all-start.1 = ((bf16[8,3,256,128]{3,2,1,0:T(8,128)(2,1)}), bf16[8,3,256,128]{3,2,1,0:T(8,128)(2,1)}, u32[]{:S(2)}, u32[]{:S(2)}) async-start(bf16[8,3,256,128]{3,2,1,0:T(8,128)(2,1)} %shard_map.123), calls=%async_computation.1 | async-start | bytes 3145728 | tf_op jit(solution)/shard_map/all_to_all | solution.py:153
  167.0 0.9 fusion.102
  168.0 11.0 %while.30 = (s32[]{:T(128)}, bf16[4,512,128]{2,1,0:T(8,128)(2,1)S(1)}, bf16[4,512,128]{2,1,0:T(8,128)(2,1)S(1)}, bf16[2048,128]{1,0:T(8,128)(2,1)S(1)}, bf16[2048,128]{1,0:T(8,128)(2,1)}, /*index=5*/s32[]{:T(128)}) while((s32[]{:T(128)}, bf16[4,512,128]{2,1,0:T(8,128)(2,1)S(1)}, bf16[4,512,128]{2,1,0:T(8,128)(2,1)S(1)}, ...), condition=%wide.region_3.4_spmd, body=%wide.region_0.3_spmd.sunk | while | flops 545389568 | bytes 16001129 | solution.py:115
  179.0 29.7 %all-to-all-done.1 = bf16[8,3,256,128]{3,2,1,0:T(8,128)(2,1)} async-done(((bf16[8,3,256,128]{3,2,1,0:T(8,128)(2,1)}), bf16[8,3,256,128]{3,2,1,0:T(8,128)(2,1)}, u32[]{:S(2)}, u32[]{:S(2)}) %all-to-all-start.1) | async-done | bytes 1572896 | tf_op jit(solution)/shard_map/all_to_all | solution.py:153
  208.7 19.6 %all-to-all-start.2 = ((bf16[8,3,256,128]{3,2,1,0:T(8,128)(2,1)}), bf16[8,3,256,128]{3,2,1,0:T(8,128)(2,1)S(1)}, u32[]{:S(2)}, u32[]{:S(2)}) async-start(bf16[8,3,256,128]{3,2,1,0:T(8,128)(2,1)} %shard_map.124), calls=%async_computation.2 | async-start | bytes 3145728 | tf_op jit(solution)/shard_map/all_to_all | solution.py:153
  228.3 2.3 fusion.101
  231.5 13.3 %while.31 = (s32[]{:T(128)}, bf16[4,512,128]{2,1,0:T(8,128)(2,1)}, bf16[4,512,128]{2,1,0:T(8,128)(2,1)S(1)}, bf16[2048,128]{1,0:T(8,128)(2,1)S(1)}, bf16[2048,128]{1,0:T(8,128)(2,1)}, /*index=5*/s32[]{:T(128)}) while((s32[]{:T(128)}, bf16[4,512,128]{2,1,0:T(8,128)(2,1)}, bf16[4,512,128]{2,1,0:T(8,128)(2,1)S(1)}, ...), condition=%wide.region_7.8_spmd, body=%wide.region_4.7_spmd.sunk | while | flops 545389568 | bytes 16001637 | solution.py:115
  233.3 1.5 fusion.138
  236.6 1.5 fusion.138
  240.0 1.5 fusion.138
  243.3 1.5 fusion.138
  244.8 1.8 all-to-all-done.2
  246.5 0.9 fusion.100
  247.5 11.0 %while.32 = (s32[]{:T(128)}, bf16[4,512,128]{2,1,0:T(8,128)(2,1)S(1)}, bf16[4,512,128]{2,1,0:T(8,128)(2,1)S(1)}, bf16[2048,128]{1,0:T(8,128)(2,1)S(1)}, bf16[2048,128]{1,0:T(8,128)(2,1)}, /*index=5*/s32[]{:T(128)}) while((s32[]{:T(128)}, bf16[4,512,128]{2,1,0:T(8,128)(2,1)S(1)}, bf16[4,512,128]{2,1,0:T(8,128)(2,1)S(1)}, ...), condition=%wide.region_11.12_spmd, body=%wide.region_8.11_spmd.sunk | while | flops 545389568 | bytes 16001129 | solution.py:115
  249.4 0.9 fusion.143
  258.5 1.0 fusion.90
  259.6 1.3 convolution_add_fusion.1
  260.9 1.0 convolution_add_fusion
  262.3 2.4 gather_fusion
  264.7 3.0 copy.63
  267.6 7.9 %all-to-all-start.3 = ((f32[8,640,64]{1,2,0:T(8,128)}), f32[8,640,64]{1,2,0:T(8,128)S(1)}, u32[]{:S(2)}, u32[]{:S(2)}) async-start(f32[8,640,64]{1,2,0:T(8,128)} %copy.63), calls=%async_computation.3 | async-start | bytes 2621440 | tf_op jit(solution)/shard_map/all_to_all | solution.py:167
  275.6 16.8 %all-to-all-done.3 = f32[8,640,64]{1,2,0:T(8,128)S(1)} async-done(((f32[8,640,64]{1,2,0:T(8,128)}), f32[8,640,64]{1,2,0:T(8,128)S(1)}, u32[]{:S(2)}, u32[]{:S(2)}) %all-to-all-start.3) | async-done | bytes 1310752 | tf_op jit(solution)/shard_map/all_to_all | solution.py:167
  295.6 2.2 copy.74
  297.9 1.5 add_convert_fusion
  299.7 1.4 copy.76
  302.9 3.3 %all-to-all-start.4 = ((f32[8,2,512]{2,1,0:T(2,128)}), f32[8,2,512]{2,1,0:T(2,128)S(1)}, u32[]{:S(2)}, u32[]{:S(2)}) async-start(f32[8,2,512]{2,1,0:T(2,128)} %reshape.185), calls=%async_computation.4 | async-start | bytes 65536 | tf_op jit(solution)/shard_map/all_to_all | solution.py:217
  306.3 1.3 copy.79
  307.6 8.7 %all-to-all-done.4 = f32[8,2,512]{2,1,0:T(2,128)S(1)} async-done(((f32[8,2,512]{2,1,0:T(2,128)}), f32[8,2,512]{2,1,0:T(2,128)S(1)}, u32[]{:S(2)}, u32[]{:S(2)}) %all-to-all-start.4) | async-done | bytes 32800 | tf_op jit(solution)/shard_map/all_to_all | solution.py:217
  (118 shorter events, 36.2 us)
Async XLA Ops:
  0.6 297.2 %copy-start = (bf16[432,512]{1,0:T(8,128)(2,1)S(1)}, bf16[432,512]{1,0:T(8,128)(2,1)}, u32[]{:S(2)}) copy-start(bf16[432,512]{1,0:T(8,128)(2,1)} %param.21) | copy-start | bytes 1327108
  49.6 107.8 %all-to-all-start = ((bf16[8,3,256,128]{3,2,1,0:T(8,128)(2,1)}), bf16[8,3,256,128]{3,2,1,0:T(8,128)(2,1)S(1)}, u32[]{:S(2)}, u32[]{:S(2)}) async-start(bf16[8,3,256,128]{3,2,1,0:T(8,128)(2,1)} %shard_map.122), calls=%async_computation | async-start | bytes 3145728 | tf_op jit(solution)/shard_map/all_to_all | solution.py:153
  107.7 49.0 %copy-start.6 = (pred[8,20,32]{2,0,1:T(8,128)(4,1)S(1)}, pred[8,20,32]{2,0,1:T(8,128)(4,1)}, u32[]{:S(2)}) copy-start(pred[8,20,32]{2,0,1:T(8,128)(4,1)} %constant.88.clone) | copy-start | bytes 15364
  107.7 49.0 %copy-start.10 = (s32[32]{0:T(128)S(1)}, s32[32]{0:T(128)}, u32[]{:S(2)}) copy-start(s32[32]{0:T(128)} %param.24) | copy-start | bytes 388
  107.8 49.4 %copy-start.7 = (s32[8,20]{0,1:T(8,128)S(1)}, s32[8,20]{0,1:T(8,128)}, u32[]{:S(2)}) copy-start(s32[8,20]{0,1:T(8,128)} %constant.89.clone) | copy-start | bytes 1924
  157.4 51.3 %all-to-all-start.1 = ((bf16[8,3,256,128]{3,2,1,0:T(8,128)(2,1)}), bf16[8,3,256,128]{3,2,1,0:T(8,128)(2,1)}, u32[]{:S(2)}, u32[]{:S(2)}) async-start(bf16[8,3,256,128]{3,2,1,0:T(8,128)(2,1)} %shard_map.123), calls=%async_computation.1 | async-start | bytes 3145728 | tf_op jit(solution)/shard_map/all_to_all | solution.py:153
  168.8 1.0 copy-start.3
  171.6 1.0 copy-start.3
  174.3 1.0 copy-start.3
  177.1 1.0 copy-start.3
  179.0 29.7 %copy-start.1 = (bf16[4,512,128]{2,1,0:T(8,128)(2,1)}, bf16[4,512,128]{2,1,0:T(8,128)(2,1)S(1)}, u32[]{:S(2)}) copy-start(bf16[4,512,128]{2,1,0:T(8,128)(2,1)S(1)} %get-tuple-element.83) | copy-start | bytes 1572868
  208.7 37.8 %all-to-all-start.2 = ((bf16[8,3,256,128]{3,2,1,0:T(8,128)(2,1)}), bf16[8,3,256,128]{3,2,1,0:T(8,128)(2,1)S(1)}, u32[]{:S(2)}, u32[]{:S(2)}) async-start(bf16[8,3,256,128]{3,2,1,0:T(8,128)(2,1)} %shard_map.124), calls=%async_computation.2 | async-start | bytes 3145728 | tf_op jit(solution)/shard_map/all_to_all | solution.py:153
  232.2 1.0 copy-start.4
  235.6 1.0 copy-start.4
  238.9 1.0 copy-start.4
  242.2 1.0 copy-start.4
  247.5 11.0 %copy-start.2 = (bf16[4,512,128]{2,1,0:T(8,128)(2,1)S(1)}, bf16[4,512,128]{2,1,0:T(8,128)(2,1)}, u32[]{:S(2)}) copy-start(bf16[4,512,128]{2,1,0:T(8,128)(2,1)} %copy-done.1) | copy-start | bytes 1572868
  248.3 1.0 copy-start.5
  251.1 1.0 copy-start.5
  253.8 1.0 copy-start.5
  256.6 1.0 copy-start.5
  264.7 10.8 %copy-start.8 = (f32[1,2,8,64]{3,2,1,0:T(8,128)S(1)}, f32[1,2,8,64]{3,2,1,0:T(8,128)}, u32[]{:S(2)}) copy-start(f32[1,2,8,64]{3,2,1,0:T(8,128)} %param.23) | copy-start | bytes 12292
  267.6 24.8 %all-to-all-start.3 = ((f32[8,640,64]{1,2,0:T(8,128)}), f32[8,640,64]{1,2,0:T(8,128)S(1)}, u32[]{:S(2)}, u32[]{:S(2)}) async-start(f32[8,640,64]{1,2,0:T(8,128)} %copy.63), calls=%async_computation.3 | async-start | bytes 2621440 | tf_op jit(solution)/shard_map/all_to_all | solution.py:167
  294.2 3.6 %copy-start.9 = (f32[512]{0:T(512)S(1)}, f32[512]{0:T(512)}, u32[]{:S(2)}) copy-start(f32[512]{0:T(512)} %param.22) | copy-start | bytes 6148
  294.2 3.6 %copy-start.12 = (pred[8,9]{0,1:T(8,128)(4,1)S(1)}, pred[8,9]{0,1:T(8,128)(4,1)}, u32[]{:S(2)}) copy-start(pred[8,9]{0,1:T(8,128)(4,1)} %constant.98) | copy-start | bytes 220
  299.7 2.4 copy-start.11
  302.9 13.4 %all-to-all-start.4 = ((f32[8,2,512]{2,1,0:T(2,128)}), f32[8,2,512]{2,1,0:T(2,128)S(1)}, u32[]{:S(2)}, u32[]{:S(2)}) async-start(f32[8,2,512]{2,1,0:T(2,128)} %reshape.185), calls=%async_computation.4 | async-start | bytes 65536 | tf_op jit(solution)/shard_map/all_to_all | solution.py:217

commit v7 on v6

--- a/solution.py
+++ b/solution.py
@@ -74,30 +74,21 @@
 
 
 def slot_operand(queries, keys_in, values_in, slot, group_count):
-    sources = (queries, keys_in, values_in)
-    base = slot * group_count * HD
-
-    def kernel(q_ref, k_ref, v_ref, out_ref, sems):
-        copies = []
+    width = group_count * HD
+
+    def kernel(q_ref, k_ref, v_ref, out_ref):
         for part, src in enumerate((q_ref, k_ref, v_ref)):
             for group in range(group_count):
-                copy = pltpu.make_async_copy(
-                    src.at[:, pl.ds(base + group * HD, HD)],
-                    out_ref.at[group, part],
-                    sems.at[part * group_count + group],
-                )
-                copy.start()
-                copies.append(copy)
-        for copy in copies:
-            copy.wait()
-
+                out_ref[group, part] = src[:, group * HD : (group + 1) * HD]
+
+    block = pl.BlockSpec((S_DEV, width), lambda i: (0, slot))
     return pl.pallas_call(
         kernel,
+        grid=(1,),
         out_shape=jax.ShapeDtypeStruct((group_count, 3, S_DEV, HD), queries.dtype),
-        in_specs=[pl.BlockSpec(memory_space=pl.ANY)] * 3,
-        out_specs=pl.BlockSpec(memory_space=pl.ANY),
-        scratch_shapes=[pltpu.SemaphoreType.DMA((3 * group_count,))],
-    )(*sources)
+        in_specs=[block] * 3,
+        out_specs=pl.BlockSpec((group_count, 3, S_DEV, HD), lambda i: (0, 0, 0, 0)),
+    )(queries, keys_in, values_in)
 
 
 def head_attention(query, key, value):

time: 320 us -> 208 us (0.65)
  Pallas kernels: 147 us -> 8.43 us
  waiting for transfers between devices: 57 us -> 91.3 us
  starting transfers between devices: 49.5 us -> 43.5 us
    pallas_call x3, Pallas kernels: 147 us -> 8.43 us  [slot_operand(): pl.pallas_call(kernel, grid=(1,), out_shape=jax.ShapeDtypeStruct((group_c...]
    all_to_all x3, waiting for transfers between devices: 31.5 us -> 65.8 us  [local(): lax.all_to_all(stacked, 'seq', split_axis=0, concat_axis=0, tiled=True)]
    all_to_all x3, starting transfers between devices: 38.3 us -> 32.4 us  [local(): lax.all_to_all(stacked, 'seq', split_axis=0, concat_axis=0, tiled=True)]
  transfers between devices with their start and end apart: 5 -> 5, of which waited for: 4 -> 5; matrix products, arithmetic and copies ran while one was open for 9% -> 14% of each run, Pallas kernels for 31% -> 3%
where the time goes in v7:
time: 208 us; the launch traced here: 207 us
  waiting for transfers between devices  91.3 us (44%)
  starting transfers between devices  43.5 us (21%)
  matrix products  27.6 us (13%)
  local copies, waits for them, and re-layouts  22.4 us (11%)
  other arithmetic  12.3 us (6%)
  Pallas kernels  8.43 us (4%)
    all_to_all x3, waiting for transfers between devices, local(): lax.all_to_all(stacked, 'seq', split_axis=0, concat_axis=0, tiled=True)  65.8 us
    all_to_all x3, starting transfers between devices, local(): lax.all_to_all(stacked, 'seq', split_axis=0, concat_axis=0, tiled=True)  32.4 us
    all_to_all x1, waiting for transfers between devices, local(): lax.all_to_all(outgoing, 'seq', split_axis=0, concat_axis=0, tiled=True)  16.7 us
    dot_general x12, matrix products, one_block(): jnp.dot(expo.astype(jnp.bfloat16), value, preferred_element_type=jnp.floa...  13.2 us
    reduce_sum x12, other arithmetic, one_block(): totals = jnp.sum(expo, axis=-1, keepdims=True)  9.81 us
    dot_general x12, matrix products, one_block(): jnp.dot(query_part, key.T, preferred_element_type=jnp.float32) * score_scale  9.45 us
    all_to_all x1, waiting for transfers between devices, local(): lax.all_to_all(by_owner.reshape(group_count, BPD, CO), 'seq', split_axis=...  8.73 us
    pallas_call x3, Pallas kernels, slot_operand(): pl.pallas_call(kernel, grid=(1,), out_shape=jax.ShapeDtypeStruct((group_c...  8.43 us
  transfers between devices with their start and end apart: 5, of which 5 were waited for; matrix products, arithmetic and copies ran while one was open for 14% of the time, Pallas kernels for 3%

profile of v7, /device:TPU:80, one launch (start us, length us, event | category | flops | bytes accessed | tf_op | source)
XLA Modules:
  0.0 206.7 jit_solution(1903167164179144836)
XLA Ops:
  0.6 2.8 %shard_map.122 = bf16[8,3,256,128]{3,2,1,0:T(8,128)(2,1)} custom-call(bf16[256,3072]{1,0:T(8,128)(2,1)} %q_ref.5, bf16[256,3072]{1,0:T(8,128)(2,1)} %k_ref.5, bf16[256,3072]{1,0:T(8,128)(2,1)} %v_ref.5), custom_call_target="tpu_custom_call" | custom-call | tf_op jit(solution)/shard_map/pallas_call | solution.py:85
  3.5 9.1 %all-to-all-start = ((bf16[8,3,256,128]{3,2,1,0:T(8,128)(2,1)}), bf16[8,3,256,128]{3,2,1,0:T(8,128)(2,1)S(1)}, u32[]{:S(2)}, u32[]{:S(2)}) async-start(bf16[8,3,256,128]{3,2,1,0:T(8,128)(2,1)} %shard_map.122), calls=%async_computation | async-start | bytes 3145728 | tf_op jit(solution)/shard_map/all_to_all | solution.py:144
  12.6 2.8 %shard_map.123 = bf16[8,3,256,128]{3,2,1,0:T(8,128)(2,1)} custom-call(bf16[256,3072]{1,0:T(8,128)(2,1)} %q_ref.5, bf16[256,3072]{1,0:T(8,128)(2,1)} %k_ref.5, bf16[256,3072]{1,0:T(8,128)(2,1)} %v_ref.5), custom_call_target="tpu_custom_call" | custom-call | tf_op jit(solution)/shard_map/pallas_call | solution.py:85
  15.4 2.8 %shard_map.124 = bf16[8,3,256,128]{3,2,1,0:T(8,128)(2,1)} custom-call(bf16[256,3072]{1,0:T(8,128)(2,1)} %q_ref.5, bf16[256,3072]{1,0:T(8,128)(2,1)} %k_ref.5, bf16[256,3072]{1,0:T(8,128)(2,1)} %v_ref.5), custom_call_target="tpu_custom_call" | custom-call | tf_op jit(solution)/shard_map/pallas_call | solution.py:85
  18.8 35.9 %all-to-all-done = bf16[8,3,256,128]{3,2,1,0:T(8,128)(2,1)S(1)} async-done(((bf16[8,3,256,128]{3,2,1,0:T(8,128)(2,1)}), bf16[8,3,256,128]{3,2,1,0:T(8,128)(2,1)S(1)}, u32[]{:S(2)}, u32[]{:S(2)}) %all-to-all-start) | async-done | bytes 1572896 | tf_op jit(solution)/shard_map/all_to_all | solution.py:144
  54.8 19.7 %all-to-all-start.1 = ((bf16[8,3,256,128]{3,2,1,0:T(8,128)(2,1)}), bf16[8,3,256,128]{3,2,1,0:T(8,128)(2,1)}, u32[]{:S(2)}, u32[]{:S(2)}) async-start(bf16[8,3,256,128]{3,2,1,0:T(8,128)(2,1)} %shard_map.123), calls=%async_computation.1 | async-start | bytes 3145728 | tf_op jit(solution)/shard_map/all_to_all | solution.py:144
  74.5 0.9 fusion.102
  75.5 11.0 %while.30 = (s32[]{:T(128)}, bf16[4,512,128]{2,1,0:T(8,128)(2,1)S(1)}, bf16[4,512,128]{2,1,0:T(8,128)(2,1)S(1)}, bf16[2048,128]{1,0:T(8,128)(2,1)S(1)}, bf16[2048,128]{1,0:T(8,128)(2,1)}, /*index=5*/s32[]{:T(128)}) while((s32[]{:T(128)}, bf16[4,512,128]{2,1,0:T(8,128)(2,1)S(1)}, bf16[4,512,128]{2,1,0:T(8,128)(2,1)S(1)}, ...), condition=%wide.region_3.4_spmd, body=%wide.region_0.3_spmd.sunk | while | flops 545389568 | bytes 16001129 | solution.py:106
  86.5 28.1 %all-to-all-done.1 = bf16[8,3,256,128]{3,2,1,0:T(8,128)(2,1)} async-done(((bf16[8,3,256,128]{3,2,1,0:T(8,128)(2,1)}), bf16[8,3,256,128]{3,2,1,0:T(8,128)(2,1)}, u32[]{:S(2)}, u32[]{:S(2)}) %all-to-all-start.1) | async-done | bytes 1572896 | tf_op jit(solution)/shard_map/all_to_all | solution.py:144
  114.6 3.6 %all-to-all-start.2 = ((bf16[8,3,256,128]{3,2,1,0:T(8,128)(2,1)}), bf16[8,3,256,128]{3,2,1,0:T(8,128)(2,1)S(1)}, u32[]{:S(2)}, u32[]{:S(2)}) async-start(bf16[8,3,256,128]{3,2,1,0:T(8,128)(2,1)} %shard_map.124), calls=%async_computation.2 | async-start | bytes 3145728 | tf_op jit(solution)/shard_map/all_to_all | solution.py:144
  118.2 2.3 %fusion.101 = (bf16[8,1,256,128]{3,2,1,0:T(8,128)(2,1)}, bf16[8,1,256,128]{3,2,1,0:T(8,128)(2,1)S(1)}, bf16[8,1,256,128]{3,2,1,0:T(8,128)(2,1)S(1)}) fusion(bf16[8,3,256,128]{3,2,1,0:T(8,128)(2,1)} %all-to-all-done.1), kind=kLoop, calls=%fused_computation.103 | loop fusion | bytes 3145728 | tf_op jit(solution)/shard_map/slice | solution.py:146
  121.4 13.3 %while.31 = (s32[]{:T(128)}, bf16[4,512,128]{2,1,0:T(8,128)(2,1)}, bf16[4,512,128]{2,1,0:T(8,128)(2,1)S(1)}, bf16[2048,128]{1,0:T(8,128)(2,1)S(1)}, bf16[2048,128]{1,0:T(8,128)(2,1)}, /*index=5*/s32[]{:T(128)}) while((s32[]{:T(128)}, bf16[4,512,128]{2,1,0:T(8,128)(2,1)}, bf16[4,512,128]{2,1,0:T(8,128)(2,1)S(1)}, ...), condition=%wide.region_7.8_spmd, body=%wide.region_4.7_spmd.sunk | while | flops 545389568 | bytes 16001637 | solution.py:106
  123.2 1.5 fusion.138
  126.6 1.5 fusion.138
  129.9 1.5 fusion.138
  133.2 1.5 fusion.138
  134.7 1.8 all-to-all-done.2
  136.5 0.9 fusion.100
  137.5 11.0 %while.32 = (s32[]{:T(128)}, bf16[4,512,128]{2,1,0:T(8,128)(2,1)S(1)}, bf16[4,512,128]{2,1,0:T(8,128)(2,1)S(1)}, bf16[2048,128]{1,0:T(8,128)(2,1)S(1)}, bf16[2048,128]{1,0:T(8,128)(2,1)}, /*index=5*/s32[]{:T(128)}) while((s32[]{:T(128)}, bf16[4,512,128]{2,1,0:T(8,128)(2,1)S(1)}, bf16[4,512,128]{2,1,0:T(8,128)(2,1)S(1)}, ...), condition=%wide.region_11.12_spmd, body=%wide.region_8.11_spmd.sunk | while | flops 545389568 | bytes 16001129 | solution.py:106
  148.5 1.0 fusion.90
  149.5 1.3 convolution_add_fusion.1
  150.9 1.0 convolution_add_fusion
  152.3 2.4 %gather_fusion = f32[160,32,64]{2,1,0:T(8,128)} fusion(f32[64,32,64]{2,1,0:T(8,128)S(1)} %bitcast.110, s32[1024]{0:T(1024)S(1)} %pad_clamp_fusion), kind=kCustom, calls=%fused_computation | custom fusion | bytes 2622080 | tf_op jit(solution)/shard_map/gather | solution.py:157
  154.6 3.0 %copy.63 = f32[8,640,64]{1,2,0:T(8,128)} copy(f32[8,640,64]{2,1,0:T(8,128)} %bitcast.111) | data formatting | bytes 2621440 | tf_op jit(solution)/shard_map/reshape | solution.py:157
  157.6 7.8 %all-to-all-start.3 = ((f32[8,640,64]{1,2,0:T(8,128)}), f32[8,640,64]{1,2,0:T(8,128)S(1)}, u32[]{:S(2)}, u32[]{:S(2)}) async-start(f32[8,640,64]{1,2,0:T(8,128)} %copy.63), calls=%async_computation.3 | async-start | bytes 2621440 | tf_op jit(solution)/shard_map/all_to_all | solution.py:158
  165.4 16.7 %all-to-all-done.3 = f32[8,640,64]{1,2,0:T(8,128)S(1)} async-done(((f32[8,640,64]{1,2,0:T(8,128)}), f32[8,640,64]{1,2,0:T(8,128)S(1)}, u32[]{:S(2)}, u32[]{:S(2)}) %all-to-all-start.3) | async-done | bytes 1310752 | tf_op jit(solution)/shard_map/all_to_all | solution.py:158
  185.4 2.2 %copy.74 = bf16[4,10,1,8,9,16]{5,3,4,1,0,2:T(8,128)(2,1)S(1)} copy(bf16[4,10,1,8,9,16]{4,3,5,1,0,2:T(8,128)(2,1)S(1)} %reshape.188) | data formatting | bytes 184320 | tf_op jit(solution)/shard_map/conv_general_dilated | solution.py:187
  187.6 1.5 add_convert_fusion
  189.5 1.4 copy.76
  192.6 3.3 %all-to-all-start.4 = ((f32[8,2,512]{2,1,0:T(2,128)}), f32[8,2,512]{2,1,0:T(2,128)S(1)}, u32[]{:S(2)}, u32[]{:S(2)}) async-start(f32[8,2,512]{2,1,0:T(2,128)} %reshape.185), calls=%async_computation.4 | async-start | bytes 65536 | tf_op jit(solution)/shard_map/all_to_all | solution.py:208
  196.1 1.3 copy.79
  197.3 8.7 %all-to-all-done.4 = f32[8,2,512]{2,1,0:T(2,128)S(1)} async-done(((f32[8,2,512]{2,1,0:T(2,128)}), f32[8,2,512]{2,1,0:T(2,128)S(1)}, u32[]{:S(2)}, u32[]{:S(2)}) %all-to-all-start.4) | async-done | bytes 32800 | tf_op jit(solution)/shard_map/all_to_all | solution.py:208
  (118 shorter events, 37.1 us)
Async XLA Ops:
  0.6 187.0 %copy-start = (bf16[432,512]{1,0:T(8,128)(2,1)S(1)}, bf16[432,512]{1,0:T(8,128)(2,1)}, u32[]{:S(2)}) copy-start(bf16[432,512]{1,0:T(8,128)(2,1)} %param.21) | copy-start | bytes 1327108
  3.5 51.3 %all-to-all-start = ((bf16[8,3,256,128]{3,2,1,0:T(8,128)(2,1)}), bf16[8,3,256,128]{3,2,1,0:T(8,128)(2,1)S(1)}, u32[]{:S(2)}, u32[]{:S(2)}) async-start(bf16[8,3,256,128]{3,2,1,0:T(8,128)(2,1)} %shard_map.122), calls=%async_computation | async-start | bytes 3145728 | tf_op jit(solution)/shard_map/all_to_all | solution.py:144
  15.4 2.8 %copy-start.6 = (pred[8,20,32]{2,0,1:T(8,128)(4,1)S(1)}, pred[8,20,32]{2,0,1:T(8,128)(4,1)}, u32[]{:S(2)}) copy-start(pred[8,20,32]{2,0,1:T(8,128)(4,1)} %constant.88.clone) | copy-start | bytes 15364
  15.4 2.8 %copy-start.10 = (s32[32]{0:T(128)S(1)}, s32[32]{0:T(128)}, u32[]{:S(2)}) copy-start(s32[32]{0:T(128)} %param.24) | copy-start | bytes 388
  15.4 3.3 %copy-start.7 = (s32[8,20]{0,1:T(8,128)S(1)}, s32[8,20]{0,1:T(8,128)}, u32[]{:S(2)}) copy-start(s32[8,20]{0,1:T(8,128)} %constant.89.clone) | copy-start | bytes 1924
  54.8 59.9 %all-to-all-start.1 = ((bf16[8,3,256,128]{3,2,1,0:T(8,128)(2,1)}), bf16[8,3,256,128]{3,2,1,0:T(8,128)(2,1)}, u32[]{:S(2)}, u32[]{:S(2)}) async-start(bf16[8,3,256,128]{3,2,1,0:T(8,128)(2,1)} %shard_map.123), calls=%async_computation.1 | async-start | bytes 3145728 | tf_op jit(solution)/shard_map/all_to_all | solution.py:144
  76.3 1.0 copy-start.3
  79.1 1.0 copy-start.3
  81.8 1.0 copy-start.3
  84.6 1.0 copy-start.3
  86.5 28.1 %copy-start.1 = (bf16[4,512,128]{2,1,0:T(8,128)(2,1)}, bf16[4,512,128]{2,1,0:T(8,128)(2,1)S(1)}, u32[]{:S(2)}) copy-start(bf16[4,512,128]{2,1,0:T(8,128)(2,1)S(1)} %get-tuple-element.83) | copy-start | bytes 1572868
  114.6 21.8 %all-to-all-start.2 = ((bf16[8,3,256,128]{3,2,1,0:T(8,128)(2,1)}), bf16[8,3,256,128]{3,2,1,0:T(8,128)(2,1)S(1)}, u32[]{:S(2)}, u32[]{:S(2)}) async-start(bf16[8,3,256,128]{3,2,1,0:T(8,128)(2,1)} %shard_map.124), calls=%async_computation.2 | async-start | bytes 3145728 | tf_op jit(solution)/shard_map/all_to_all | solution.py:144
  122.2 1.0 copy-start.4
  125.5 1.0 copy-start.4
  128.8 1.0 copy-start.4
  132.2 1.0 copy-start.4
  137.5 11.0 %copy-start.2 = (bf16[4,512,128]{2,1,0:T(8,128)(2,1)S(1)}, bf16[4,512,128]{2,1,0:T(8,128)(2,1)}, u32[]{:S(2)}) copy-start(bf16[4,512,128]{2,1,0:T(8,128)(2,1)} %copy-done.1) | copy-start | bytes 1572868
  138.3 1.0 copy-start.5
  141.1 1.0 copy-start.5
  143.8 1.0 copy-start.5
  146.6 1.0 copy-start.5
  154.6 10.7 %copy-start.8 = (f32[1,2,8,64]{3,2,1,0:T(8,128)S(1)}, f32[1,2,8,64]{3,2,1,0:T(8,128)}, u32[]{:S(2)}) copy-start(f32[1,2,8,64]{3,2,1,0:T(8,128)} %param.23) | copy-start | bytes 12292
  157.6 24.6 %all-to-all-start.3 = ((f32[8,640,64]{1,2,0:T(8,128)}), f32[8,640,64]{1,2,0:T(8,128)S(1)}, u32[]{:S(2)}, u32[]{:S(2)}) async-start(f32[8,640,64]{1,2,0:T(8,128)} %copy.63), calls=%async_computation.3 | async-start | bytes 2621440 | tf_op jit(solution)/shard_map/all_to_all | solution.py:158
  184.0 3.6 %copy-start.9 = (f32[512]{0:T(512)S(1)}, f32[512]{0:T(512)}, u32[]{:S(2)}) copy-start(f32[512]{0:T(512)} %param.22) | copy-start | bytes 6148
  184.0 3.6 %copy-start.12 = (pred[8,9]{0,1:T(8,128)(4,1)S(1)}, pred[8,9]{0,1:T(8,128)(4,1)}, u32[]{:S(2)}) copy-start(pred[8,9]{0,1:T(8,128)(4,1)} %constant.98) | copy-start | bytes 220
  189.5 2.4 %copy-start.11 = (s32[16]{0:T(128)S(1)}, s32[16]{0:T(128)}, u32[]{:S(2)}) copy-start(s32[16]{0:T(128)} %param.25) | copy-start | bytes 196
  192.6 13.4 %all-to-all-start.4 = ((f32[8,2,512]{2,1,0:T(2,128)}), f32[8,2,512]{2,1,0:T(2,128)S(1)}, u32[]{:S(2)}, u32[]{:S(2)}) async-start(f32[8,2,512]{2,1,0:T(2,128)} %reshape.185), calls=%async_computation.4 | async-start | bytes 65536 | tf_op jit(solution)/shard_map/all_to_all | solution.py:208

commit v8 on v7

--- a/solution.py
+++ b/solution.py
@@ -91,7 +91,7 @@
     )(queries, keys_in, values_in)
 
 
-def head_attention(query, key, value):
+def head_attention(query, key, value, proj_rows):
     length = query.shape[0]
     score_scale = 1.0 / math.sqrt(query.shape[1])
     query_blocks = query.reshape(length // QUERY_BLOCK, QUERY_BLOCK, query.shape[1])
@@ -101,9 +101,10 @@
         expo = jnp.exp(scores - jnp.max(scores, axis=-1, keepdims=True))
         totals = jnp.sum(expo, axis=-1, keepdims=True)
         mixed = jnp.dot(expo.astype(jnp.bfloat16), value, preferred_element_type=jnp.float32)
-        return (mixed / totals).astype(jnp.bfloat16)
-
-    return lax.map(one_block, query_blocks).reshape(length, query.shape[1])
+        head_out = (mixed / totals).astype(jnp.bfloat16)
+        return jnp.dot(head_out, proj_rows, preferred_element_type=jnp.float32)
+
+    return lax.map(one_block, query_blocks).reshape(length, proj_rows.shape[1])
 
 
 def window_columns(volume):
@@ -142,21 +143,20 @@
     for slot in range(heads_dev):
         stacked = slot_operand(queries, keys_in, values_in, slot, group_count)
         gathered = lax.all_to_all(stacked, "seq", split_axis=0, concat_axis=0, tiled=True)
-        head_out = head_attention(
-            *(gathered[:, part].reshape(seq_len, HD) for part in range(3))
+        proj_rows = lax.dynamic_slice_in_dim(latent_proj, (slot * group_count + my_index) * HD, HD, 0)
+        term = head_attention(
+            *(gathered[:, part].reshape(seq_len, HD) for part in range(3)), proj_rows
         )
-        proj_rows = lax.dynamic_slice_in_dim(latent_proj, (slot * group_count + my_index) * HD, HD, 0)
-        term = jnp.dot(head_out, proj_rows, preferred_element_type=jnp.float32)
         partial = term if partial is None else partial + term
 
     positions, halves = halo_tables(group_count)
     picks = jnp.sum(
         jnp.where(positions[..., None] == np.arange(4 * group_count), tile_block, 0), axis=-1
     )
-    half_pieces = partial.reshape(8 * group_count, quarter // 2, 4 * LC)
-    outgoing = half_pieces[picks * 2 + halves].reshape(group_count, -1, 4 * LC)
+    half_pieces = partial.reshape(8 * group_count, quarter // 4, 8 * LC)
+    outgoing = half_pieces[picks * 2 + halves].reshape(group_count, -1, 8 * LC)
     returned = lax.all_to_all(outgoing, "seq", split_axis=0, concat_axis=0, tiled=True)
-    tokens = jnp.sum(returned, axis=0).astype(jnp.bfloat16)
+    tokens = jnp.sum(returned, axis=0).reshape(-1, 4 * LC).astype(jnp.bfloat16)
     band_row = my_index % TR
     upper_band = band_row == 0
     has_earlier = my_index >= TR

time: 208 us -> 231 us (1.11)
  waiting for transfers between devices: 91.3 us -> 60.2 us
  matrix products: 27.6 us -> 53.2 us
  local copies, waits for them, and re-layouts: 22.4 us -> 42.3 us
  starting transfers between devices: 43.5 us -> 51.4 us
    all_to_all x3, waiting for transfers between devices: 65.8 us -> 34.7 us  [local(): lax.all_to_all(stacked, 'seq', split_axis=0, concat_axis=0, tiled=True)]
    dot_general x15 -> x12, matrix products: 16.6 us -> 42.1 us  [one_block(): return jnp.dot(head_out, proj_rows, preferred_element_type=jnp.float32)]
    while x24 -> x32, local copies, waits for them, and re-layouts: 2.69 us -> 23.2 us
    all_to_all x3, starting transfers between devices: 32.4 us -> 38.5 us  [local(): lax.all_to_all(stacked, 'seq', split_axis=0, concat_axis=0, tiled=True)]
    reshape x1 -> x0, local copies, waits for them, and re-layouts: 2.95 us -> none  [local(): outgoing = half_pieces[picks * 2 + halves].reshape(group_count, -1, 4 * LC)]
  transfers between devices with their start and end apart: 5 -> 5, of which waited for: 5 -> 3; matrix products, arithmetic and copies ran while one was open for 14% -> 21% of each run, Pallas kernels for 3% -> 2%
where the time goes in v8:
time: 231 us; the launch traced here: 230 us
  waiting for transfers between devices  60.2 us (26%)
  matrix products  53.2 us (23%)
  starting transfers between devices  51.4 us (22%)
  local copies, waits for them, and re-layouts  42.3 us (18%)
  other arithmetic  13.4 us (6%)
  Pallas kernels  8.55 us (4%)
    dot_general x12, matrix products, one_block(): return jnp.dot(head_out, proj_rows, preferred_element_type=jnp.float32)  42.1 us
    all_to_all x3, starting transfers between devices, local(): lax.all_to_all(stacked, 'seq', split_axis=0, concat_axis=0, tiled=True)  38.5 us
    all_to_all x3, waiting for transfers between devices, local(): lax.all_to_all(stacked, 'seq', split_axis=0, concat_axis=0, tiled=True)  34.7 us
    while x32, local copies, waits for them, and re-layouts  23.2 us
    all_to_all x1, waiting for transfers between devices, local(): lax.all_to_all(outgoing, 'seq', split_axis=0, concat_axis=0, tiled=True)  16.8 us
    reduce_sum x12, other arithmetic, one_block(): totals = jnp.sum(expo, axis=-1, keepdims=True)  9.78 us
    all_to_all x1, starting transfers between devices, local(): lax.all_to_all(outgoing, 'seq', split_axis=0, concat_axis=0, tiled=True)  9.61 us
    dot_general x12, matrix products, one_block(): jnp.dot(query_part, key.T, preferred_element_type=jnp.float32) * score_scale  9.45 us
  transfers between devices with their start and end apart: 5, of which 3 were waited for; matrix products, arithmetic and copies ran while one was open for 21% of the time, Pallas kernels for 2%

profile of v8, /device:TPU:80, one launch (start us, length us, event | category | flops | bytes accessed | tf_op | source)
XLA Modules:
  0.0 230.4 jit_solution(18160536243847280346)
XLA Ops:
  0.6 2.9 %shard_map.123 = bf16[8,3,256,128]{3,2,1,0:T(8,128)(2,1)} custom-call(bf16[256,3072]{1,0:T(8,128)(2,1)} %q_ref.5, bf16[256,3072]{1,0:T(8,128)(2,1)} %k_ref.5, bf16[256,3072]{1,0:T(8,128)(2,1)} %v_ref.5), custom_call_target="tpu_custom_call" | custom-call | tf_op jit(solution)/shard_map/pallas_call | solution.py:85
  3.5 9.1 %all-to-all-start.1 = ((bf16[8,3,256,128]{3,2,1,0:T(8,128)(2,1)}), bf16[8,3,256,128]{3,2,1,0:T(8,128)(2,1)S(1)}, u32[]{:S(2)}, u32[]{:S(2)}) async-start(bf16[8,3,256,128]{3,2,1,0:T(8,128)(2,1)} %shard_map.123), calls=%async_computation.1 | async-start | bytes 3145728 | tf_op jit(solution)/shard_map/all_to_all | solution.py:145
  12.6 2.8 %shard_map.122 = bf16[8,3,256,128]{3,2,1,0:T(8,128)(2,1)} custom-call(bf16[256,3072]{1,0:T(8,128)(2,1)} %q_ref.5, bf16[256,3072]{1,0:T(8,128)(2,1)} %k_ref.5, bf16[256,3072]{1,0:T(8,128)(2,1)} %v_ref.5), custom_call_target="tpu_custom_call" | custom-call | tf_op jit(solution)/shard_map/pallas_call | solution.py:85
  15.5 2.9 %shard_map.124 = bf16[8,3,256,128]{3,2,1,0:T(8,128)(2,1)} custom-call(bf16[256,3072]{1,0:T(8,128)(2,1)} %q_ref.5, bf16[256,3072]{1,0:T(8,128)(2,1)} %k_ref.5, bf16[256,3072]{1,0:T(8,128)(2,1)} %v_ref.5), custom_call_target="tpu_custom_call" | custom-call | tf_op jit(solution)/shard_map/pallas_call | solution.py:85
  20.1 34.7 %all-to-all-done.1 = bf16[8,3,256,128]{3,2,1,0:T(8,128)(2,1)S(1)} async-done(((bf16[8,3,256,128]{3,2,1,0:T(8,128)(2,1)}), bf16[8,3,256,128]{3,2,1,0:T(8,128)(2,1)S(1)}, u32[]{:S(2)}, u32[]{:S(2)}) %all-to-all-start.1) | async-done | bytes 1572896 | tf_op jit(solution)/shard_map/all_to_all | solution.py:145
  54.8 19.7 %all-to-all-start = ((bf16[8,3,256,128]{3,2,1,0:T(8,128)(2,1)}), bf16[8,3,256,128]{3,2,1,0:T(8,128)(2,1)}, u32[]{:S(2)}, u32[]{:S(2)}) async-start(bf16[8,3,256,128]{3,2,1,0:T(8,128)(2,1)} %shard_map.122), calls=%async_computation | async-start | bytes 3145728 | tf_op jit(solution)/shard_map/all_to_all | solution.py:145
  75.5 27.2 %while.31 = (s32[]{:T(128)}, f32[4,512,64]{1,2,0:T(8,128)S(1)}, bf16[4,512,128]{2,1,0:T(8,128)(2,1)S(1)}, bf16[2048,128]{1,0:T(8,128)(2,1)S(1)}, bf16[2048,128]{...) while((s32[]{:T(128)}, f32[4,512,64]{1,2,0:T(8,128)S(1)}, bf16[4,512,128]{2,1,0:T(8,128)(2,1)S(1)}, ...), condition=%wide.region_7.8_spmd, body=%wide.region_4.7_spmd.sunk | while | flops 553778176 | bytes 32811148 | solution.py:107
  76.3 1.9 copy-done.1
  79.1 3.2 %fusion.151 = f32[4,512,64]{1,2,0:T(8,128)S(1)} fusion(f32[4,512,64]{1,2,0:T(8,128)S(1)} %get-tuple-element.346, s32[]{:T(128)} %get-tuple-element.345, bf16[128,64]{1,0:T(8,128)(2,1)S(1)} %get-tuple-element.357, bf16[2048,128]{1,0:T(8,128)(2,1)S(1)} %copy-done.8, f32[512,2048]{1,0:T(8,128)} %copy-done.1, f32[512]{0:T(512)S(1)} %get-tuple-element.287, ...), kind=kOutput, calls=%fused_computation.30.clone.1 | convolution fusion | flops 280100864 | bytes 4886532 | tf_op jit(solution)/shard_map/while/body/eval_jaxpr/dot_general | solution.py:105
  83.1 1.9 copy-done.1
  85.9 3.2 %fusion.151 = f32[4,512,64]{1,2,0:T(8,128)S(1)} fusion(f32[4,512,64]{1,2,0:T(8,128)S(1)} %get-tuple-element.346, s32[]{:T(128)} %get-tuple-element.345, bf16[128,64]{1,0:T(8,128)(2,1)S(1)} %get-tuple-element.357, bf16[2048,128]{1,0:T(8,128)(2,1)S(1)} %copy-done.8, f32[512,2048]{1,0:T(8,128)} %copy-done.1, f32[512]{0:T(512)S(1)} %get-tuple-element.287, ...), kind=kOutput, calls=%fused_computation.30.clone.1 | convolution fusion | flops 280100864 | bytes 4886532 | tf_op jit(solution)/shard_map/while/body/eval_jaxpr/dot_general | solution.py:105
  89.9 1.9 copy-done.1
  92.7 3.2 %fusion.151 = f32[4,512,64]{1,2,0:T(8,128)S(1)} fusion(f32[4,512,64]{1,2,0:T(8,128)S(1)} %get-tuple-element.346, s32[]{:T(128)} %get-tuple-element.345, bf16[128,64]{1,0:T(8,128)(2,1)S(1)} %get-tuple-element.357, bf16[2048,128]{1,0:T(8,128)(2,1)S(1)} %copy-done.8, f32[512,2048]{1,0:T(8,128)} %copy-done.1, f32[512]{0:T(512)S(1)} %get-tuple-element.287, ...), kind=kOutput, calls=%fused_computation.30.clone.1 | convolution fusion | flops 280100864 | bytes 4886532 | tf_op jit(solution)/shard_map/while/body/eval_jaxpr/dot_general | solution.py:105
  96.7 1.9 copy-done.1
  99.5 3.2 %fusion.151 = f32[4,512,64]{1,2,0:T(8,128)S(1)} fusion(f32[4,512,64]{1,2,0:T(8,128)S(1)} %get-tuple-element.346, s32[]{:T(128)} %get-tuple-element.345, bf16[128,64]{1,0:T(8,128)(2,1)S(1)} %get-tuple-element.357, bf16[2048,128]{1,0:T(8,128)(2,1)S(1)} %copy-done.8, f32[512,2048]{1,0:T(8,128)} %copy-done.1, f32[512]{0:T(512)S(1)} %get-tuple-element.287, ...), kind=kOutput, calls=%fused_computation.30.clone.1 | convolution fusion | flops 280100864 | bytes 4886532 | tf_op jit(solution)/shard_map/while/body/eval_jaxpr/dot_general | solution.py:105
  103.6 9.6 %all-to-all-start.2 = ((bf16[8,3,256,128]{3,2,1,0:T(8,128)(2,1)}), bf16[8,3,256,128]{3,2,1,0:T(8,128)(2,1)S(1)}, u32[]{:S(2)}, u32[]{:S(2)}) async-start(bf16[8,3,256,128]{3,2,1,0:T(8,128)(2,1)} %shard_map.124), calls=%async_computation.2 | async-start | bytes 3145728 | tf_op jit(solution)/shard_map/all_to_all | solution.py:145
  113.2 2.3 fusion.109
  116.3 30.2 %while.30 = (s32[]{:T(128)}, f32[4,512,64]{1,2,0:T(8,128)}, bf16[4,512,128]{2,1,0:T(8,128)(2,1)S(1)}, bf16[2048,128]{1,0:T(8,128)(2,1)S(1)}, bf16[2048,128]{1,0:...) while((s32[]{:T(128)}, f32[4,512,64]{1,2,0:T(8,128)}, bf16[4,512,128]{2,1,0:T(8,128)(2,1)S(1)}, ...), condition=%wide.region_3.4_spmd, body=%wide.region_0.3_spmd.sunk | while | flops 553778176 | bytes 30698092 | solution.py:107
  119.9 4.0 %fusion.145 = f32[4,512,64]{1,2,0:T(8,128)} fusion(f32[4,512,64]{1,2,0:T(8,128)} %get-tuple-element.325, s32[]{:T(128)} %get-tuple-element.324, bf16[128,64]{1,0:T(8,128)(2,1)S(1)} %get-tuple-element.336, bf16[2048,128]{1,0:T(8,128)(2,1)} %get-tuple-element.335, f32[512,2048]{1,0:T(8,128)} %copy-done.2, f32[512]{0:T(512)S(1)} %get-tuple-element.279, ...), kind=kOutput, calls=%fused_computation.12.clone.1 | convolution fusion | flops 280100864 | bytes 4870656 | tf_op jit(solution)/shard_map/while/body/eval_jaxpr/dot_general | solution.py:105
  127.4 4.0 %fusion.145 = f32[4,512,64]{1,2,0:T(8,128)} fusion(f32[4,512,64]{1,2,0:T(8,128)} %get-tuple-element.325, s32[]{:T(128)} %get-tuple-element.324, bf16[128,64]{1,0:T(8,128)(2,1)S(1)} %get-tuple-element.336, bf16[2048,128]{1,0:T(8,128)(2,1)} %get-tuple-element.335, f32[512,2048]{1,0:T(8,128)} %copy-done.2, f32[512]{0:T(512)S(1)} %get-tuple-element.279, ...), kind=kOutput, calls=%fused_computation.12.clone.1 | convolution fusion | flops 280100864 | bytes 4870656 | tf_op jit(solution)/shard_map/while/body/eval_jaxpr/dot_general | solution.py:105
  134.9 4.0 %fusion.145 = f32[4,512,64]{1,2,0:T(8,128)} fusion(f32[4,512,64]{1,2,0:T(8,128)} %get-tuple-element.325, s32[]{:T(128)} %get-tuple-element.324, bf16[128,64]{1,0:T(8,128)(2,1)S(1)} %get-tuple-element.336, bf16[2048,128]{1,0:T(8,128)(2,1)} %get-tuple-element.335, f32[512,2048]{1,0:T(8,128)} %copy-done.2, f32[512]{0:T(512)S(1)} %get-tuple-element.279, ...), kind=kOutput, calls=%fused_computation.12.clone.1 | convolution fusion | flops 280100864 | bytes 4870656 | tf_op jit(solution)/shard_map/while/body/eval_jaxpr/dot_general | solution.py:105
  142.5 4.0 %fusion.145 = f32[4,512,64]{1,2,0:T(8,128)} fusion(f32[4,512,64]{1,2,0:T(8,128)} %get-tuple-element.325, s32[]{:T(128)} %get-tuple-element.324, bf16[128,64]{1,0:T(8,128)(2,1)S(1)} %get-tuple-element.336, bf16[2048,128]{1,0:T(8,128)(2,1)} %get-tuple-element.335, f32[512,2048]{1,0:T(8,128)} %copy-done.2, f32[512]{0:T(512)S(1)} %get-tuple-element.279, ...), kind=kOutput, calls=%fused_computation.12.clone.1 | convolution fusion | flops 280100864 | bytes 4870656 | tf_op jit(solution)/shard_map/while/body/eval_jaxpr/dot_general | solution.py:105
  147.5 27.6 %while.32 = (s32[]{:T(128)}, f32[4,512,64]{1,2,0:T(8,128)S(1)}, bf16[4,512,128]{2,1,0:T(8,128)(2,1)S(1)}, bf16[2048,128]{1,0:T(8,128)(2,1)S(1)}, bf16[2048,128]{...) while((s32[]{:T(128)}, f32[4,512,64]{1,2,0:T(8,128)S(1)}, bf16[4,512,128]{2,1,0:T(8,128)(2,1)S(1)}, ...), condition=%wide.region_11.12_spmd, body=%wide.region_8.11_spmd.sunk | while | flops 553778176 | bytes 30713968 | solution.py:107
  151.0 3.3 %fusion.157 = f32[4,512,64]{1,2,0:T(8,128)S(1)} fusion(f32[4,512,64]{1,2,0:T(8,128)S(1)} %get-tuple-element.304, s32[]{:T(128)} %get-tuple-element.303, bf16[128,64]{1,0:T(8,128)(2,1)S(1)} %get-tuple-element.315, bf16[2048,128]{1,0:T(8,128)(2,1)} %get-tuple-element.314, f32[512,2048]{1,0:T(8,128)} %copy-done.3, f32[512]{0:T(512)S(1)} %get-tuple-element.295, ...), kind=kOutput, calls=%fused_computation.48.clone.1 | convolution fusion | flops 280100864 | bytes 4886532 | tf_op jit(solution)/shard_map/while/body/eval_jaxpr/dot_general | solution.py:105
  157.9 3.3 %fusion.157 = f32[4,512,64]{1,2,0:T(8,128)S(1)} fusion(f32[4,512,64]{1,2,0:T(8,128)S(1)} %get-tuple-element.304, s32[]{:T(128)} %get-tuple-element.303, bf16[128,64]{1,0:T(8,128)(2,1)S(1)} %get-tuple-element.315, bf16[2048,128]{1,0:T(8,128)(2,1)} %get-tuple-element.314, f32[512,2048]{1,0:T(8,128)} %copy-done.3, f32[512]{0:T(512)S(1)} %get-tuple-element.295, ...), kind=kOutput, calls=%fused_computation.48.clone.1 | convolution fusion | flops 280100864 | bytes 4886532 | tf_op jit(solution)/shard_map/while/body/eval_jaxpr/dot_general | solution.py:105
  164.8 3.3 %fusion.157 = f32[4,512,64]{1,2,0:T(8,128)S(1)} fusion(f32[4,512,64]{1,2,0:T(8,128)S(1)} %get-tuple-element.304, s32[]{:T(128)} %get-tuple-element.303, bf16[128,64]{1,0:T(8,128)(2,1)S(1)} %get-tuple-element.315, bf16[2048,128]{1,0:T(8,128)(2,1)} %get-tuple-element.314, f32[512,2048]{1,0:T(8,128)} %copy-done.3, f32[512]{0:T(512)S(1)} %get-tuple-element.295, ...), kind=kOutput, calls=%fused_computation.48.clone.1 | convolution fusion | flops 280100864 | bytes 4886532 | tf_op jit(solution)/shard_map/while/body/eval_jaxpr/dot_general | solution.py:105
  171.7 3.3 %fusion.157 = f32[4,512,64]{1,2,0:T(8,128)S(1)} fusion(f32[4,512,64]{1,2,0:T(8,128)S(1)} %get-tuple-element.304, s32[]{:T(128)} %get-tuple-element.303, bf16[128,64]{1,0:T(8,128)(2,1)S(1)} %get-tuple-element.315, bf16[2048,128]{1,0:T(8,128)(2,1)} %get-tuple-element.314, f32[512,2048]{1,0:T(8,128)} %copy-done.3, f32[512]{0:T(512)S(1)} %get-tuple-element.295, ...), kind=kOutput, calls=%fused_computation.48.clone.1 | convolution fusion | flops 280100864 | bytes 4886532 | tf_op jit(solution)/shard_map/while/body/eval_jaxpr/dot_general | solution.py:105
  179.5 9.6 %all-to-all-start.3 = ((f32[8,320,128]{2,1,0:T(8,128)}), f32[8,320,128]{2,1,0:T(8,128)S(1)}, u32[]{:S(2)}, u32[]{:S(2)}) async-start(f32[8,320,128]{2,1,0:T(8,128)} %bitcast.15), calls=%async_computation.3 | async-start | bytes 2621440 | tf_op jit(solution)/shard_map/all_to_all | solution.py:158
  189.2 16.8 %all-to-all-done.3 = f32[8,320,128]{2,1,0:T(8,128)S(1)} async-done(((f32[8,320,128]{2,1,0:T(8,128)}), f32[8,320,128]{2,1,0:T(8,128)S(1)}, u32[]{:S(2)}, u32[]{:S(2)}) %all-to-all-start.3) | async-done | bytes 1310752 | tf_op jit(solution)/shard_map/all_to_all | solution.py:158
  209.1 2.2 copy.75
  216.4 3.3 %all-to-all-start.4 = ((f32[8,2,512]{2,1,0:T(2,128)}), f32[8,2,512]{2,1,0:T(2,128)S(1)}, u32[]{:S(2)}, u32[]{:S(2)}) async-start(f32[8,2,512]{2,1,0:T(2,128)} %reshape.188), calls=%async_computation.4 | async-start | bytes 65536 | tf_op jit(solution)/shard_map/all_to_all | solution.py:208
  221.1 8.7 %all-to-all-done.4 = f32[8,2,512]{2,1,0:T(2,128)S(1)} async-done(((f32[8,2,512]{2,1,0:T(2,128)}), f32[8,2,512]{2,1,0:T(2,128)S(1)}, u32[]{:S(2)}, u32[]{:S(2)}) %all-to-all-start.4) | async-done | bytes 32800 | tf_op jit(solution)/shard_map/all_to_all | solution.py:208
  (129 shorter events, 54.6 us)
Async XLA Ops:
  0.6 210.7 %copy-start = (bf16[432,512]{1,0:T(8,128)(2,1)S(1)}, bf16[432,512]{1,0:T(8,128)(2,1)}, u32[]{:S(2)}) copy-start(bf16[432,512]{1,0:T(8,128)(2,1)} %param.21) | copy-start | bytes 1327108
  3.5 51.3 %all-to-all-start.1 = ((bf16[8,3,256,128]{3,2,1,0:T(8,128)(2,1)}), bf16[8,3,256,128]{3,2,1,0:T(8,128)(2,1)S(1)}, u32[]{:S(2)}, u32[]{:S(2)}) async-start(bf16[8,3,256,128]{3,2,1,0:T(8,128)(2,1)} %shard_map.123), calls=%async_computation.1 | async-start | bytes 3145728 | tf_op jit(solution)/shard_map/all_to_all | solution.py:145
  15.4 4.0 %copy-start.9 = (pred[8,20,32]{2,0,1:T(8,128)(4,1)S(1)}, pred[8,20,32]{2,0,1:T(8,128)(4,1)}, u32[]{:S(2)}) copy-start(pred[8,20,32]{2,0,1:T(8,128)(4,1)} %constant.88.clone) | copy-start | bytes 15364
  15.5 4.0 %copy-start.13 = (s32[32]{0:T(128)S(1)}, s32[32]{0:T(128)}, u32[]{:S(2)}) copy-start(s32[32]{0:T(128)} %param.24) | copy-start | bytes 388
  15.5 4.4 %copy-start.10 = (s32[8,20]{0,1:T(8,128)S(1)}, s32[8,20]{0,1:T(8,128)}, u32[]{:S(2)}) copy-start(s32[8,20]{0,1:T(8,128)} %constant.89.clone) | copy-start | bytes 1924
  54.8 47.9 %all-to-all-start = ((bf16[8,3,256,128]{3,2,1,0:T(8,128)(2,1)}), bf16[8,3,256,128]{3,2,1,0:T(8,128)(2,1)}, u32[]{:S(2)}, u32[]{:S(2)}) async-start(bf16[8,3,256,128]{3,2,1,0:T(8,128)(2,1)} %shard_map.122), calls=%async_computation | async-start | bytes 3145728 | tf_op jit(solution)/shard_map/all_to_all | solution.py:145
  75.5 3.6 %copy-start.8 = (bf16[2048,128]{1,0:T(8,128)(2,1)S(1)}, bf16[2048,128]{1,0:T(8,128)(2,1)}, u32[]{:S(2)}) copy-start(bf16[2048,128]{1,0:T(8,128)(2,1)} %get-tuple-element.356) | copy-start | bytes 1572868 | tf_op jit(solution)/shard_map/while
  76.3 1.9 copy-start.1
  82.3 3.6 %copy-start.8 = (bf16[2048,128]{1,0:T(8,128)(2,1)S(1)}, bf16[2048,128]{1,0:T(8,128)(2,1)}, u32[]{:S(2)}) copy-start(bf16[2048,128]{1,0:T(8,128)(2,1)} %get-tuple-element.356) | copy-start | bytes 1572868 | tf_op jit(solution)/shard_map/while
  83.1 1.9 copy-start.1
  89.1 3.6 %copy-start.8 = (bf16[2048,128]{1,0:T(8,128)(2,1)S(1)}, bf16[2048,128]{1,0:T(8,128)(2,1)}, u32[]{:S(2)}) copy-start(bf16[2048,128]{1,0:T(8,128)(2,1)} %get-tuple-element.356) | copy-start | bytes 1572868 | tf_op jit(solution)/shard_map/while
  89.9 1.9 copy-start.1
  95.9 3.6 %copy-start.8 = (bf16[2048,128]{1,0:T(8,128)(2,1)S(1)}, bf16[2048,128]{1,0:T(8,128)(2,1)}, u32[]{:S(2)}) copy-start(bf16[2048,128]{1,0:T(8,128)(2,1)} %get-tuple-element.356) | copy-start | bytes 1572868 | tf_op jit(solution)/shard_map/while
  96.7 1.9 copy-start.1
  102.7 0.8 copy-start.4
  103.6 42.9 %all-to-all-start.2 = ((bf16[8,3,256,128]{3,2,1,0:T(8,128)(2,1)}), bf16[8,3,256,128]{3,2,1,0:T(8,128)(2,1)S(1)}, u32[]{:S(2)}, u32[]{:S(2)}) async-start(bf16[8,3,256,128]{3,2,1,0:T(8,128)(2,1)} %shard_map.124), calls=%async_computation.2 | async-start | bytes 3145728 | tf_op jit(solution)/shard_map/all_to_all | solution.py:145
  117.1 1.9 copy-start.2
  124.6 1.9 copy-start.2
  132.2 1.9 copy-start.2
  139.7 1.9 copy-start.2
  147.5 28.4 %copy-start.5 = (f32[4,512,64]{1,2,0:T(8,128)S(1)}, f32[4,512,64]{1,2,0:T(8,128)}, u32[]{:S(2)}) copy-start(f32[4,512,64]{1,2,0:T(8,128)} %copy-done.4) | copy-start | bytes 1572868
  147.5 28.4 %copy-start.6 = (f32[4,512,64]{1,2,0:T(8,128)S(1)}, f32[4,512,64]{1,2,0:T(8,128)}, u32[]{:S(2)}) copy-start(f32[4,512,64]{1,2,0:T(8,128)} %get-tuple-element.98) | copy-start | bytes 1572868
  148.3 1.9 copy-start.3
  155.2 1.9 copy-start.3
  162.1 1.9 copy-start.3
  169.0 1.9 copy-start.3
  177.0 12.1 %copy-start.11 = (f32[1,2,8,64]{3,2,1,0:T(8,128)S(1)}, f32[1,2,8,64]{3,2,1,0:T(8,128)}, u32[]{:S(2)}) copy-start(f32[1,2,8,64]{3,2,1,0:T(8,128)} %param.23) | copy-start | bytes 12292
  179.5 26.5 %all-to-all-start.3 = ((f32[8,320,128]{2,1,0:T(8,128)}), f32[8,320,128]{2,1,0:T(8,128)S(1)}, u32[]{:S(2)}, u32[]{:S(2)}) async-start(f32[8,320,128]{2,1,0:T(8,128)} %bitcast.15), calls=%async_computation.3 | async-start | bytes 2621440 | tf_op jit(solution)/shard_map/all_to_all | solution.py:158
  189.2 22.1 %copy-start.12 = (f32[512]{0:T(512)S(1)}, f32[512]{0:T(512)}, u32[]{:S(2)}) copy-start(f32[512]{0:T(512)} %param.22) | copy-start | bytes 6148
  189.2 22.1 %copy-start.15 = (pred[8,9]{0,1:T(8,128)(4,1)S(1)}, pred[8,9]{0,1:T(8,128)(4,1)}, u32[]{:S(2)}) copy-start(pred[8,9]{0,1:T(8,128)(4,1)} %constant.98) | copy-start | bytes 220
  213.2 2.4 %copy-start.14 = (s32[16]{0:T(128)S(1)}, s32[16]{0:T(128)}, u32[]{:S(2)}) copy-start(s32[16]{0:T(128)} %param.25) | copy-start | bytes 196
  216.4 13.4 %all-to-all-start.4 = ((f32[8,2,512]{2,1,0:T(2,128)}), f32[8,2,512]{2,1,0:T(2,128)S(1)}, u32[]{:S(2)}, u32[]{:S(2)}) async-start(f32[8,2,512]{2,1,0:T(2,128)} %reshape.188), calls=%async_computation.4 | async-start | bytes 65536 | tf_op jit(solution)/shard_map/all_to_all | solution.py:208
  (1 other events, 0.8 us)

commit v9 on v7

--- a/solution.py
+++ b/solution.py
@@ -153,10 +153,10 @@
     picks = jnp.sum(
         jnp.where(positions[..., None] == np.arange(4 * group_count), tile_block, 0), axis=-1
     )
-    half_pieces = partial.reshape(8 * group_count, quarter // 2, 4 * LC)
-    outgoing = half_pieces[picks * 2 + halves].reshape(group_count, -1, 4 * LC)
+    half_pieces = partial.reshape(8 * group_count, quarter // 4, 8 * LC)
+    outgoing = half_pieces[picks * 2 + halves].reshape(group_count, -1, 8 * LC)
     returned = lax.all_to_all(outgoing, "seq", split_axis=0, concat_axis=0, tiled=True)
-    tokens = jnp.sum(returned, axis=0).astype(jnp.bfloat16)
+    tokens = jnp.sum(returned, axis=0).reshape(-1, 4 * LC).astype(jnp.bfloat16)
     band_row = my_index % TR
     upper_band = band_row == 0
     has_earlier = my_index >= TR

time: 208 us -> 205 us (0.986)
  local copies, waits for them, and re-layouts: 22.4 us -> 19.1 us
    reshape x1, local copies, waits for them, and re-layouts: 2.95 us -> 0.21 us  [local(): half_pieces = partial.reshape(8 * group_count, quarter // 4, 8 * LC)]
where the time goes in v9:
time: 205 us; the launch traced here: 203 us
  waiting for transfers between devices  91.3 us (45%)
  starting transfers between devices  43.5 us (21%)
  matrix products  27.6 us (13%)
  local copies, waits for them, and re-layouts  19.1 us (9%)
  other arithmetic  12.3 us (6%)
  Pallas kernels  8.43 us (4%)
    all_to_all x3, waiting for transfers between devices, local(): lax.all_to_all(stacked, 'seq', split_axis=0, concat_axis=0, tiled=True)  65.9 us
    all_to_all x3, starting transfers between devices, local(): lax.all_to_all(stacked, 'seq', split_axis=0, concat_axis=0, tiled=True)  32.4 us
    all_to_all x1, waiting for transfers between devices, local(): lax.all_to_all(outgoing, 'seq', split_axis=0, concat_axis=0, tiled=True)  16.7 us
    dot_general x12, matrix products, one_block(): jnp.dot(expo.astype(jnp.bfloat16), value, preferred_element_type=jnp.floa...  13.2 us
    reduce_sum x12, other arithmetic, one_block(): totals = jnp.sum(expo, axis=-1, keepdims=True)  9.81 us
    dot_general x12, matrix products, one_block(): jnp.dot(query_part, key.T, preferred_element_type=jnp.float32) * score_scale  9.45 us
    all_to_all x1, waiting for transfers between devices, local(): lax.all_to_all(by_owner.reshape(group_count, BPD, CO), 'seq', split_axis=...  8.73 us
    pallas_call x3, Pallas kernels, slot_operand(): pl.pallas_call(kernel, grid=(1,), out_shape=jax.ShapeDtypeStruct((group_c...  8.43 us
  transfers between devices with their start and end apart: 5, of which 5 were waited for; matrix products, arithmetic and copies ran while one was open for 14% of the time, Pallas kernels for 3%

profile of v9, /device:TPU:80, one launch (start us, length us, event | category | flops | bytes accessed | tf_op | source)
XLA Modules:
  0.0 203.3 jit_solution(12798871067443323218)
XLA Ops:
  0.6 2.8 %shard_map.122 = bf16[8,3,256,128]{3,2,1,0:T(8,128)(2,1)} custom-call(bf16[256,3072]{1,0:T(8,128)(2,1)} %q_ref.5, bf16[256,3072]{1,0:T(8,128)(2,1)} %k_ref.5, bf16[256,3072]{1,0:T(8,128)(2,1)} %v_ref.5), custom_call_target="tpu_custom_call" | custom-call | tf_op jit(solution)/shard_map/pallas_call | solution.py:85
  3.5 9.1 %all-to-all-start = ((bf16[8,3,256,128]{3,2,1,0:T(8,128)(2,1)}), bf16[8,3,256,128]{3,2,1,0:T(8,128)(2,1)S(1)}, u32[]{:S(2)}, u32[]{:S(2)}) async-start(bf16[8,3,256,128]{3,2,1,0:T(8,128)(2,1)} %shard_map.122), calls=%async_computation | async-start | bytes 3145728 | tf_op jit(solution)/shard_map/all_to_all | solution.py:144
  12.6 2.8 %shard_map.123 = bf16[8,3,256,128]{3,2,1,0:T(8,128)(2,1)} custom-call(bf16[256,3072]{1,0:T(8,128)(2,1)} %q_ref.5, bf16[256,3072]{1,0:T(8,128)(2,1)} %k_ref.5, bf16[256,3072]{1,0:T(8,128)(2,1)} %v_ref.5), custom_call_target="tpu_custom_call" | custom-call | tf_op jit(solution)/shard_map/pallas_call | solution.py:85
  15.4 2.8 %shard_map.124 = bf16[8,3,256,128]{3,2,1,0:T(8,128)(2,1)} custom-call(bf16[256,3072]{1,0:T(8,128)(2,1)} %q_ref.5, bf16[256,3072]{1,0:T(8,128)(2,1)} %k_ref.5, bf16[256,3072]{1,0:T(8,128)(2,1)} %v_ref.5), custom_call_target="tpu_custom_call" | custom-call | tf_op jit(solution)/shard_map/pallas_call | solution.py:85
  18.8 35.9 %all-to-all-done = bf16[8,3,256,128]{3,2,1,0:T(8,128)(2,1)S(1)} async-done(((bf16[8,3,256,128]{3,2,1,0:T(8,128)(2,1)}), bf16[8,3,256,128]{3,2,1,0:T(8,128)(2,1)S(1)}, u32[]{:S(2)}, u32[]{:S(2)}) %all-to-all-start) | async-done | bytes 1572896 | tf_op jit(solution)/shard_map/all_to_all | solution.py:144
  54.8 19.7 %all-to-all-start.1 = ((bf16[8,3,256,128]{3,2,1,0:T(8,128)(2,1)}), bf16[8,3,256,128]{3,2,1,0:T(8,128)(2,1)}, u32[]{:S(2)}, u32[]{:S(2)}) async-start(bf16[8,3,256,128]{3,2,1,0:T(8,128)(2,1)} %shard_map.123), calls=%async_computation.1 | async-start | bytes 3145728 | tf_op jit(solution)/shard_map/all_to_all | solution.py:144
  74.5 0.9 fusion.102
  75.5 11.0 %while.30 = (s32[]{:T(128)}, bf16[4,512,128]{2,1,0:T(8,128)(2,1)S(1)}, bf16[4,512,128]{2,1,0:T(8,128)(2,1)S(1)}, bf16[2048,128]{1,0:T(8,128)(2,1)S(1)}, bf16[2048,128]{1,0:T(8,128)(2,1)}, /*index=5*/s32[]{:T(128)}) while((s32[]{:T(128)}, bf16[4,512,128]{2,1,0:T(8,128)(2,1)S(1)}, bf16[4,512,128]{2,1,0:T(8,128)(2,1)S(1)}, ...), condition=%wide.region_3.4_spmd, body=%wide.region_0.3_spmd.sunk | while | flops 545389568 | bytes 16001129 | solution.py:106
  86.5 28.1 %all-to-all-done.1 = bf16[8,3,256,128]{3,2,1,0:T(8,128)(2,1)} async-done(((bf16[8,3,256,128]{3,2,1,0:T(8,128)(2,1)}), bf16[8,3,256,128]{3,2,1,0:T(8,128)(2,1)}, u32[]{:S(2)}, u32[]{:S(2)}) %all-to-all-start.1) | async-done | bytes 1572896 | tf_op jit(solution)/shard_map/all_to_all | solution.py:144
  114.6 3.6 %all-to-all-start.2 = ((bf16[8,3,256,128]{3,2,1,0:T(8,128)(2,1)}), bf16[8,3,256,128]{3,2,1,0:T(8,128)(2,1)S(1)}, u32[]{:S(2)}, u32[]{:S(2)}) async-start(bf16[8,3,256,128]{3,2,1,0:T(8,128)(2,1)} %shard_map.124), calls=%async_computation.2 | async-start | bytes 3145728 | tf_op jit(solution)/shard_map/all_to_all | solution.py:144
  118.2 2.3 %fusion.101 = (bf16[8,1,256,128]{3,2,1,0:T(8,128)(2,1)}, bf16[8,1,256,128]{3,2,1,0:T(8,128)(2,1)S(1)}, bf16[8,1,256,128]{3,2,1,0:T(8,128)(2,1)S(1)}) fusion(bf16[8,3,256,128]{3,2,1,0:T(8,128)(2,1)} %all-to-all-done.1), kind=kLoop, calls=%fused_computation.103 | loop fusion | bytes 3145728 | tf_op jit(solution)/shard_map/slice | solution.py:146
  121.4 13.3 %while.31 = (s32[]{:T(128)}, bf16[4,512,128]{2,1,0:T(8,128)(2,1)}, bf16[4,512,128]{2,1,0:T(8,128)(2,1)S(1)}, bf16[2048,128]{1,0:T(8,128)(2,1)S(1)}, bf16[2048,128]{1,0:T(8,128)(2,1)}, /*index=5*/s32[]{:T(128)}) while((s32[]{:T(128)}, bf16[4,512,128]{2,1,0:T(8,128)(2,1)}, bf16[4,512,128]{2,1,0:T(8,128)(2,1)S(1)}, ...), condition=%wide.region_7.8_spmd, body=%wide.region_4.7_spmd.sunk | while | flops 545389568 | bytes 16001637 | solution.py:106
  123.2 1.5 fusion.138
  126.6 1.5 fusion.138
  129.9 1.5 fusion.138
  133.2 1.5 fusion.138
  134.7 1.8 all-to-all-done.2
  136.5 0.9 fusion.100
  137.5 11.0 %while.32 = (s32[]{:T(128)}, bf16[4,512,128]{2,1,0:T(8,128)(2,1)S(1)}, bf16[4,512,128]{2,1,0:T(8,128)(2,1)S(1)}, bf16[2048,128]{1,0:T(8,128)(2,1)S(1)}, bf16[2048,128]{1,0:T(8,128)(2,1)}, /*index=5*/s32[]{:T(128)}) while((s32[]{:T(128)}, bf16[4,512,128]{2,1,0:T(8,128)(2,1)S(1)}, bf16[4,512,128]{2,1,0:T(8,128)(2,1)S(1)}, ...), condition=%wide.region_11.12_spmd, body=%wide.region_8.11_spmd.sunk | while | flops 545389568 | bytes 16001129 | solution.py:106
  142.1 0.9 fusion.143
  148.6 1.0 fusion.90
  149.6 1.3 convolution_add_fusion.1
  150.9 1.0 convolution_add_fusion
  152.5 1.9 gather_fusion
  154.4 7.7 %all-to-all-start.3 = ((f32[8,320,128]{2,1,0:T(8,128)}), f32[8,320,128]{2,1,0:T(8,128)S(1)}, u32[]{:S(2)}, u32[]{:S(2)}) async-start(f32[8,320,128]{2,1,0:T(8,128)} %bitcast.18), calls=%async_computation.3 | async-start | bytes 2621440 | tf_op jit(solution)/shard_map/all_to_all | solution.py:158
  162.2 16.7 %all-to-all-done.3 = f32[8,320,128]{2,1,0:T(8,128)S(1)} async-done(((f32[8,320,128]{2,1,0:T(8,128)}), f32[8,320,128]{2,1,0:T(8,128)S(1)}, u32[]{:S(2)}, u32[]{:S(2)}) %all-to-all-start.3) | async-done | bytes 1310752 | tf_op jit(solution)/shard_map/all_to_all | solution.py:158
  182.0 2.2 %copy.60 = bf16[4,10,1,8,9,16]{5,3,4,1,0,2:T(8,128)(2,1)S(1)} copy(bf16[4,10,1,8,9,16]{4,3,5,1,0,2:T(8,128)(2,1)S(1)} %reshape.198) | data formatting | bytes 184320 | tf_op jit(solution)/shard_map/conv_general_dilated | solution.py:187
  184.3 1.5 add_convert_fusion
  186.1 1.4 copy.62
  189.3 3.3 %all-to-all-start.4 = ((f32[8,2,512]{2,1,0:T(2,128)}), f32[8,2,512]{2,1,0:T(2,128)S(1)}, u32[]{:S(2)}, u32[]{:S(2)}) async-start(f32[8,2,512]{2,1,0:T(2,128)} %reshape.195), calls=%async_computation.4 | async-start | bytes 65536 | tf_op jit(solution)/shard_map/all_to_all | solution.py:208
  192.7 1.3 copy.65
  194.0 8.7 %all-to-all-done.4 = f32[8,2,512]{2,1,0:T(2,128)S(1)} async-done(((f32[8,2,512]{2,1,0:T(2,128)}), f32[8,2,512]{2,1,0:T(2,128)S(1)}, u32[]{:S(2)}, u32[]{:S(2)}) %all-to-all-start.4) | async-done | bytes 32800 | tf_op jit(solution)/shard_map/all_to_all | solution.py:208
  (115 shorter events, 36.3 us)
Async XLA Ops:
  0.6 183.6 %copy-start = (bf16[432,512]{1,0:T(8,128)(2,1)S(1)}, bf16[432,512]{1,0:T(8,128)(2,1)}, u32[]{:S(2)}) copy-start(bf16[432,512]{1,0:T(8,128)(2,1)} %param.21) | copy-start | bytes 1327108
  3.5 51.3 %all-to-all-start = ((bf16[8,3,256,128]{3,2,1,0:T(8,128)(2,1)}), bf16[8,3,256,128]{3,2,1,0:T(8,128)(2,1)S(1)}, u32[]{:S(2)}, u32[]{:S(2)}) async-start(bf16[8,3,256,128]{3,2,1,0:T(8,128)(2,1)} %shard_map.122), calls=%async_computation | async-start | bytes 3145728 | tf_op jit(solution)/shard_map/all_to_all | solution.py:144
  15.4 2.8 %copy-start.6 = (pred[8,20,32]{2,0,1:T(8,128)(4,1)S(1)}, pred[8,20,32]{2,0,1:T(8,128)(4,1)}, u32[]{:S(2)}) copy-start(pred[8,20,32]{2,0,1:T(8,128)(4,1)} %constant.88.clone) | copy-start | bytes 15364
  15.4 2.8 %copy-start.10 = (s32[32]{0:T(128)S(1)}, s32[32]{0:T(128)}, u32[]{:S(2)}) copy-start(s32[32]{0:T(128)} %param.24) | copy-start | bytes 388
  15.4 3.3 %copy-start.7 = (s32[8,20]{0,1:T(8,128)S(1)}, s32[8,20]{0,1:T(8,128)}, u32[]{:S(2)}) copy-start(s32[8,20]{0,1:T(8,128)} %constant.89.clone) | copy-start | bytes 1924
  54.8 59.9 %all-to-all-start.1 = ((bf16[8,3,256,128]{3,2,1,0:T(8,128)(2,1)}), bf16[8,3,256,128]{3,2,1,0:T(8,128)(2,1)}, u32[]{:S(2)}, u32[]{:S(2)}) async-start(bf16[8,3,256,128]{3,2,1,0:T(8,128)(2,1)} %shard_map.123), calls=%async_computation.1 | async-start | bytes 3145728 | tf_op jit(solution)/shard_map/all_to_all | solution.py:144
  76.3 1.0 copy-start.3
  79.1 1.0 copy-start.3
  81.8 1.0 copy-start.3
  84.6 1.0 copy-start.3
  86.5 28.1 %copy-start.1 = (bf16[4,512,128]{2,1,0:T(8,128)(2,1)}, bf16[4,512,128]{2,1,0:T(8,128)(2,1)S(1)}, u32[]{:S(2)}) copy-start(bf16[4,512,128]{2,1,0:T(8,128)(2,1)S(1)} %get-tuple-element.83) | copy-start | bytes 1572868
  114.6 21.9 %all-to-all-start.2 = ((bf16[8,3,256,128]{3,2,1,0:T(8,128)(2,1)}), bf16[8,3,256,128]{3,2,1,0:T(8,128)(2,1)S(1)}, u32[]{:S(2)}, u32[]{:S(2)}) async-start(bf16[8,3,256,128]{3,2,1,0:T(8,128)(2,1)} %shard_map.124), calls=%async_computation.2 | async-start | bytes 3145728 | tf_op jit(solution)/shard_map/all_to_all | solution.py:144
  122.2 1.0 copy-start.4
  125.5 1.0 copy-start.4
  128.8 1.0 copy-start.4
  132.2 1.0 copy-start.4
  137.5 11.0 %copy-start.2 = (bf16[4,512,128]{2,1,0:T(8,128)(2,1)S(1)}, bf16[4,512,128]{2,1,0:T(8,128)(2,1)}, u32[]{:S(2)}) copy-start(bf16[4,512,128]{2,1,0:T(8,128)(2,1)} %copy-done.1) | copy-start | bytes 1572868
  138.3 1.0 copy-start.5
  141.1 1.0 copy-start.5
  143.8 1.0 copy-start.5
  146.6 1.0 copy-start.5
  152.5 9.6 %copy-start.8 = (f32[1,2,8,64]{3,2,1,0:T(8,128)S(1)}, f32[1,2,8,64]{3,2,1,0:T(8,128)}, u32[]{:S(2)}) copy-start(f32[1,2,8,64]{3,2,1,0:T(8,128)} %param.23) | copy-start | bytes 12292
  154.4 24.5 %all-to-all-start.3 = ((f32[8,320,128]{2,1,0:T(8,128)}), f32[8,320,128]{2,1,0:T(8,128)S(1)}, u32[]{:S(2)}, u32[]{:S(2)}) async-start(f32[8,320,128]{2,1,0:T(8,128)} %bitcast.18), calls=%async_computation.3 | async-start | bytes 2621440 | tf_op jit(solution)/shard_map/all_to_all | solution.py:158
  181.0 3.3 %copy-start.9 = (f32[512]{0:T(512)S(1)}, f32[512]{0:T(512)}, u32[]{:S(2)}) copy-start(f32[512]{0:T(512)} %param.22) | copy-start | bytes 6148
  181.0 3.3 %copy-start.12 = (pred[8,9]{0,1:T(8,128)(4,1)S(1)}, pred[8,9]{0,1:T(8,128)(4,1)}, u32[]{:S(2)}) copy-start(pred[8,9]{0,1:T(8,128)(4,1)} %constant.98) | copy-start | bytes 220
  187.5 1.0 copy-start.11
  189.3 13.4 %all-to-all-start.4 = ((f32[8,2,512]{2,1,0:T(2,128)}), f32[8,2,512]{2,1,0:T(2,128)S(1)}, u32[]{:S(2)}, u32[]{:S(2)}) async-start(f32[8,2,512]{2,1,0:T(2,128)} %reshape.195), calls=%async_computation.4 | async-start | bytes 65536 | tf_op jit(solution)/shard_map/all_to_all | solution.py:208

commit v10 on v9

--- a/solution.py
+++ b/solution.py
@@ -20,7 +20,7 @@
 FT = 2
 RL = 8
 COLS = 64
-QUERY_BLOCK = 512
+QUERY_BLOCK = 256
 
 
 def shifted(array, axis, by):
@@ -92,18 +92,33 @@
 
 
 def head_attention(query, key, value):
-    length = query.shape[0]
-    score_scale = 1.0 / math.sqrt(query.shape[1])
-    query_blocks = query.reshape(length // QUERY_BLOCK, QUERY_BLOCK, query.shape[1])
-
-    def one_block(query_part):
-        scores = jnp.dot(query_part, key.T, preferred_element_type=jnp.float32) * score_scale
+    length, width = query.shape
+    score_scale = 1.0 / math.sqrt(width)
+
+    def kernel(q_ref, k_ref, v_ref, out_ref):
+        scores = (
+            lax.dot_general(
+                q_ref[...],
+                k_ref[...],
+                (((1,), (1,)), ((), ())),
+                preferred_element_type=jnp.float32,
+            )
+            * score_scale
+        )
         expo = jnp.exp(scores - jnp.max(scores, axis=-1, keepdims=True))
         totals = jnp.sum(expo, axis=-1, keepdims=True)
-        mixed = jnp.dot(expo.astype(jnp.bfloat16), value, preferred_element_type=jnp.float32)
-        return (mixed / totals).astype(jnp.bfloat16)
-
-    return lax.map(one_block, query_blocks).reshape(length, query.shape[1])
+        mixed = jnp.dot(expo.astype(jnp.bfloat16), v_ref[...], preferred_element_type=jnp.float32)
+        out_ref[...] = (mixed / totals).astype(out_ref.dtype)
+
+    whole = pl.BlockSpec((length, width), lambda i: (0, 0))
+    rows = pl.BlockSpec((QUERY_BLOCK, width), lambda i: (i, 0))
+    return pl.pallas_call(
+        kernel,
+        grid=(length // QUERY_BLOCK,),
+        out_shape=jax.ShapeDtypeStruct((length, width), query.dtype),
+        in_specs=[rows, whole, whole],
+        out_specs=rows,
+    )(query, key, value)
 
 
 def window_columns(volume):

time: 205 us -> 217 us (1.059)
  Pallas kernels: 8.43 us -> 42.3 us
  matrix products: 27.6 us -> 5.33 us
  waiting for transfers between devices: 91.3 us -> 102 us
  other arithmetic: 12.3 us -> 2.44 us
    pallas_call x0 -> x3, Pallas kernels: none -> 33.8 us  [head_attention(): pl.pallas_call(kernel, grid=(length // QUERY_BLOCK,), out_shape=jax.Shape...]
    dot_general x24 -> x0, matrix products: 22.6 us -> none  [the longest x12 13.2 us: one_block(): jnp.dot(expo.astype(jnp.bfloat16), value, preferred_element_type=jnp.floa...]
    all_to_all x3, waiting for transfers between devices: 65.9 us -> 76.8 us  [local(): lax.all_to_all(stacked, 'seq', split_axis=0, concat_axis=0, tiled=True)]
    reduce_sum x12 -> x0, other arithmetic: 9.81 us -> none  [one_block(): totals = jnp.sum(expo, axis=-1, keepdims=True)]
    while x24 -> x0, local copies, waits for them, and re-layouts: 2.69 us -> none
  transfers between devices with their start and end apart: 5 -> 5, of which waited for: 5 -> 4; matrix products, arithmetic and copies ran while one was open for 14% -> 4% of each run, Pallas kernels for 3% -> 13%
where the time goes in v10:
time: 217 us; the launch traced here: 216 us
  waiting for transfers between devices  102 us (47%)
  starting transfers between devices  45.4 us (21%)
  Pallas kernels  42.3 us (19%)
  local copies, waits for them, and re-layouts  17.5 us (8%)
  matrix products  5.33 us (2%)
  other arithmetic  2.44 us (1%)
    all_to_all x3, waiting for transfers between devices, local(): lax.all_to_all(stacked, 'seq', split_axis=0, concat_axis=0, tiled=True)  76.8 us
    pallas_call x3, Pallas kernels, head_attention(): pl.pallas_call(kernel, grid=(length // QUERY_BLOCK,), out_shape=jax.Shape...  33.8 us
    all_to_all x3, starting transfers between devices, local(): lax.all_to_all(stacked, 'seq', split_axis=0, concat_axis=0, tiled=True)  32.4 us
    all_to_all x1, waiting for transfers between devices, local(): lax.all_to_all(outgoing, 'seq', split_axis=0, concat_axis=0, tiled=True)  16.9 us
    all_to_all x1, starting transfers between devices, local(): lax.all_to_all(outgoing, 'seq', split_axis=0, concat_axis=0, tiled=True)  9.65 us
    all_to_all x1, waiting for transfers between devices, local(): lax.all_to_all(by_owner.reshape(group_count, BPD, CO), 'seq', split_axis=...  8.73 us
    pallas_call x3, Pallas kernels, slot_operand(): pl.pallas_call(kernel, grid=(1,), out_shape=jax.ShapeDtypeStruct((group_c...  8.42 us
    slice x3, local copies, waits for them, and re-layouts, local(): gathered[:, part].reshape(seq_len, HD)  6.28 us
  transfers between devices with their start and end apart: 5, of which 4 were waited for; matrix products, arithmetic and copies ran while one was open for 4% of the time, Pallas kernels for 13%

profile of v10, /device:TPU:80, one launch (start us, length us, event | category | flops | bytes accessed | tf_op | source)
XLA Modules:
  0.0 216.2 jit_solution(16551038044311467016)
XLA Ops:
  0.6 2.8 %shard_map.122 = bf16[8,3,256,128]{3,2,1,0:T(8,128)(2,1)} custom-call(bf16[256,3072]{1,0:T(8,128)(2,1)} %q_ref.5, bf16[256,3072]{1,0:T(8,128)(2,1)} %k_ref.5, bf16[256,3072]{1,0:T(8,128)(2,1)} %v_ref.5), custom_call_target="tpu_custom_call" | custom-call | tf_op jit(solution)/shard_map/pallas_call | solution.py:85
  3.5 9.1 %all-to-all-start = ((bf16[8,3,256,128]{3,2,1,0:T(8,128)(2,1)}), bf16[8,3,256,128]{3,2,1,0:T(8,128)(2,1)S(1)}, u32[]{:S(2)}, u32[]{:S(2)}) async-start(bf16[8,3,256,128]{3,2,1,0:T(8,128)(2,1)} %shard_map.122), calls=%async_computation | async-start | bytes 3145728 | tf_op jit(solution)/shard_map/all_to_all | solution.py:159
  12.6 2.8 %shard_map.124 = bf16[8,3,256,128]{3,2,1,0:T(8,128)(2,1)} custom-call(bf16[256,3072]{1,0:T(8,128)(2,1)} %q_ref.5, bf16[256,3072]{1,0:T(8,128)(2,1)} %k_ref.5, bf16[256,3072]{1,0:T(8,128)(2,1)} %v_ref.5), custom_call_target="tpu_custom_call" | custom-call | tf_op jit(solution)/shard_map/pallas_call | solution.py:85
  15.4 39.4 %all-to-all-done = bf16[8,3,256,128]{3,2,1,0:T(8,128)(2,1)S(1)} async-done(((bf16[8,3,256,128]{3,2,1,0:T(8,128)(2,1)}), bf16[8,3,256,128]{3,2,1,0:T(8,128)(2,1)S(1)}, u32[]{:S(2)}, u32[]{:S(2)}) %all-to-all-start) | async-done | bytes 1572896 | tf_op jit(solution)/shard_map/all_to_all | solution.py:159
  54.8 19.7 %all-to-all-start.1 = ((bf16[8,3,256,128]{3,2,1,0:T(8,128)(2,1)}), bf16[8,3,256,128]{3,2,1,0:T(8,128)(2,1)}, u32[]{:S(2)}, u32[]{:S(2)}) async-start(bf16[8,3,256,128]{3,2,1,0:T(8,128)(2,1)} %shard_map.124), calls=%async_computation.1 | async-start | bytes 3145728 | tf_op jit(solution)/shard_map/all_to_all | solution.py:159
  74.5 2.8 %shard_map.126 = bf16[8,3,256,128]{3,2,1,0:T(8,128)(2,1)} custom-call(bf16[256,3072]{1,0:T(8,128)(2,1)} %q_ref.5, bf16[256,3072]{1,0:T(8,128)(2,1)} %k_ref.5, bf16[256,3072]{1,0:T(8,128)(2,1)} %v_ref.5), custom_call_target="tpu_custom_call" | custom-call | tf_op jit(solution)/shard_map/pallas_call | solution.py:85
  77.3 37.4 %all-to-all-done.1 = bf16[8,3,256,128]{3,2,1,0:T(8,128)(2,1)} async-done(((bf16[8,3,256,128]{3,2,1,0:T(8,128)(2,1)}), bf16[8,3,256,128]{3,2,1,0:T(8,128)(2,1)}, u32[]{:S(2)}, u32[]{:S(2)}) %all-to-all-start.1) | async-done | bytes 1572896 | tf_op jit(solution)/shard_map/all_to_all | solution.py:159
  114.7 3.6 %all-to-all-start.2 = ((bf16[8,3,256,128]{3,2,1,0:T(8,128)(2,1)}), bf16[8,3,256,128]{3,2,1,0:T(8,128)(2,1)S(1)}, u32[]{:S(2)}, u32[]{:S(2)}) async-start(bf16[8,3,256,128]{3,2,1,0:T(8,128)(2,1)} %shard_map.126), calls=%async_computation.2 | async-start | bytes 3145728 | tf_op jit(solution)/shard_map/all_to_all | solution.py:159
  118.3 0.4 select_reduce_fusion
  118.9 2.6 %fusion.33 = (bf16[8,1,256,128]{3,2,1,0:T(8,128)(2,1)}, bf16[8,1,256,128]{3,2,1,0:T(8,128)(2,1)}, bf16[8,1,256,128]{3,2,1,0:T(8,128)(2,1)}) fusion(bf16[8,3,256,128]{3,2,1,0:T(8,128)(2,1)} %copy-done.1), kind=kLoop, calls=%fused_computation.56 | loop fusion | bytes 3145728 | tf_op jit(solution)/shard_map/slice | solution.py:161
  121.5 11.3 %shard_map.123 = bf16[2048,128]{1,0:T(8,128)(2,1)} custom-call(bf16[2048,128]{1,0:T(8,128)(2,1)} %bitcast.46, bf16[2048,128]{1,0:T(8,128)(2,1)} %bitcast.45, bf16[2048,128]{1,0:T(8,128)(2,1)} %bitcast.44), custom_call_target="tpu_custom_call" | custom-call | tf_op jit(solution)/shard_map/pallas_call | solution.py:115
  132.7 2.5 %fusion.32 = (bf16[8,1,256,128]{3,2,1,0:T(8,128)(2,1)}, bf16[8,1,256,128]{3,2,1,0:T(8,128)(2,1)}, bf16[8,1,256,128]{3,2,1,0:T(8,128)(2,1)}) fusion(bf16[8,3,256,128]{3,2,1,0:T(8,128)(2,1)} %all-to-all-done.1), kind=kLoop, calls=%fused_computation.55 | loop fusion | bytes 3145728 | tf_op jit(solution)/shard_map/slice | solution.py:161
  135.3 11.3 %shard_map.125 = bf16[2048,128]{1,0:T(8,128)(2,1)} custom-call(bf16[2048,128]{1,0:T(8,128)(2,1)} %bitcast.49, bf16[2048,128]{1,0:T(8,128)(2,1)} %bitcast.48, bf16[2048,128]{1,0:T(8,128)(2,1)} %bitcast.47), custom_call_target="tpu_custom_call" | custom-call | tf_op jit(solution)/shard_map/pallas_call | solution.py:115
  146.6 1.0 fusion.21
  147.6 1.3 convolution_add_fusion.1
  149.0 1.2 fusion.31
  150.1 11.3 %shard_map.127 = bf16[2048,128]{1,0:T(8,128)(2,1)} custom-call(bf16[2048,128]{1,0:T(8,128)(2,1)} %bitcast.52, bf16[2048,128]{1,0:T(8,128)(2,1)} %bitcast.51, bf16[2048,128]{1,0:T(8,128)(2,1)} %bitcast.50), custom_call_target="tpu_custom_call" | custom-call | tf_op jit(solution)/shard_map/pallas_call | solution.py:115
  161.4 1.3 convolution_add_fusion
  163.3 1.9 gather_fusion
  165.2 9.7 %all-to-all-start.3 = ((f32[8,320,128]{2,1,0:T(8,128)}), f32[8,320,128]{2,1,0:T(8,128)S(1)}, u32[]{:S(2)}, u32[]{:S(2)}) async-start(f32[8,320,128]{2,1,0:T(8,128)} %bitcast.9), calls=%async_computation.3 | async-start | bytes 2621440 | tf_op jit(solution)/shard_map/all_to_all | solution.py:173
  175.0 16.9 %all-to-all-done.3 = f32[8,320,128]{2,1,0:T(8,128)S(1)} async-done(((f32[8,320,128]{2,1,0:T(8,128)}), f32[8,320,128]{2,1,0:T(8,128)S(1)}, u32[]{:S(2)}, u32[]{:S(2)}) %all-to-all-start.3) | async-done | bytes 1310752 | tf_op jit(solution)/shard_map/all_to_all | solution.py:173
  194.1 0.8 reshape.180
  195.0 2.2 %copy.60 = bf16[4,10,1,8,9,16]{5,3,4,1,0,2:T(8,128)(2,1)S(1)} copy(bf16[4,10,1,8,9,16]{4,3,5,1,0,2:T(8,128)(2,1)S(1)} %reshape.180) | data formatting | bytes 184320 | tf_op jit(solution)/shard_map/conv_general_dilated | solution.py:202
  197.2 1.5 add_convert_fusion
  198.7 0.4 copy.61
  199.1 1.4 copy.62
  200.4 0.9 multiply_reduce_fusion
  201.6 0.6 reshape.177
  202.2 3.3 %all-to-all-start.4 = ((f32[8,2,512]{2,1,0:T(2,128)}), f32[8,2,512]{2,1,0:T(2,128)S(1)}, u32[]{:S(2)}, u32[]{:S(2)}) async-start(f32[8,2,512]{2,1,0:T(2,128)} %reshape.177), calls=%async_computation.4 | async-start | bytes 65536 | tf_op jit(solution)/shard_map/all_to_all | solution.py:223
  205.6 1.3 copy.65
  206.9 8.7 %all-to-all-done.4 = f32[8,2,512]{2,1,0:T(2,128)S(1)} async-done(((f32[8,2,512]{2,1,0:T(2,128)}), f32[8,2,512]{2,1,0:T(2,128)S(1)}, u32[]{:S(2)}, u32[]{:S(2)}) %all-to-all-start.4) | async-done | bytes 32800 | tf_op jit(solution)/shard_map/all_to_all | solution.py:223
  215.6 0.6 reduce_sum.49
  (52 shorter events, 3.4 us)
Async XLA Ops:
  0.6 196.6 %copy-start = (bf16[432,512]{1,0:T(8,128)(2,1)S(1)}, bf16[432,512]{1,0:T(8,128)(2,1)}, u32[]{:S(2)}) copy-start(bf16[432,512]{1,0:T(8,128)(2,1)} %param.15) | copy-start | bytes 1327108
  3.5 51.3 %all-to-all-start = ((bf16[8,3,256,128]{3,2,1,0:T(8,128)(2,1)}), bf16[8,3,256,128]{3,2,1,0:T(8,128)(2,1)S(1)}, u32[]{:S(2)}, u32[]{:S(2)}) async-start(bf16[8,3,256,128]{3,2,1,0:T(8,128)(2,1)} %shard_map.122), calls=%async_computation | async-start | bytes 3145728 | tf_op jit(solution)/shard_map/all_to_all | solution.py:159
  54.8 22.5 %copy-start.1 = (bf16[8,3,256,128]{3,2,1,0:T(8,128)(2,1)}, bf16[8,3,256,128]{3,2,1,0:T(8,128)(2,1)S(1)}, u32[]{:S(2)}) copy-start(bf16[8,3,256,128]{3,2,1,0:T(8,128)(2,1)S(1)} %all-to-all-done) | copy-start | bytes 4718596
  54.8 59.9 %all-to-all-start.1 = ((bf16[8,3,256,128]{3,2,1,0:T(8,128)(2,1)}), bf16[8,3,256,128]{3,2,1,0:T(8,128)(2,1)}, u32[]{:S(2)}, u32[]{:S(2)}) async-start(bf16[8,3,256,128]{3,2,1,0:T(8,128)(2,1)} %shard_map.124), calls=%async_computation.1 | async-start | bytes 3145728 | tf_op jit(solution)/shard_map/all_to_all | solution.py:159
  77.3 41.0 %copy-start.3 = (pred[8,20,32]{2,0,1:T(8,128)(4,1)S(1)}, pred[8,20,32]{2,0,1:T(8,128)(4,1)}, u32[]{:S(2)}) copy-start(pred[8,20,32]{2,0,1:T(8,128)(4,1)} %constant.46.clone) | copy-start | bytes 15364
  77.3 41.0 %copy-start.7 = (s32[32]{0:T(128)S(1)}, s32[32]{0:T(128)}, u32[]{:S(2)}) copy-start(s32[32]{0:T(128)} %param.18) | copy-start | bytes 388
  77.3 41.4 %copy-start.4 = (s32[8,20]{0,1:T(8,128)S(1)}, s32[8,20]{0,1:T(8,128)}, u32[]{:S(2)}) copy-start(s32[8,20]{0,1:T(8,128)} %constant.47.clone) | copy-start | bytes 1924
  114.7 34.3 %all-to-all-start.2 = ((bf16[8,3,256,128]{3,2,1,0:T(8,128)(2,1)}), bf16[8,3,256,128]{3,2,1,0:T(8,128)(2,1)S(1)}, u32[]{:S(2)}, u32[]{:S(2)}) async-start(bf16[8,3,256,128]{3,2,1,0:T(8,128)(2,1)} %shard_map.126), calls=%async_computation.2 | async-start | bytes 3145728 | tf_op jit(solution)/shard_map/all_to_all | solution.py:159
  135.3 11.3 %copy-start.2 = (bf16[2048,128]{1,0:T(8,128)(2,1)S(1)}, bf16[2048,128]{1,0:T(8,128)(2,1)}, u32[]{:S(2)}) copy-start(bf16[2048,128]{1,0:T(8,128)(2,1)} %shard_map.123) | copy-start | bytes 1572868
  165.2 9.7 %copy-start.5 = (f32[1,2,8,64]{3,2,1,0:T(8,128)S(1)}, f32[1,2,8,64]{3,2,1,0:T(8,128)}, u32[]{:S(2)}) copy-start(f32[1,2,8,64]{3,2,1,0:T(8,128)} %param.17) | copy-start | bytes 12292
  165.2 26.6 %all-to-all-start.3 = ((f32[8,320,128]{2,1,0:T(8,128)}), f32[8,320,128]{2,1,0:T(8,128)S(1)}, u32[]{:S(2)}, u32[]{:S(2)}) async-start(f32[8,320,128]{2,1,0:T(8,128)} %bitcast.9), calls=%async_computation.3 | async-start | bytes 2621440 | tf_op jit(solution)/shard_map/all_to_all | solution.py:173
  194.1 3.1 %copy-start.6 = (f32[512]{0:T(512)S(1)}, f32[512]{0:T(512)}, u32[]{:S(2)}) copy-start(f32[512]{0:T(512)} %param.16) | copy-start | bytes 6148
  194.1 3.1 %copy-start.9 = (pred[8,9]{0,1:T(8,128)(4,1)S(1)}, pred[8,9]{0,1:T(8,128)(4,1)}, u32[]{:S(2)}) copy-start(pred[8,9]{0,1:T(8,128)(4,1)} %constant.56) | copy-start | bytes 220
  200.4 1.0 copy-start.8
  202.2 13.4 %all-to-all-start.4 = ((f32[8,2,512]{2,1,0:T(2,128)}), f32[8,2,512]{2,1,0:T(2,128)S(1)}, u32[]{:S(2)}, u32[]{:S(2)}) async-start(f32[8,2,512]{2,1,0:T(2,128)} %reshape.177), calls=%async_computation.4 | async-start | bytes 65536 | tf_op jit(solution)/shard_map/all_to_all | solution.py:223

commit v11 on v9

--- a/solution.py
+++ b/solution.py
@@ -20,7 +20,7 @@
 FT = 2
 RL = 8
 COLS = 64
-QUERY_BLOCK = 512
+QUERY_BLOCK = 1024
 
 
 def shifted(array, axis, by):

time: 205 us -> 204 us (level)
  local copies, waits for them, and re-layouts: 19.1 us -> 16.4 us
    while x24 -> x12, local copies, waits for them, and re-layouts: 2.69 us -> 0.03 us
    reduce_sum x12 -> x6, other arithmetic: 9.81 us -> 11.6 us  [one_block(): totals = jnp.sum(expo, axis=-1, keepdims=True)]
    dot_general x12 -> x6, matrix products: 9.45 us -> 7.96 us  [one_block(): jnp.dot(query_part, key.T, preferred_element_type=jnp.float32) * score_scale]
    dot_general x12 -> x6, matrix products: 13.2 us -> 13.7 us  [one_block(): jnp.dot(expo.astype(jnp.bfloat16), value, preferred_element_type=jnp.floa...]
where the time goes in v11:
time: 204 us; the launch traced here: 203 us
  waiting for transfers between devices  92.8 us (45%)
  starting transfers between devices  43.6 us (21%)
  matrix products  26.7 us (13%)
  local copies, waits for them, and re-layouts  16.4 us (8%)
  other arithmetic  14 us (7%)
  Pallas kernels  8.43 us (4%)
    all_to_all x3, waiting for transfers between devices, local(): lax.all_to_all(stacked, 'seq', split_axis=0, concat_axis=0, tiled=True)  67.4 us
    all_to_all x3, starting transfers between devices, local(): lax.all_to_all(stacked, 'seq', split_axis=0, concat_axis=0, tiled=True)  32.6 us
    all_to_all x1, waiting for transfers between devices, local(): lax.all_to_all(outgoing, 'seq', split_axis=0, concat_axis=0, tiled=True)  16.7 us
    dot_general x6, matrix products, one_block(): jnp.dot(expo.astype(jnp.bfloat16), value, preferred_element_type=jnp.floa...  13.7 us
    reduce_sum x6, other arithmetic, one_block(): totals = jnp.sum(expo, axis=-1, keepdims=True)  11.6 us
    all_to_all x1, waiting for transfers between devices, local(): lax.all_to_all(by_owner.reshape(group_count, BPD, CO), 'seq', split_axis=...  8.73 us
    pallas_call x3, Pallas kernels, slot_operand(): pl.pallas_call(kernel, grid=(1,), out_shape=jax.ShapeDtypeStruct((group_c...  8.43 us
    dot_general x6, matrix products, one_block(): jnp.dot(query_part, key.T, preferred_element_type=jnp.float32) * score_scale  7.96 us
  transfers between devices with their start and end apart: 5, of which 5 were waited for; matrix products, arithmetic and copies ran while one was open for 14% of the time, Pallas kernels for 3%

profile of v11, /device:TPU:80, one launch (start us, length us, event | category | flops | bytes accessed | tf_op | source)
XLA Modules:
  0.0 203.1 jit_solution(10894490206157210234)
XLA Ops:
  0.6 2.8 %shard_map.122 = bf16[8,3,256,128]{3,2,1,0:T(8,128)(2,1)} custom-call(bf16[256,3072]{1,0:T(8,128)(2,1)} %q_ref.5, bf16[256,3072]{1,0:T(8,128)(2,1)} %k_ref.5, bf16[256,3072]{1,0:T(8,128)(2,1)} %v_ref.5), custom_call_target="tpu_custom_call" | custom-call | tf_op jit(solution)/shard_map/pallas_call | solution.py:85
  3.5 9.1 %all-to-all-start = ((bf16[8,3,256,128]{3,2,1,0:T(8,128)(2,1)}), bf16[8,3,256,128]{3,2,1,0:T(8,128)(2,1)S(1)}, u32[]{:S(2)}, u32[]{:S(2)}) async-start(bf16[8,3,256,128]{3,2,1,0:T(8,128)(2,1)} %shard_map.122), calls=%async_computation | async-start | bytes 3145728 | tf_op jit(solution)/shard_map/all_to_all | solution.py:144
  12.6 2.8 %shard_map.123 = bf16[8,3,256,128]{3,2,1,0:T(8,128)(2,1)} custom-call(bf16[256,3072]{1,0:T(8,128)(2,1)} %q_ref.5, bf16[256,3072]{1,0:T(8,128)(2,1)} %k_ref.5, bf16[256,3072]{1,0:T(8,128)(2,1)} %v_ref.5), custom_call_target="tpu_custom_call" | custom-call | tf_op jit(solution)/shard_map/pallas_call | solution.py:85
  15.4 2.8 %shard_map.124 = bf16[8,3,256,128]{3,2,1,0:T(8,128)(2,1)} custom-call(bf16[256,3072]{1,0:T(8,128)(2,1)} %q_ref.5, bf16[256,3072]{1,0:T(8,128)(2,1)} %k_ref.5, bf16[256,3072]{1,0:T(8,128)(2,1)} %v_ref.5), custom_call_target="tpu_custom_call" | custom-call | tf_op jit(solution)/shard_map/pallas_call | solution.py:85
  18.8 35.9 %all-to-all-done = bf16[8,3,256,128]{3,2,1,0:T(8,128)(2,1)S(1)} async-done(((bf16[8,3,256,128]{3,2,1,0:T(8,128)(2,1)}), bf16[8,3,256,128]{3,2,1,0:T(8,128)(2,1)S(1)}, u32[]{:S(2)}, u32[]{:S(2)}) %all-to-all-start) | async-done | bytes 1572896 | tf_op jit(solution)/shard_map/all_to_all | solution.py:144
  54.8 19.7 %all-to-all-start.1 = ((bf16[8,3,256,128]{3,2,1,0:T(8,128)(2,1)}), bf16[8,3,256,128]{3,2,1,0:T(8,128)(2,1)}, u32[]{:S(2)}, u32[]{:S(2)}) async-start(bf16[8,3,256,128]{3,2,1,0:T(8,128)(2,1)} %shard_map.123), calls=%async_computation.1 | async-start | bytes 3145728 | tf_op jit(solution)/shard_map/all_to_all | solution.py:144
  75.5 10.8 %while.30 = (s32[]{:T(128)}, bf16[2,1024,128]{2,1,0:T(8,128)(2,1)S(1)}, bf16[2,1024,128]{2,1,0:T(8,128)(2,1)S(1)}, bf16[2048,128]{1,0:T(8,128)(2,1)S(1)}, bf16[2048,128]{1,0:T(8,128)(2,1)}, /*index=5*/s32[]{:T(128)}) while((s32[]{:T(128)}, bf16[2,1024,128]{2,1,0:T(8,128)(2,1)S(1)}, bf16[2,1024,128]{2,1,0:T(8,128)(2,1)S(1)}, ...), condition=%wide.region_3.4_spmd, body=%wide.region_0.3_spmd.sunk | while | flops 1090779136 | bytes 28856424 | solution.py:106
  76.9 1.9 fusion.126
  78.8 2.1 %fusion.127 = bf16[2,1024,128]{2,1,0:T(8,128)(2,1)S(1)} fusion(bf16[2,1024,128]{2,1,0:T(8,128)(2,1)S(1)} %get-tuple-element.261, s32[]{:T(128)} %get-tuple-element.260, bf16[2048,128]{1,0:T(8,128)(2,1)S(1)} %copy-done.3, f32[1024,2048]{1,0:T(8,128)S(1)} %get-tuple-element.238, f32[1024]{0:T(1024)S(1)} %get-tuple-element.239, f32[1024]{0:T(1024)S(1)} %fusion.126), kind=kOutput, calls=%fused_computation.9.clone.1 | convolution fusion | flops 543424512 | bytes 9183236 | tf_op jit(solution)/shard_map/while/body/eval_jaxpr/dot_general | solution.py:103
  82.3 1.9 fusion.126
  84.2 2.1 %fusion.127 = bf16[2,1024,128]{2,1,0:T(8,128)(2,1)S(1)} fusion(bf16[2,1024,128]{2,1,0:T(8,128)(2,1)S(1)} %get-tuple-element.261, s32[]{:T(128)} %get-tuple-element.260, bf16[2048,128]{1,0:T(8,128)(2,1)S(1)} %copy-done.3, f32[1024,2048]{1,0:T(8,128)S(1)} %get-tuple-element.238, f32[1024]{0:T(1024)S(1)} %get-tuple-element.239, f32[1024]{0:T(1024)S(1)} %fusion.126), kind=kOutput, calls=%fused_computation.9.clone.1 | convolution fusion | flops 543424512 | bytes 9183236 | tf_op jit(solution)/shard_map/while/body/eval_jaxpr/dot_general | solution.py:103
  86.4 28.3 %all-to-all-done.1 = bf16[8,3,256,128]{3,2,1,0:T(8,128)(2,1)} async-done(((bf16[8,3,256,128]{3,2,1,0:T(8,128)(2,1)}), bf16[8,3,256,128]{3,2,1,0:T(8,128)(2,1)}, u32[]{:S(2)}, u32[]{:S(2)}) %all-to-all-start.1) | async-done | bytes 1572896 | tf_op jit(solution)/shard_map/all_to_all | solution.py:144
  114.6 3.8 %all-to-all-start.2 = ((bf16[8,3,256,128]{3,2,1,0:T(8,128)(2,1)}), bf16[8,3,256,128]{3,2,1,0:T(8,128)(2,1)S(1)}, u32[]{:S(2)}, u32[]{:S(2)}) async-start(bf16[8,3,256,128]{3,2,1,0:T(8,128)(2,1)} %shard_map.124), calls=%async_computation.2 | async-start | bytes 3145728 | tf_op jit(solution)/shard_map/all_to_all | solution.py:144
  118.4 2.3 %fusion.95 = (bf16[8,1,256,128]{3,2,1,0:T(8,128)(2,1)}, bf16[8,1,256,128]{3,2,1,0:T(8,128)(2,1)S(1)}, bf16[8,1,256,128]{3,2,1,0:T(8,128)(2,1)S(1)}) fusion(bf16[8,3,256,128]{3,2,1,0:T(8,128)(2,1)} %all-to-all-done.1), kind=kLoop, calls=%fused_computation.97 | loop fusion | bytes 3145728 | tf_op jit(solution)/shard_map/slice | solution.py:146
  121.6 11.8 %while.31 = (s32[]{:T(128)}, bf16[2,1024,128]{2,1,0:T(8,128)(2,1)}, bf16[2,1024,128]{2,1,0:T(8,128)(2,1)S(1)}, bf16[2048,128]{1,0:T(8,128)(2,1)S(1)}, bf16[2048,128]{1,0:T(8,128)(2,1)}, /*index=5*/s32[]{:T(128)}) while((s32[]{:T(128)}, bf16[2,1024,128]{2,1,0:T(8,128)(2,1)}, bf16[2,1024,128]{2,1,0:T(8,128)(2,1)S(1)}, ...), condition=%wide.region_7.8_spmd, body=%wide.region_4.7_spmd.sunk | while | flops 1090779136 | bytes 28856932 | solution.py:106
  122.9 1.9 fusion.131
  124.9 2.6 %fusion.132 = bf16[2,1024,128]{2,1,0:T(8,128)(2,1)} fusion(bf16[2,1024,128]{2,1,0:T(8,128)(2,1)} %get-tuple-element.279, s32[]{:T(128)} %get-tuple-element.278, bf16[2048,128]{1,0:T(8,128)(2,1)S(1)} %copy-done.4, f32[1024,2048]{1,0:T(8,128)S(1)} %get-tuple-element.245, f32[1024]{0:T(1024)S(1)} %get-tuple-element.246, f32[1024]{0:T(1024)S(1)} %fusion.131), kind=kOutput, calls=%fused_computation.23.clone.1 | convolution fusion | flops 543424512 | bytes 9183744 | tf_op jit(solution)/shard_map/while/body/eval_jaxpr/dot_general | solution.py:103
  128.8 1.9 fusion.131
  130.8 2.6 %fusion.132 = bf16[2,1024,128]{2,1,0:T(8,128)(2,1)} fusion(bf16[2,1024,128]{2,1,0:T(8,128)(2,1)} %get-tuple-element.279, s32[]{:T(128)} %get-tuple-element.278, bf16[2048,128]{1,0:T(8,128)(2,1)S(1)} %copy-done.4, f32[1024,2048]{1,0:T(8,128)S(1)} %get-tuple-element.245, f32[1024]{0:T(1024)S(1)} %get-tuple-element.246, f32[1024]{0:T(1024)S(1)} %fusion.131), kind=kOutput, calls=%fused_computation.23.clone.1 | convolution fusion | flops 543424512 | bytes 9183744 | tf_op jit(solution)/shard_map/while/body/eval_jaxpr/dot_general | solution.py:103
  133.4 3.2 %all-to-all-done.2 = bf16[8,3,256,128]{3,2,1,0:T(8,128)(2,1)S(1)} async-done(((bf16[8,3,256,128]{3,2,1,0:T(8,128)(2,1)}), bf16[8,3,256,128]{3,2,1,0:T(8,128)(2,1)S(1)}, u32[]{:S(2)}, u32[]{:S(2)}) %all-to-all-start.2) | async-done | bytes 1572896 | tf_op jit(solution)/shard_map/all_to_all | solution.py:144
  137.6 10.8 %while.32 = (s32[]{:T(128)}, bf16[2,1024,128]{2,1,0:T(8,128)(2,1)S(1)}, bf16[2,1024,128]{2,1,0:T(8,128)(2,1)S(1)}, bf16[2048,128]{1,0:T(8,128)(2,1)S(1)}, bf16[2048,128]{1,0:T(8,128)(2,1)}, /*index=5*/s32[]{:T(128)}) while((s32[]{:T(128)}, bf16[2,1024,128]{2,1,0:T(8,128)(2,1)S(1)}, bf16[2,1024,128]{2,1,0:T(8,128)(2,1)S(1)}, ...), condition=%wide.region_11.12_spmd, body=%wide.region_8.11_spmd.sunk | while | flops 1090779136 | bytes 28856424 | solution.py:106
  138.9 1.9 fusion.136
  140.9 2.1 %fusion.137 = bf16[2,1024,128]{2,1,0:T(8,128)(2,1)S(1)} fusion(bf16[2,1024,128]{2,1,0:T(8,128)(2,1)S(1)} %get-tuple-element.297, s32[]{:T(128)} %get-tuple-element.296, bf16[2048,128]{1,0:T(8,128)(2,1)S(1)} %copy-done.5, f32[1024,2048]{1,0:T(8,128)S(1)} %get-tuple-element.252, f32[1024]{0:T(1024)S(1)} %get-tuple-element.253, f32[1024]{0:T(1024)S(1)} %fusion.136), kind=kOutput, calls=%fused_computation.37.clone.1 | convolution fusion | flops 543424512 | bytes 9183236 | tf_op jit(solution)/shard_map/while/body/eval_jaxpr/dot_general | solution.py:103
  144.4 1.9 fusion.136
  146.3 2.1 %fusion.137 = bf16[2,1024,128]{2,1,0:T(8,128)(2,1)S(1)} fusion(bf16[2,1024,128]{2,1,0:T(8,128)(2,1)S(1)} %get-tuple-element.297, s32[]{:T(128)} %get-tuple-element.296, bf16[2048,128]{1,0:T(8,128)(2,1)S(1)} %copy-done.5, f32[1024,2048]{1,0:T(8,128)S(1)} %get-tuple-element.252, f32[1024]{0:T(1024)S(1)} %get-tuple-element.253, f32[1024]{0:T(1024)S(1)} %fusion.136), kind=kOutput, calls=%fused_computation.37.clone.1 | convolution fusion | flops 543424512 | bytes 9183236 | tf_op jit(solution)/shard_map/while/body/eval_jaxpr/dot_general | solution.py:103
  152.4 1.9 gather_fusion
  154.3 7.6 %all-to-all-start.3 = ((f32[8,320,128]{2,1,0:T(8,128)}), f32[8,320,128]{2,1,0:T(8,128)S(1)}, u32[]{:S(2)}, u32[]{:S(2)}) async-start(f32[8,320,128]{2,1,0:T(8,128)} %bitcast.18), calls=%async_computation.3 | async-start | bytes 2621440 | tf_op jit(solution)/shard_map/all_to_all | solution.py:158
  162.1 16.7 %all-to-all-done.3 = f32[8,320,128]{2,1,0:T(8,128)S(1)} async-done(((f32[8,320,128]{2,1,0:T(8,128)}), f32[8,320,128]{2,1,0:T(8,128)S(1)}, u32[]{:S(2)}, u32[]{:S(2)}) %all-to-all-start.3) | async-done | bytes 1310752 | tf_op jit(solution)/shard_map/all_to_all | solution.py:158
  181.8 2.2 %copy.60 = bf16[4,10,1,8,9,16]{5,3,4,1,0,2:T(8,128)(2,1)S(1)} copy(bf16[4,10,1,8,9,16]{4,3,5,1,0,2:T(8,128)(2,1)S(1)} %reshape.198) | data formatting | bytes 184320 | tf_op jit(solution)/shard_map/conv_general_dilated | solution.py:187
  184.1 1.5 add_convert_fusion
  189.1 3.3 %all-to-all-start.4 = ((f32[8,2,512]{2,1,0:T(2,128)}), f32[8,2,512]{2,1,0:T(2,128)S(1)}, u32[]{:S(2)}, u32[]{:S(2)}) async-start(f32[8,2,512]{2,1,0:T(2,128)} %reshape.195), calls=%async_computation.4 | async-start | bytes 65536 | tf_op jit(solution)/shard_map/all_to_all | solution.py:208
  193.8 8.7 %all-to-all-done.4 = f32[8,2,512]{2,1,0:T(2,128)S(1)} async-done(((f32[8,2,512]{2,1,0:T(2,128)}), f32[8,2,512]{2,1,0:T(2,128)S(1)}, u32[]{:S(2)}, u32[]{:S(2)}) %all-to-all-start.4) | async-done | bytes 32800 | tf_op jit(solution)/shard_map/all_to_all | solution.py:208
  (85 shorter events, 24.0 us)
Async XLA Ops:
  0.6 183.4 %copy-start = (bf16[432,512]{1,0:T(8,128)(2,1)S(1)}, bf16[432,512]{1,0:T(8,128)(2,1)}, u32[]{:S(2)}) copy-start(bf16[432,512]{1,0:T(8,128)(2,1)} %param.21) | copy-start | bytes 1327108
  3.5 51.3 %all-to-all-start = ((bf16[8,3,256,128]{3,2,1,0:T(8,128)(2,1)}), bf16[8,3,256,128]{3,2,1,0:T(8,128)(2,1)S(1)}, u32[]{:S(2)}, u32[]{:S(2)}) async-start(bf16[8,3,256,128]{3,2,1,0:T(8,128)(2,1)} %shard_map.122), calls=%async_computation | async-start | bytes 3145728 | tf_op jit(solution)/shard_map/all_to_all | solution.py:144
  15.4 2.8 %copy-start.6 = (pred[8,20,32]{2,0,1:T(8,128)(4,1)S(1)}, pred[8,20,32]{2,0,1:T(8,128)(4,1)}, u32[]{:S(2)}) copy-start(pred[8,20,32]{2,0,1:T(8,128)(4,1)} %constant.88.clone) | copy-start | bytes 15364
  15.4 2.8 %copy-start.10 = (s32[32]{0:T(128)S(1)}, s32[32]{0:T(128)}, u32[]{:S(2)}) copy-start(s32[32]{0:T(128)} %param.24) | copy-start | bytes 388
  15.4 3.3 %copy-start.7 = (s32[8,20]{0,1:T(8,128)S(1)}, s32[8,20]{0,1:T(8,128)}, u32[]{:S(2)}) copy-start(s32[8,20]{0,1:T(8,128)} %constant.89.clone) | copy-start | bytes 1924
  54.8 59.9 %all-to-all-start.1 = ((bf16[8,3,256,128]{3,2,1,0:T(8,128)(2,1)}), bf16[8,3,256,128]{3,2,1,0:T(8,128)(2,1)}, u32[]{:S(2)}, u32[]{:S(2)}) async-start(bf16[8,3,256,128]{3,2,1,0:T(8,128)(2,1)} %shard_map.123), calls=%async_computation.1 | async-start | bytes 3145728 | tf_op jit(solution)/shard_map/all_to_all | solution.py:144
  76.8 2.0 copy-start.3
  82.3 2.0 copy-start.3
  86.4 28.3 %copy-start.1 = (bf16[2,1024,128]{2,1,0:T(8,128)(2,1)}, bf16[2,1024,128]{2,1,0:T(8,128)(2,1)S(1)}, u32[]{:S(2)}) copy-start(bf16[2,1024,128]{2,1,0:T(8,128)(2,1)S(1)} %get-tuple-element.83) | copy-start | bytes 1572868
  114.6 21.9 %all-to-all-start.2 = ((bf16[8,3,256,128]{3,2,1,0:T(8,128)(2,1)}), bf16[8,3,256,128]{3,2,1,0:T(8,128)(2,1)S(1)}, u32[]{:S(2)}, u32[]{:S(2)}) async-start(bf16[8,3,256,128]{3,2,1,0:T(8,128)(2,1)} %shard_map.124), calls=%async_computation.2 | async-start | bytes 3145728 | tf_op jit(solution)/shard_map/all_to_all | solution.py:144
  122.9 1.9 copy-start.4
  128.8 1.9 copy-start.4
  137.6 10.9 %copy-start.2 = (bf16[2,1024,128]{2,1,0:T(8,128)(2,1)S(1)}, bf16[2,1024,128]{2,1,0:T(8,128)(2,1)}, u32[]{:S(2)}) copy-start(bf16[2,1024,128]{2,1,0:T(8,128)(2,1)} %copy-done.1) | copy-start | bytes 1572868
  138.9 1.9 copy-start.5
  144.4 1.9 copy-start.5
  151.9 10.1 %copy-start.8 = (f32[1,2,8,64]{3,2,1,0:T(8,128)S(1)}, f32[1,2,8,64]{3,2,1,0:T(8,128)}, u32[]{:S(2)}) copy-start(f32[1,2,8,64]{3,2,1,0:T(8,128)} %param.23) | copy-start | bytes 12292
  154.3 24.4 %all-to-all-start.3 = ((f32[8,320,128]{2,1,0:T(8,128)}), f32[8,320,128]{2,1,0:T(8,128)S(1)}, u32[]{:S(2)}, u32[]{:S(2)}) async-start(f32[8,320,128]{2,1,0:T(8,128)} %bitcast.18), calls=%async_computation.3 | async-start | bytes 2621440 | tf_op jit(solution)/shard_map/all_to_all | solution.py:158
  162.0 22.0 %copy-start.9 = (f32[512]{0:T(512)S(1)}, f32[512]{0:T(512)}, u32[]{:S(2)}) copy-start(f32[512]{0:T(512)} %param.22) | copy-start | bytes 6148
  162.0 22.0 %copy-start.12 = (pred[8,9]{0,1:T(8,128)(4,1)S(1)}, pred[8,9]{0,1:T(8,128)(4,1)}, u32[]{:S(2)}) copy-start(pred[8,9]{0,1:T(8,128)(4,1)} %constant.98) | copy-start | bytes 220
  185.9 2.4 %copy-start.11 = (s32[16]{0:T(128)S(1)}, s32[16]{0:T(128)}, u32[]{:S(2)}) copy-start(s32[16]{0:T(128)} %param.25) | copy-start | bytes 196
  189.1 13.4 %all-to-all-start.4 = ((f32[8,2,512]{2,1,0:T(2,128)}), f32[8,2,512]{2,1,0:T(2,128)S(1)}, u32[]{:S(2)}, u32[]{:S(2)}) async-start(f32[8,2,512]{2,1,0:T(2,128)} %reshape.195), calls=%async_computation.4 | async-start | bytes 65536 | tf_op jit(solution)/shard_map/all_to_all | solution.py:208

commit v12 on v11

--- a/solution.py
+++ b/solution.py
@@ -46,10 +46,9 @@
     positions, halves = [], []
     for tile in range(tile_count):
         lower = 0 if tile % TR == 0 else 1
-        earlier = tile - TR if tile >= TR else 0
         diagonal = (tile - TR) ^ 1 if tile >= TR else 0
         pos, half = [], []
-        for src in (earlier, tile):
+        for src in (tile,):
             for q in range(4):
                 pos += [4 * src + q, 4 * src + q]
                 half += [0, 1]
@@ -170,13 +169,13 @@
         rows = flat.reshape(FT, WT, 2, 2 * LC)
         return jnp.where(upper_band, rows[:, :, 0], rows[:, :, 1]).reshape(FT, 1, COLS * LC)
 
-    earlier = jnp.where(has_earlier, to_tile(tokens[:S_DEV]), jnp.zeros((), jnp.bfloat16))
-    tile_latent = to_tile(tokens[S_DEV : 2 * S_DEV])
+    tile_latent = to_tile(tokens[:S_DEV])
+    earlier = shifted(tile_latent, "seq", TR)
     halo_len = FT * WT
     diagonal = jnp.where(
-        has_earlier, to_row(tokens[2 * S_DEV : 2 * S_DEV + halo_len]), jnp.zeros((), jnp.bfloat16)
-    )
-    beside = to_row(tokens[2 * S_DEV + halo_len :])
+        has_earlier, to_row(tokens[S_DEV : S_DEV + halo_len]), jnp.zeros((), jnp.bfloat16)
+    )
+    beside = to_row(tokens[S_DEV + halo_len :])
     extended = jnp.concatenate([earlier, tile_latent], axis=0)
     incoming = jnp.concatenate([diagonal, beside], axis=0)
     above = jnp.where(upper_band, jnp.zeros_like(incoming), incoming)

time: 204 us -> 205 us (level)
  starting transfers between devices: 43.6 us -> 45.9 us
    all_to_all x1, waiting for transfers between devices: 16.7 us -> 14.1 us  [local(): lax.all_to_all(outgoing, 'seq', split_axis=0, concat_axis=0, tiled=True)]
  transfers between devices with their start and end apart: 5 -> 6, of which waited for: 5 -> 6; matrix products, arithmetic and copies ran while one was open for 14% -> 14% of each run, Pallas kernels for 3% -> 3%
where the time goes in v12:
time: 205 us; the launch traced here: 204 us
  waiting for transfers between devices  91.7 us (45%)
  starting transfers between devices  45.9 us (22%)
  matrix products  26.7 us (13%)
  local copies, waits for them, and re-layouts  16.2 us (8%)
  other arithmetic  13.9 us (7%)
  Pallas kernels  8.39 us (4%)
    all_to_all x3, waiting for transfers between devices, local(): lax.all_to_all(stacked, 'seq', split_axis=0, concat_axis=0, tiled=True)  67.6 us
    all_to_all x3, starting transfers between devices, local(): lax.all_to_all(stacked, 'seq', split_axis=0, concat_axis=0, tiled=True)  32.7 us
    all_to_all x1, waiting for transfers between devices, local(): lax.all_to_all(outgoing, 'seq', split_axis=0, concat_axis=0, tiled=True)  14.1 us
    dot_general x6, matrix products, one_block(): jnp.dot(expo.astype(jnp.bfloat16), value, preferred_element_type=jnp.floa...  13.7 us
    reduce_sum x6, other arithmetic, one_block(): totals = jnp.sum(expo, axis=-1, keepdims=True)  11.6 us
    all_to_all x1, waiting for transfers between devices, local(): lax.all_to_all(by_owner.reshape(group_count, BPD, CO), 'seq', split_axis=...  8.81 us
    pallas_call x3, Pallas kernels, slot_operand(): pl.pallas_call(kernel, grid=(1,), out_shape=jax.ShapeDtypeStruct((group_c...  8.39 us
    dot_general x6, matrix products, one_block(): jnp.dot(query_part, key.T, preferred_element_type=jnp.float32) * score_scale  7.96 us
  transfers between devices with their start and end apart: 6, of which 6 were waited for; matrix products, arithmetic and copies ran while one was open for 14% of the time, Pallas kernels for 3%

profile of v12, /device:TPU:80, one launch (start us, length us, event | category | flops | bytes accessed | tf_op | source)
XLA Modules:
  0.0 203.9 jit_solution(11523693265355949914)
XLA Ops:
  0.6 2.8 %shard_map.122 = bf16[8,3,256,128]{3,2,1,0:T(8,128)(2,1)} custom-call(bf16[256,3072]{1,0:T(8,128)(2,1)} %q_ref.5, bf16[256,3072]{1,0:T(8,128)(2,1)} %k_ref.5, bf16[256,3072]{1,0:T(8,128)(2,1)} %v_ref.5), custom_call_target="tpu_custom_call" | custom-call | tf_op jit(solution)/shard_map/pallas_call | solution.py:84
  3.5 9.3 %all-to-all-start = ((bf16[8,3,256,128]{3,2,1,0:T(8,128)(2,1)}), bf16[8,3,256,128]{3,2,1,0:T(8,128)(2,1)S(1)}, u32[]{:S(2)}, u32[]{:S(2)}) async-start(bf16[8,3,256,128]{3,2,1,0:T(8,128)(2,1)} %shard_map.122), calls=%async_computation | async-start | bytes 3145728 | tf_op jit(solution)/shard_map/all_to_all | solution.py:143
  12.7 2.8 %shard_map.123 = bf16[8,3,256,128]{3,2,1,0:T(8,128)(2,1)} custom-call(bf16[256,3072]{1,0:T(8,128)(2,1)} %q_ref.5, bf16[256,3072]{1,0:T(8,128)(2,1)} %k_ref.5, bf16[256,3072]{1,0:T(8,128)(2,1)} %v_ref.5), custom_call_target="tpu_custom_call" | custom-call | tf_op jit(solution)/shard_map/pallas_call | solution.py:84
  15.5 2.8 %shard_map.124 = bf16[8,3,256,128]{3,2,1,0:T(8,128)(2,1)} custom-call(bf16[256,3072]{1,0:T(8,128)(2,1)} %q_ref.5, bf16[256,3072]{1,0:T(8,128)(2,1)} %k_ref.5, bf16[256,3072]{1,0:T(8,128)(2,1)} %v_ref.5), custom_call_target="tpu_custom_call" | custom-call | tf_op jit(solution)/shard_map/pallas_call | solution.py:84
  18.8 36.1 %all-to-all-done = bf16[8,3,256,128]{3,2,1,0:T(8,128)(2,1)S(1)} async-done(((bf16[8,3,256,128]{3,2,1,0:T(8,128)(2,1)}), bf16[8,3,256,128]{3,2,1,0:T(8,128)(2,1)S(1)}, u32[]{:S(2)}, u32[]{:S(2)}) %all-to-all-start) | async-done | bytes 1572896 | tf_op jit(solution)/shard_map/all_to_all | solution.py:143
  54.9 19.7 %all-to-all-start.1 = ((bf16[8,3,256,128]{3,2,1,0:T(8,128)(2,1)}), bf16[8,3,256,128]{3,2,1,0:T(8,128)(2,1)}, u32[]{:S(2)}, u32[]{:S(2)}) async-start(bf16[8,3,256,128]{3,2,1,0:T(8,128)(2,1)} %shard_map.123), calls=%async_computation.1 | async-start | bytes 3145728 | tf_op jit(solution)/shard_map/all_to_all | solution.py:143
  75.6 10.8 %while.30 = (s32[]{:T(128)}, bf16[2,1024,128]{2,1,0:T(8,128)(2,1)S(1)}, bf16[2,1024,128]{2,1,0:T(8,128)(2,1)S(1)}, bf16[2048,128]{1,0:T(8,128)(2,1)S(1)}, bf16[2048,128]{1,0:T(8,128)(2,1)}, /*index=5*/s32[]{:T(128)}) while((s32[]{:T(128)}, bf16[2,1024,128]{2,1,0:T(8,128)(2,1)S(1)}, bf16[2,1024,128]{2,1,0:T(8,128)(2,1)S(1)}, ...), condition=%wide.region_3.4_spmd, body=%wide.region_0.3_spmd.sunk | while | flops 1090779136 | bytes 28856424 | solution.py:105
  77.0 1.9 fusion.126
  78.9 2.1 %fusion.127 = bf16[2,1024,128]{2,1,0:T(8,128)(2,1)S(1)} fusion(bf16[2,1024,128]{2,1,0:T(8,128)(2,1)S(1)} %get-tuple-element.259, s32[]{:T(128)} %get-tuple-element.258, bf16[2048,128]{1,0:T(8,128)(2,1)S(1)} %copy-done.3, f32[1024,2048]{1,0:T(8,128)S(1)} %get-tuple-element.236, f32[1024]{0:T(1024)S(1)} %get-tuple-element.237, f32[1024]{0:T(1024)S(1)} %fusion.126), kind=kOutput, calls=%fused_computation.9.clone.1 | convolution fusion | flops 543424512 | bytes 9183236 | tf_op jit(solution)/shard_map/while/body/eval_jaxpr/dot_general | solution.py:102
  82.4 1.9 fusion.126
  84.4 2.1 %fusion.127 = bf16[2,1024,128]{2,1,0:T(8,128)(2,1)S(1)} fusion(bf16[2,1024,128]{2,1,0:T(8,128)(2,1)S(1)} %get-tuple-element.259, s32[]{:T(128)} %get-tuple-element.258, bf16[2048,128]{1,0:T(8,128)(2,1)S(1)} %copy-done.3, f32[1024,2048]{1,0:T(8,128)S(1)} %get-tuple-element.236, f32[1024]{0:T(1024)S(1)} %get-tuple-element.237, f32[1024]{0:T(1024)S(1)} %fusion.126), kind=kOutput, calls=%fused_computation.9.clone.1 | convolution fusion | flops 543424512 | bytes 9183236 | tf_op jit(solution)/shard_map/while/body/eval_jaxpr/dot_general | solution.py:102
  86.5 28.3 %all-to-all-done.1 = bf16[8,3,256,128]{3,2,1,0:T(8,128)(2,1)} async-done(((bf16[8,3,256,128]{3,2,1,0:T(8,128)(2,1)}), bf16[8,3,256,128]{3,2,1,0:T(8,128)(2,1)}, u32[]{:S(2)}, u32[]{:S(2)}) %all-to-all-start.1) | async-done | bytes 1572896 | tf_op jit(solution)/shard_map/all_to_all | solution.py:143
  114.8 3.8 %all-to-all-start.2 = ((bf16[8,3,256,128]{3,2,1,0:T(8,128)(2,1)}), bf16[8,3,256,128]{3,2,1,0:T(8,128)(2,1)S(1)}, u32[]{:S(2)}, u32[]{:S(2)}) async-start(bf16[8,3,256,128]{3,2,1,0:T(8,128)(2,1)} %shard_map.124), calls=%async_computation.2 | async-start | bytes 3145728 | tf_op jit(solution)/shard_map/all_to_all | solution.py:143
  118.6 2.3 %fusion.95 = (bf16[8,1,256,128]{3,2,1,0:T(8,128)(2,1)}, bf16[8,1,256,128]{3,2,1,0:T(8,128)(2,1)S(1)}, bf16[8,1,256,128]{3,2,1,0:T(8,128)(2,1)S(1)}) fusion(bf16[8,3,256,128]{3,2,1,0:T(8,128)(2,1)} %all-to-all-done.1), kind=kLoop, calls=%fused_computation.96 | loop fusion | bytes 3145728 | tf_op jit(solution)/shard_map/slice | solution.py:145
  121.7 11.8 %while.31 = (s32[]{:T(128)}, bf16[2,1024,128]{2,1,0:T(8,128)(2,1)}, bf16[2,1024,128]{2,1,0:T(8,128)(2,1)S(1)}, bf16[2048,128]{1,0:T(8,128)(2,1)S(1)}, bf16[2048,128]{1,0:T(8,128)(2,1)}, /*index=5*/s32[]{:T(128)}) while((s32[]{:T(128)}, bf16[2,1024,128]{2,1,0:T(8,128)(2,1)}, bf16[2,1024,128]{2,1,0:T(8,128)(2,1)S(1)}, ...), condition=%wide.region_7.8_spmd, body=%wide.region_4.7_spmd.sunk | while | flops 1090779136 | bytes 28856932 | solution.py:105
  123.0 1.9 fusion.131
  125.0 2.6 %fusion.132 = bf16[2,1024,128]{2,1,0:T(8,128)(2,1)} fusion(bf16[2,1024,128]{2,1,0:T(8,128)(2,1)} %get-tuple-element.277, s32[]{:T(128)} %get-tuple-element.276, bf16[2048,128]{1,0:T(8,128)(2,1)S(1)} %copy-done.4, f32[1024,2048]{1,0:T(8,128)S(1)} %get-tuple-element.243, f32[1024]{0:T(1024)S(1)} %get-tuple-element.244, f32[1024]{0:T(1024)S(1)} %fusion.131), kind=kOutput, calls=%fused_computation.23.clone.1 | convolution fusion | flops 543424512 | bytes 9183744 | tf_op jit(solution)/shard_map/while/body/eval_jaxpr/dot_general | solution.py:102
  129.0 1.9 fusion.131
  130.9 2.6 %fusion.132 = bf16[2,1024,128]{2,1,0:T(8,128)(2,1)} fusion(bf16[2,1024,128]{2,1,0:T(8,128)(2,1)} %get-tuple-element.277, s32[]{:T(128)} %get-tuple-element.276, bf16[2048,128]{1,0:T(8,128)(2,1)S(1)} %copy-done.4, f32[1024,2048]{1,0:T(8,128)S(1)} %get-tuple-element.243, f32[1024]{0:T(1024)S(1)} %get-tuple-element.244, f32[1024]{0:T(1024)S(1)} %fusion.131), kind=kOutput, calls=%fused_computation.23.clone.1 | convolution fusion | flops 543424512 | bytes 9183744 | tf_op jit(solution)/shard_map/while/body/eval_jaxpr/dot_general | solution.py:102
  133.6 3.2 %all-to-all-done.2 = bf16[8,3,256,128]{3,2,1,0:T(8,128)(2,1)S(1)} async-done(((bf16[8,3,256,128]{3,2,1,0:T(8,128)(2,1)}), bf16[8,3,256,128]{3,2,1,0:T(8,128)(2,1)S(1)}, u32[]{:S(2)}, u32[]{:S(2)}) %all-to-all-start.2) | async-done | bytes 1572896 | tf_op jit(solution)/shard_map/all_to_all | solution.py:143
  137.7 10.8 %while.32 = (s32[]{:T(128)}, bf16[2,1024,128]{2,1,0:T(8,128)(2,1)S(1)}, bf16[2,1024,128]{2,1,0:T(8,128)(2,1)S(1)}, bf16[2048,128]{1,0:T(8,128)(2,1)S(1)}, bf16[2048,128]{1,0:T(8,128)(2,1)}, /*index=5*/s32[]{:T(128)}) while((s32[]{:T(128)}, bf16[2,1024,128]{2,1,0:T(8,128)(2,1)S(1)}, bf16[2,1024,128]{2,1,0:T(8,128)(2,1)S(1)}, ...), condition=%wide.region_11.12_spmd, body=%wide.region_8.11_spmd.sunk | while | flops 1090779136 | bytes 28856424 | solution.py:105
  139.1 1.9 fusion.136
  141.0 2.1 %fusion.137 = bf16[2,1024,128]{2,1,0:T(8,128)(2,1)S(1)} fusion(bf16[2,1024,128]{2,1,0:T(8,128)(2,1)S(1)} %get-tuple-element.295, s32[]{:T(128)} %get-tuple-element.294, bf16[2048,128]{1,0:T(8,128)(2,1)S(1)} %copy-done.5, f32[1024,2048]{1,0:T(8,128)S(1)} %get-tuple-element.250, f32[1024]{0:T(1024)S(1)} %get-tuple-element.251, f32[1024]{0:T(1024)S(1)} %fusion.136), kind=kOutput, calls=%fused_computation.37.clone.1 | convolution fusion | flops 543424512 | bytes 9183236 | tf_op jit(solution)/shard_map/while/body/eval_jaxpr/dot_general | solution.py:102
  144.5 1.9 fusion.136
  146.5 2.1 %fusion.137 = bf16[2,1024,128]{2,1,0:T(8,128)(2,1)S(1)} fusion(bf16[2,1024,128]{2,1,0:T(8,128)(2,1)S(1)} %get-tuple-element.295, s32[]{:T(128)} %get-tuple-element.294, bf16[2048,128]{1,0:T(8,128)(2,1)S(1)} %copy-done.5, f32[1024,2048]{1,0:T(8,128)S(1)} %get-tuple-element.250, f32[1024]{0:T(1024)S(1)} %get-tuple-element.251, f32[1024]{0:T(1024)S(1)} %fusion.136), kind=kOutput, calls=%fused_computation.37.clone.1 | convolution fusion | flops 543424512 | bytes 9183236 | tf_op jit(solution)/shard_map/while/body/eval_jaxpr/dot_general | solution.py:102
  152.6 1.6 gather_fusion
  154.2 6.2 %all-to-all-start.3 = ((f32[8,192,128]{2,1,0:T(8,128)}), f32[8,192,128]{2,1,0:T(8,128)S(1)}, u32[]{:S(2)}, u32[]{:S(2)}) async-start(f32[8,192,128]{2,1,0:T(8,128)} %bitcast.18), calls=%async_computation.3 | async-start | bytes 1572864 | tf_op jit(solution)/shard_map/all_to_all | solution.py:157
  160.5 14.1 %all-to-all-done.3 = f32[8,192,128]{2,1,0:T(8,128)S(1)} async-done(((f32[8,192,128]{2,1,0:T(8,128)}), f32[8,192,128]{2,1,0:T(8,128)S(1)}, u32[]{:S(2)}, u32[]{:S(2)}) %all-to-all-start.3) | async-done | bytes 786464 | tf_op jit(solution)/shard_map/all_to_all | solution.py:157
  176.1 1.7 collective-permute-start
  180.6 2.2 %copy.61 = bf16[4,10,1,8,9,16]{5,3,4,1,0,2:T(8,128)(2,1)S(1)} copy(bf16[4,10,1,8,9,16]{4,3,5,1,0,2:T(8,128)(2,1)S(1)} %reshape.190) | data formatting | bytes 184320 | tf_op jit(solution)/shard_map/conv_general_dilated | solution.py:186
  187.9 5.2 %all-to-all-start.4 = ((f32[8,2,512]{2,1,0:T(2,128)}), f32[8,2,512]{2,1,0:T(2,128)S(1)}, u32[]{:S(2)}, u32[]{:S(2)}) async-start(f32[8,2,512]{2,1,0:T(2,128)} %reshape.187), calls=%async_computation.4 | async-start | bytes 65536 | tf_op jit(solution)/shard_map/all_to_all | solution.py:207
  194.5 8.8 %all-to-all-done.4 = f32[8,2,512]{2,1,0:T(2,128)S(1)} async-done(((f32[8,2,512]{2,1,0:T(2,128)}), f32[8,2,512]{2,1,0:T(2,128)S(1)}, u32[]{:S(2)}, u32[]{:S(2)}) %all-to-all-start.4) | async-done | bytes 32800 | tf_op jit(solution)/shard_map/all_to_all | solution.py:207
  (87 shorter events, 26.6 us)
Async XLA Ops:
  0.6 182.2 %copy-start = (bf16[432,512]{1,0:T(8,128)(2,1)S(1)}, bf16[432,512]{1,0:T(8,128)(2,1)}, u32[]{:S(2)}) copy-start(bf16[432,512]{1,0:T(8,128)(2,1)} %param.21) | copy-start | bytes 1327108
  3.5 14.8 %copy-start.6 = (pred[8,12,32]{2,0,1:T(8,128)(4,1)S(1)}, pred[8,12,32]{2,0,1:T(8,128)(4,1)}, u32[]{:S(2)}) copy-start(pred[8,12,32]{2,0,1:T(8,128)(4,1)} %constant.88.clone) | copy-start | bytes 9220
  3.5 14.8 %copy-start.11 = (s32[32]{0:T(128)S(1)}, s32[32]{0:T(128)}, u32[]{:S(2)}) copy-start(s32[32]{0:T(128)} %param.24) | copy-start | bytes 388
  3.5 15.1 %copy-start.8 = (s32[8,12]{0,1:T(8,128)S(1)}, s32[8,12]{0,1:T(8,128)}, u32[]{:S(2)}) copy-start(s32[8,12]{0,1:T(8,128)} %constant.89.clone) | copy-start | bytes 1156
  3.5 51.4 %all-to-all-start = ((bf16[8,3,256,128]{3,2,1,0:T(8,128)(2,1)}), bf16[8,3,256,128]{3,2,1,0:T(8,128)(2,1)S(1)}, u32[]{:S(2)}, u32[]{:S(2)}) async-start(bf16[8,3,256,128]{3,2,1,0:T(8,128)(2,1)} %shard_map.122), calls=%async_computation | async-start | bytes 3145728 | tf_op jit(solution)/shard_map/all_to_all | solution.py:143
  54.9 59.9 %all-to-all-start.1 = ((bf16[8,3,256,128]{3,2,1,0:T(8,128)(2,1)}), bf16[8,3,256,128]{3,2,1,0:T(8,128)(2,1)}, u32[]{:S(2)}, u32[]{:S(2)}) async-start(bf16[8,3,256,128]{3,2,1,0:T(8,128)(2,1)} %shard_map.123), calls=%async_computation.1 | async-start | bytes 3145728 | tf_op jit(solution)/shard_map/all_to_all | solution.py:143
  75.7 3.3 %copy-start.3 = (bf16[2048,128]{1,0:T(8,128)(2,1)S(1)}, bf16[2048,128]{1,0:T(8,128)(2,1)}, u32[]{:S(2)}) copy-start(bf16[2048,128]{1,0:T(8,128)(2,1)} %get-tuple-element.268) | copy-start | bytes 1572868 | tf_op jit(solution)/shard_map/while
  81.1 3.3 %copy-start.3 = (bf16[2048,128]{1,0:T(8,128)(2,1)S(1)}, bf16[2048,128]{1,0:T(8,128)(2,1)}, u32[]{:S(2)}) copy-start(bf16[2048,128]{1,0:T(8,128)(2,1)} %get-tuple-element.268) | copy-start | bytes 1572868 | tf_op jit(solution)/shard_map/while
  86.5 28.3 %copy-start.1 = (bf16[2,1024,128]{2,1,0:T(8,128)(2,1)}, bf16[2,1024,128]{2,1,0:T(8,128)(2,1)S(1)}, u32[]{:S(2)}) copy-start(bf16[2,1024,128]{2,1,0:T(8,128)(2,1)S(1)} %get-tuple-element.83) | copy-start | bytes 1572868
  114.8 21.9 %all-to-all-start.2 = ((bf16[8,3,256,128]{3,2,1,0:T(8,128)(2,1)}), bf16[8,3,256,128]{3,2,1,0:T(8,128)(2,1)S(1)}, u32[]{:S(2)}, u32[]{:S(2)}) async-start(bf16[8,3,256,128]{3,2,1,0:T(8,128)(2,1)} %shard_map.124), calls=%async_computation.2 | async-start | bytes 3145728 | tf_op jit(solution)/shard_map/all_to_all | solution.py:143
  121.7 3.3 %copy-start.4 = (bf16[2048,128]{1,0:T(8,128)(2,1)S(1)}, bf16[2048,128]{1,0:T(8,128)(2,1)}, u32[]{:S(2)}) copy-start(bf16[2048,128]{1,0:T(8,128)(2,1)} %get-tuple-element.286) | copy-start | bytes 1572868 | tf_op jit(solution)/shard_map/while
  127.6 3.3 %copy-start.4 = (bf16[2048,128]{1,0:T(8,128)(2,1)S(1)}, bf16[2048,128]{1,0:T(8,128)(2,1)}, u32[]{:S(2)}) copy-start(bf16[2048,128]{1,0:T(8,128)(2,1)} %get-tuple-element.286) | copy-start | bytes 1572868 | tf_op jit(solution)/shard_map/while
  137.7 10.9 %copy-start.2 = (bf16[2,1024,128]{2,1,0:T(8,128)(2,1)S(1)}, bf16[2,1024,128]{2,1,0:T(8,128)(2,1)}, u32[]{:S(2)}) copy-start(bf16[2,1024,128]{2,1,0:T(8,128)(2,1)} %copy-done.1) | copy-start | bytes 1572868
  137.7 3.3 %copy-start.5 = (bf16[2048,128]{1,0:T(8,128)(2,1)S(1)}, bf16[2048,128]{1,0:T(8,128)(2,1)}, u32[]{:S(2)}) copy-start(bf16[2048,128]{1,0:T(8,128)(2,1)} %get-tuple-element.304) | copy-start | bytes 1572868 | tf_op jit(solution)/shard_map/while
  143.2 3.3 %copy-start.5 = (bf16[2048,128]{1,0:T(8,128)(2,1)S(1)}, bf16[2048,128]{1,0:T(8,128)(2,1)}, u32[]{:S(2)}) copy-start(bf16[2048,128]{1,0:T(8,128)(2,1)} %get-tuple-element.304) | copy-start | bytes 1572868 | tf_op jit(solution)/shard_map/while
  148.6 11.8 %copy-start.7 = (f32[1,2,8,64]{3,2,1,0:T(8,128)S(1)}, f32[1,2,8,64]{3,2,1,0:T(8,128)}, u32[]{:S(2)}) copy-start(f32[1,2,8,64]{3,2,1,0:T(8,128)} %param.23) | copy-start | bytes 12292
  151.0 31.9 %copy-start.9 = (f32[512]{0:T(512)S(1)}, f32[512]{0:T(512)}, u32[]{:S(2)}) copy-start(f32[512]{0:T(512)} %param.22) | copy-start | bytes 6148
  151.0 31.9 %copy-start.12 = (pred[8,9]{0,1:T(8,128)(4,1)S(1)}, pred[8,9]{0,1:T(8,128)(4,1)}, u32[]{:S(2)}) copy-start(pred[8,9]{0,1:T(8,128)(4,1)} %constant.98) | copy-start | bytes 220
  154.2 20.4 %all-to-all-start.3 = ((f32[8,192,128]{2,1,0:T(8,128)}), f32[8,192,128]{2,1,0:T(8,128)S(1)}, u32[]{:S(2)}, u32[]{:S(2)}) async-start(f32[8,192,128]{2,1,0:T(8,128)} %bitcast.18), calls=%async_computation.3 | async-start | bytes 1572864 | tf_op jit(solution)/shard_map/all_to_all | solution.py:157
  176.1 3.1 %collective-permute-start = (bf16[2,8,1024]{2,1,0:T(8,128)(2,1)S(1)}, bf16[2,8,1024]{2,1,0:T(8,128)(2,1)S(1)}, u32[]{:S(2)}, u32[]{:S(2)}) collective-permute-start(bf16[2,8,1024]{2,1,0:T(8,128)(2,1)S(1)} %reshape.184), channel_id=1, source_target_pairs={{0,2},{1,3},{2,4},{3,5},{4,6},{5,7},{8,10},{9,11},{10,12},{11,13},... | collective-permute-start | bytes 98312 | tf_op jit(solution)/shard_map/ppermute | solution.py:29
  184.4 2.7 %copy-start.10 = (s32[16]{0:T(128)S(1)}, s32[16]{0:T(128)}, u32[]{:S(2)}) copy-start(s32[16]{0:T(128)} %param.25) | copy-start | bytes 196
  187.9 15.4 %all-to-all-start.4 = ((f32[8,2,512]{2,1,0:T(2,128)}), f32[8,2,512]{2,1,0:T(2,128)S(1)}, u32[]{:S(2)}, u32[]{:S(2)}) async-start(f32[8,2,512]{2,1,0:T(2,128)} %reshape.187), calls=%async_computation.4 | async-start | bytes 65536 | tf_op jit(solution)/shard_map/all_to_all | solution.py:207

commit v13 on v11

--- a/solution.py
+++ b/solution.py
@@ -103,7 +103,7 @@
         mixed = jnp.dot(expo.astype(jnp.bfloat16), value, preferred_element_type=jnp.float32)
         return (mixed / totals).astype(jnp.bfloat16)
 
-    return lax.map(one_block, query_blocks).reshape(length, query.shape[1])
+    return jnp.concatenate([one_block(part) for part in query_blocks], axis=0)
 
 
 def window_columns(volume):

time: 204 us -> 225 us (1.10)
  waiting for transfers between devices: 92.8 us -> 109 us
  matrix products: 26.7 us -> 31.1 us
  starting transfers between devices: 43.6 us -> 40.5 us
  local copies, waits for them, and re-layouts: 16.4 us -> 19.4 us
    all_to_all x3, waiting for transfers between devices: 67.4 us -> 84.1 us  [local(): lax.all_to_all(stacked, 'seq', split_axis=0, concat_axis=0, tiled=True)]
    dot_general x6, matrix products: 7.96 us -> 14.3 us  [one_block(): jnp.dot(query_part, key.T, preferred_element_type=jnp.float32) * score_scale]
    all_to_all x1, starting transfers between devices: 7.62 us -> 3.83 us  [local(): lax.all_to_all(outgoing, 'seq', split_axis=0, concat_axis=0, tiled=True)]
    unnamed x21 -> x27, local copies, waits for them, and re-layouts: 1.34 us -> 4.73 us
  transfers between devices with their start and end apart: 5 -> 5, of which waited for: 5 -> 5; matrix products, arithmetic and copies ran while one was open for 14% -> 14% of each run, Pallas kernels for 3% -> 2%
where the time goes in v13:
time: 225 us; the launch traced here: 224 us
  waiting for transfers between devices  109 us (48%)
  starting transfers between devices  40.5 us (18%)
  matrix products  31.1 us (14%)
  local copies, waits for them, and re-layouts  19.4 us (9%)
  other arithmetic  14 us (6%)
  Pallas kernels  8.43 us (4%)
    all_to_all x3, waiting for transfers between devices, local(): lax.all_to_all(stacked, 'seq', split_axis=0, concat_axis=0, tiled=True)  84.1 us
    all_to_all x3, starting transfers between devices, local(): lax.all_to_all(stacked, 'seq', split_axis=0, concat_axis=0, tiled=True)  33.3 us
    all_to_all x1, waiting for transfers between devices, local(): lax.all_to_all(outgoing, 'seq', split_axis=0, concat_axis=0, tiled=True)  16.4 us
    dot_general x6, matrix products, one_block(): jnp.dot(query_part, key.T, preferred_element_type=jnp.float32) * score_scale  14.3 us
    dot_general x6, matrix products, one_block(): jnp.dot(expo.astype(jnp.bfloat16), value, preferred_element_type=jnp.floa...  12.2 us
    reduce_sum x6, other arithmetic, one_block(): totals = jnp.sum(expo, axis=-1, keepdims=True)  11.6 us
    all_to_all x1, waiting for transfers between devices, local(): lax.all_to_all(by_owner.reshape(group_count, BPD, CO), 'seq', split_axis=...  8.73 us
    pallas_call x3, Pallas kernels, slot_operand(): pl.pallas_call(kernel, grid=(1,), out_shape=jax.ShapeDtypeStruct((group_c...  8.43 us
  transfers between devices with their start and end apart: 5, of which 5 were waited for; matrix products, arithmetic and copies ran while one was open for 14% of the time, Pallas kernels for 2%

profile of v13, /device:TPU:80, one launch (start us, length us, event | category | flops | bytes accessed | tf_op | source)
XLA Modules:
  0.0 223.8 jit_solution(17232438339871220355)
XLA Ops:
  0.6 2.8 %shard_map.122 = bf16[8,3,256,128]{3,2,1,0:T(8,128)(2,1)} custom-call(bf16[256,3072]{1,0:T(8,128)(2,1)} %q_ref.5, bf16[256,3072]{1,0:T(8,128)(2,1)} %k_ref.5, bf16[256,3072]{1,0:T(8,128)(2,1)} %v_ref.5), custom_call_target="tpu_custom_call" | custom-call | tf_op jit(solution)/shard_map/pallas_call | solution.py:85
  3.5 9.1 %all-to-all-start = ((bf16[8,3,256,128]{3,2,1,0:T(8,128)(2,1)}), bf16[8,3,256,128]{3,2,1,0:T(8,128)(2,1)S(1)}, u32[]{:S(2)}, u32[]{:S(2)}) async-start(bf16[8,3,256,128]{3,2,1,0:T(8,128)(2,1)} %shard_map.122), calls=%async_computation | async-start | bytes 3145728 | tf_op jit(solution)/shard_map/all_to_all | solution.py:144
  12.6 2.8 %shard_map.123 = bf16[8,3,256,128]{3,2,1,0:T(8,128)(2,1)} custom-call(bf16[256,3072]{1,0:T(8,128)(2,1)} %q_ref.5, bf16[256,3072]{1,0:T(8,128)(2,1)} %k_ref.5, bf16[256,3072]{1,0:T(8,128)(2,1)} %v_ref.5), custom_call_target="tpu_custom_call" | custom-call | tf_op jit(solution)/shard_map/pallas_call | solution.py:85
  15.4 39.4 %all-to-all-done = bf16[8,3,256,128]{3,2,1,0:T(8,128)(2,1)S(1)} async-done(((bf16[8,3,256,128]{3,2,1,0:T(8,128)(2,1)}), bf16[8,3,256,128]{3,2,1,0:T(8,128)(2,1)S(1)}, u32[]{:S(2)}, u32[]{:S(2)}) %all-to-all-start) | async-done | bytes 1572896 | tf_op jit(solution)/shard_map/all_to_all | solution.py:144
  55.9 19.7 %all-to-all-start.1 = ((bf16[8,3,256,128]{3,2,1,0:T(8,128)(2,1)}), bf16[8,3,256,128]{3,2,1,0:T(8,128)(2,1)S(1)}, u32[]{:S(2)}, u32[]{:S(2)}) async-start(bf16[8,3,256,128]{3,2,1,0:T(8,128)(2,1)} %shard_map.123), calls=%async_computation.1 | async-start | bytes 3145728 | tf_op jit(solution)/shard_map/all_to_all | solution.py:144
  75.6 2.8 %shard_map.124 = bf16[8,3,256,128]{3,2,1,0:T(8,128)(2,1)} custom-call(bf16[256,3072]{1,0:T(8,128)(2,1)} %q_ref.5, bf16[256,3072]{1,0:T(8,128)(2,1)} %k_ref.5, bf16[256,3072]{1,0:T(8,128)(2,1)} %v_ref.5), custom_call_target="tpu_custom_call" | custom-call | tf_op jit(solution)/shard_map/pallas_call | solution.py:85
  81.4 4.5 %multiply_reduce_fusion.5 = (f32[1024]{0:T(1024)S(1)}, f32[1024,2048]{1,0:T(8,128)}) fusion(bf16[1024,128]{1,0:T(8,128)(2,1)S(1)} %bitcast.75, bf16[2048,128]{1,0:T(8,128)(2,1)S(1)} %bitcast.69), kind=kOutput, calls=%fused_computation.12 | convolution fusion | flops 541064192 | bytes 9179136 | tf_op jit(solution)/shard_map/dot_general | solution.py:100
  85.9 4.5 %multiply_reduce_fusion.4 = (f32[1024]{0:T(1024)S(1)}, f32[1024,2048]{1,0:T(8,128)}) fusion(bf16[1024,128]{1,0:T(8,128)(2,1)S(1)} %bitcast.72, bf16[2048,128]{1,0:T(8,128)(2,1)S(1)} %bitcast.70), kind=kOutput, calls=%fused_computation.11 | convolution fusion | flops 541064192 | bytes 9179136 | tf_op jit(solution)/shard_map/dot_general | solution.py:100
  90.3 28.1 %all-to-all-done.1 = bf16[8,3,256,128]{3,2,1,0:T(8,128)(2,1)S(1)} async-done(((bf16[8,3,256,128]{3,2,1,0:T(8,128)(2,1)}), bf16[8,3,256,128]{3,2,1,0:T(8,128)(2,1)S(1)}, u32[]{:S(2)}, u32[]{:S(2)}) %all-to-all-start.1) | async-done | bytes 1572896 | tf_op jit(solution)/shard_map/all_to_all | solution.py:144
  118.4 4.5 %all-to-all-start.2 = ((bf16[8,3,256,128]{3,2,1,0:T(8,128)(2,1)}), bf16[8,3,256,128]{3,2,1,0:T(8,128)(2,1)}, u32[]{:S(2)}, u32[]{:S(2)}) async-start(bf16[8,3,256,128]{3,2,1,0:T(8,128)(2,1)} %shard_map.124), calls=%async_computation.2 | async-start | bytes 3145728 | tf_op jit(solution)/shard_map/all_to_all | solution.py:144
  125.7 2.2 slice-done.1
  127.9 1.9 fusion
  129.9 1.9 fusion.2
  131.8 1.9 fusion.4
  133.7 1.9 fusion.6
  135.7 2.0 fusion.29
  137.7 2.0 fusion.35
  139.7 2.0 fusion.41
  141.7 2.2 fusion.47
  143.9 16.7 %all-to-all-done.2 = bf16[8,3,256,128]{3,2,1,0:T(8,128)(2,1)} async-done(((bf16[8,3,256,128]{3,2,1,0:T(8,128)(2,1)}), bf16[8,3,256,128]{3,2,1,0:T(8,128)(2,1)}, u32[]{:S(2)}, u32[]{:S(2)}) %all-to-all-start.2) | async-done | bytes 1572896 | tf_op jit(solution)/shard_map/all_to_all | solution.py:144
  165.7 1.9 fusion.8
  167.6 2.0 fusion.53
  169.6 1.9 fusion.10
  171.5 2.0 fusion.59
  177.2 1.9 gather_fusion
  179.1 3.8 %all-to-all-start.3 = ((f32[8,320,128]{2,1,0:T(8,128)}), f32[8,320,128]{2,1,0:T(8,128)S(1)}, u32[]{:S(2)}, u32[]{:S(2)}) async-start(f32[8,320,128]{2,1,0:T(8,128)} %bitcast.12), calls=%async_computation.3 | async-start | bytes 2621440 | tf_op jit(solution)/shard_map/all_to_all | solution.py:158
  183.1 16.4 %all-to-all-done.3 = f32[8,320,128]{2,1,0:T(8,128)S(1)} async-done(((f32[8,320,128]{2,1,0:T(8,128)}), f32[8,320,128]{2,1,0:T(8,128)S(1)}, u32[]{:S(2)}, u32[]{:S(2)}) %all-to-all-start.3) | async-done | bytes 1310752 | tf_op jit(solution)/shard_map/all_to_all | solution.py:158
  202.5 2.2 copy.60
  204.8 1.5 add_convert_fusion
  206.6 1.4 copy.62
  209.8 3.3 %all-to-all-start.4 = ((f32[8,2,512]{2,1,0:T(2,128)}), f32[8,2,512]{2,1,0:T(2,128)S(1)}, u32[]{:S(2)}, u32[]{:S(2)}) async-start(f32[8,2,512]{2,1,0:T(2,128)} %reshape.201), calls=%async_computation.4 | async-start | bytes 65536 | tf_op jit(solution)/shard_map/all_to_all | solution.py:208
  214.5 8.7 %all-to-all-done.4 = f32[8,2,512]{2,1,0:T(2,128)S(1)} async-done(((f32[8,2,512]{2,1,0:T(2,128)}), f32[8,2,512]{2,1,0:T(2,128)S(1)}, u32[]{:S(2)}, u32[]{:S(2)}) %all-to-all-start.4) | async-done | bytes 32800 | tf_op jit(solution)/shard_map/all_to_all | solution.py:208
  (78 shorter events, 22.7 us)
Async XLA Ops:
  0.6 204.1 %copy-start = (bf16[432,512]{1,0:T(8,128)(2,1)S(1)}, bf16[432,512]{1,0:T(8,128)(2,1)}, u32[]{:S(2)}) copy-start(bf16[432,512]{1,0:T(8,128)(2,1)} %param.15) | copy-start | bytes 1327108
  3.5 51.3 %all-to-all-start = ((bf16[8,3,256,128]{3,2,1,0:T(8,128)(2,1)}), bf16[8,3,256,128]{3,2,1,0:T(8,128)(2,1)S(1)}, u32[]{:S(2)}, u32[]{:S(2)}) async-start(bf16[8,3,256,128]{3,2,1,0:T(8,128)(2,1)} %shard_map.122), calls=%async_computation | async-start | bytes 3145728 | tf_op jit(solution)/shard_map/all_to_all | solution.py:144
  12.6 65.8 %copy-start.2 = (pred[8,20,32]{2,0,1:T(8,128)(4,1)S(1)}, pred[8,20,32]{2,0,1:T(8,128)(4,1)}, u32[]{:S(2)}) copy-start(pred[8,20,32]{2,0,1:T(8,128)(4,1)} %constant.50.clone) | copy-start | bytes 15364
  12.6 65.8 %copy-start.6 = (s32[32]{0:T(128)S(1)}, s32[32]{0:T(128)}, u32[]{:S(2)}) copy-start(s32[32]{0:T(128)} %param.18) | copy-start | bytes 388
  12.6 66.2 %copy-start.3 = (s32[8,20]{0,1:T(8,128)S(1)}, s32[8,20]{0,1:T(8,128)}, u32[]{:S(2)}) copy-start(s32[8,20]{0,1:T(8,128)} %constant.51.clone) | copy-start | bytes 1924
  54.8 1.2 copy-start.1
  55.9 62.4 %all-to-all-start.1 = ((bf16[8,3,256,128]{3,2,1,0:T(8,128)(2,1)}), bf16[8,3,256,128]{3,2,1,0:T(8,128)(2,1)S(1)}, u32[]{:S(2)}, u32[]{:S(2)}) async-start(bf16[8,3,256,128]{3,2,1,0:T(8,128)(2,1)} %shard_map.123), calls=%async_computation.1 | async-start | bytes 3145728 | tf_op jit(solution)/shard_map/all_to_all | solution.py:144
  118.4 42.3 %all-to-all-start.2 = ((bf16[8,3,256,128]{3,2,1,0:T(8,128)(2,1)}), bf16[8,3,256,128]{3,2,1,0:T(8,128)(2,1)}, u32[]{:S(2)}, u32[]{:S(2)}) async-start(bf16[8,3,256,128]{3,2,1,0:T(8,128)(2,1)} %shard_map.124), calls=%async_computation.2 | async-start | bytes 3145728 | tf_op jit(solution)/shard_map/all_to_all | solution.py:144
  123.0 2.7 %slice-start = ((s8[8388608]{0:T(1024)(128)(4,1)}), s8[4194304]{0:T(1024)(128)(4,1)S(1)}, s32[]{:S(2)}) async-start(s8[8388608]{0:T(1024)(128)(4,1)} %bitcast.60), calls=%async_computation.5 | async-start | bytes 8388608
  124.3 5.5 %slice-start.2 = ((s8[8388608]{0:T(1024)(128)(4,1)}), s8[4194304]{0:T(1024)(128)(4,1)S(1)}, s32[]{:S(2)}) async-start(s8[8388608]{0:T(1024)(128)(4,1)} %bitcast.62), calls=%async_computation.7 | async-start | bytes 8388608
  124.3 3.6 %slice-start.1 = ((s8[8388608]{0:T(1024)(128)(4,1)}), s8[4194304]{0:T(1024)(128)(4,1)S(1)}, s32[]{:S(2)}) async-start(s8[8388608]{0:T(1024)(128)(4,1)} %bitcast.60), calls=%async_computation.6 | async-start | bytes 8388608
  124.4 5.5 %slice-start.3 = ((s8[8388608]{0:T(1024)(128)(4,1)}), s8[4194304]{0:T(1024)(128)(4,1)S(1)}, s32[]{:S(2)}) async-start(s8[8388608]{0:T(1024)(128)(4,1)} %bitcast.62), calls=%async_computation.8 | async-start | bytes 8388608
  173.5 9.4 %copy-start.4 = (f32[1,2,8,64]{3,2,1,0:T(8,128)S(1)}, f32[1,2,8,64]{3,2,1,0:T(8,128)}, u32[]{:S(2)}) copy-start(f32[1,2,8,64]{3,2,1,0:T(8,128)} %param.17) | copy-start | bytes 12292
  176.6 28.1 %copy-start.5 = (f32[512]{0:T(512)S(1)}, f32[512]{0:T(512)}, u32[]{:S(2)}) copy-start(f32[512]{0:T(512)} %param.16) | copy-start | bytes 6148
  176.6 28.1 %copy-start.8 = (pred[8,9]{0,1:T(8,128)(4,1)S(1)}, pred[8,9]{0,1:T(8,128)(4,1)}, u32[]{:S(2)}) copy-start(pred[8,9]{0,1:T(8,128)(4,1)} %constant.60) | copy-start | bytes 220
  179.1 20.3 %all-to-all-start.3 = ((f32[8,320,128]{2,1,0:T(8,128)}), f32[8,320,128]{2,1,0:T(8,128)S(1)}, u32[]{:S(2)}, u32[]{:S(2)}) async-start(f32[8,320,128]{2,1,0:T(8,128)} %bitcast.12), calls=%async_computation.3 | async-start | bytes 2621440 | tf_op jit(solution)/shard_map/all_to_all | solution.py:158
  206.2 2.7 %copy-start.7 = (s32[16]{0:T(128)S(1)}, s32[16]{0:T(128)}, u32[]{:S(2)}) copy-start(s32[16]{0:T(128)} %param.19) | copy-start | bytes 196
  209.8 13.4 %all-to-all-start.4 = ((f32[8,2,512]{2,1,0:T(2,128)}), f32[8,2,512]{2,1,0:T(2,128)S(1)}, u32[]{:S(2)}, u32[]{:S(2)}) async-start(f32[8,2,512]{2,1,0:T(2,128)} %reshape.201), calls=%async_computation.4 | async-start | bytes 65536 | tf_op jit(solution)/shard_map/all_to_all | solution.py:208
